TPU v7x, 32 devices: a whole 2x2x4 slice. The times are simulated.
32 devices in a mesh: groups: 2 (over y), rows: 16 (over z, x, core).
Axes of the slice: x: 2, y: 2, z: 4, core: 2. Of those that a mesh axis runs over, the one named last changes fastest.
Arguments:
- queries: bfloat16 [32, 4096], P(('groups', 'rows')), parts along dimension 0, may hold values from -135 to 135
- keys: bfloat16 [32, 384, 512], P(('groups', 'rows')), parts along dimension 0, may hold values from -4.5 to 4.5
- values: bfloat16 [32, 384, 512], P(('groups', 'rows')), parts along dimension 0, may hold values from -4.5 to 4.5
- lengths: int32 [32], P(('groups', 'rows')), parts along dimension 0, may hold values from 2 to 384
- resid: bfloat16 [32, 4096], P(('groups', 'rows')), parts along dimension 0, may hold values from -6 to 6
- out_weight: bfloat16 [4096, 4096], P('rows'), may hold values from -0.09375 to 0.09375
- chat_ids: int32 [256], replicated, may hold values from 0 to 8191, as said below
- enc_weight: bfloat16 [4096, 8192], P(None, 'rows'), may hold values from -0.09375 to 0.09375
- enc_bias: float32 [8192], P('rows'), may hold values from -3 to 3
- dec_weight: bfloat16 [8192, 4096], P('rows'), may hold values from -0.09375 to 0.09375
- dec_bias: float32 [4096], replicated, may hold values from -3 to 3
Outputs:
- spliced: bfloat16 [32, 4096], P(('groups', 'rows')), parts along dimension 0
- activity: bfloat16 [32, 8192], P('groups', 'rows'), parts along dimension 0
There are 2 independent parts, one for each index of `groups`. A program takes and returns all parts, laid end to end along the dimension named above; an argument that names none is the same for every part. Nothing has to cross between parts.
Inputs may be any that keep to these rules, and one draw needn't show every extreme that they name: `chat_ids`: 256 distinct latent numbers.
All inputs are finite; a program needn't handle non-finite values.
Results may differ from a plain program's by a relative error of at most 0.0057.
Values may be sent and summed in bfloat16 or wider, within the bound.
No kernel may reach another device: no remote copies, remote signals or barrier semaphores. Data moves between devices by JAX's collectives and lax.ppermute only.
A program may use at most 64 MiB of HBM per device.

v0:
```python
import jax
import jax.numpy as jnp
from jax import lax
from jax.sharding import PartitionSpec as P

HEAD_DIM = 128


def shards(
    queries,
    keys,
    values,
    lengths,
    resid,
    out_weight,
    chat_ids,
    enc_weight,
    enc_bias,
    dec_weight,
    dec_bias,
):
    rows_here = queries.shape[0]
    cache_span = keys.shape[1]
    key_width = keys.shape[2]
    kv_count = key_width // HEAD_DIM
    group_size = queries.shape[1] // key_width
    query_heads = queries.reshape(rows_here, kv_count, group_size, HEAD_DIM)
    key_heads = keys.reshape(rows_here, cache_span, kv_count, HEAD_DIM)
    value_heads = values.reshape(rows_here, cache_span, kv_count, HEAD_DIM)
    scores = jnp.einsum(
        "rkgd,rskd->rkgs", query_heads, key_heads, preferred_element_type=jnp.float32
    )
    scores = scores / jnp.sqrt(jnp.float32(HEAD_DIM))
    visible = lax.broadcasted_iota(jnp.int32, (rows_here, cache_span), 1) < lengths[:, None]
    scores = jnp.where(visible[:, None, None, :], scores, -jnp.inf)
    highest = jnp.max(scores, axis=-1, keepdims=True)
    expo = jnp.exp(scores - highest)
    weights = (expo / jnp.sum(expo, axis=-1, keepdims=True)).astype(jnp.bfloat16)
    attended = jnp.einsum(
        "rkgs,rskd->rkgd", weights, value_heads, preferred_element_type=jnp.float32
    )
    attended = attended.astype(jnp.bfloat16).reshape(rows_here, kv_count * group_size * HEAD_DIM)
    features = lax.all_to_all(attended, "rows", split_axis=1, concat_axis=0, tiled=True)
    partial_value = jnp.dot(features, out_weight, preferred_element_type=jnp.float32)
    lat_here = enc_weight.shape[1]
    latent_ids = lax.axis_index("rows") * lat_here + lax.broadcasted_iota(jnp.int32, (lat_here,), 0)
    listed = jnp.any(chat_ids[:, None] == latent_ids[None, :], axis=0)
    row_start = lax.axis_index("rows") * rows_here
    own_rows = lax.dynamic_slice_in_dim(partial_value, row_start, rows_here, 0) + resid.astype(
        jnp.float32
    )
    partial_value = lax.dynamic_update_slice_in_dim(partial_value, own_rows, row_start, 0)
    hidden = lax.psum(partial_value, "rows").astype(jnp.bfloat16)
    activity = jnp.where(
        listed[None, :],
        0.0,
        jax.nn.relu(
            jnp.dot(hidden, enc_weight, preferred_element_type=jnp.float32) + enc_bias[None, :]
        ),
    ).astype(jnp.bfloat16)
    rebuilt = lax.psum_scatter(
        jnp.dot(activity, dec_weight, preferred_element_type=jnp.float32),
        "rows",
        scatter_dimension=0,
        tiled=True,
    )
    spliced = (rebuilt + dec_bias[None, :]).astype(jnp.bfloat16)
    return (spliced, activity)


def solution(mesh):
    placed = (
        P(("groups", "rows"), None),
        P(("groups", "rows"), None, None),
        P(("groups", "rows"), None, None),
        P(("groups", "rows")),
        P(("groups", "rows"), None),
        P("rows", None),
        P(),
        P(None, "rows"),
        P("rows"),
        P("rows", None),
        P(),
    )
    return jax.shard_map(
        shards,
        mesh=mesh,
        in_specs=placed,
        out_specs=(P(("groups", "rows"), None), P("groups", "rows")),
        check_vma=False,
    )
```

profile of v0, /device:TPU:0, one launch (start us, length us, event | category | flops | bytes accessed | tf_op | source)
XLA Modules:
  0.0 189.1 jit_solution(12662302225228097001)
XLA Ops:
  7.2 0.0 copy-start
  7.2 0.0 copy-start.3
  7.2 0.0 copy-start.5
  7.2 1.2 reshape.68
  9.1 0.8 reduce.4
  9.9 0.2 fusion.3
  10.1 0.2 fusion.16
  10.3 1.1 reshape.69
  11.4 0.2 convolution_convert_fusion
  11.7 0.5 broadcast.26
  12.2 0.7 reduce.5
  12.9 0.6 reshape.72
  13.5 7.4 %all-to-all-start = ((bf16[16,2,128]{2,1,0:T(2,128)(2,1)}), bf16[16,2,128]{2,1,0:T(2,128)(2,1)S(1)}, u32[]{:S(2)}, u32[]{:S(2)}) async-start(bf16[16,2,128]{2,1,0:T(2,128)(2,1)} %reshape.72), calls=%async_computation | async-start | bytes 16384 | tf_op jit(solution)/shard_map/all_to_all | solution.py:43
  20.9 0.0 all-reduce.4.cloned.1.call-start
  20.9 0.8 compare_reduce_fusion
  21.8 5.5 %all-to-all-done = bf16[16,2,128]{2,1,0:T(2,128)(2,1)S(1)} async-done(((bf16[16,2,128]{2,1,0:T(2,128)(2,1)}), bf16[16,2,128]{2,1,0:T(2,128)(2,1)S(1)}, u32[]{:S(2)}, u32[]{:S(2)}) %all-to-all-start) | async-done | bytes 8224 | tf_op jit(solution)/shard_map/all_to_all | solution.py:43
  27.3 0.0 copy-done
  27.3 0.4 fusion.13
  27.6 0.0 copy-done.3
  27.7 0.4 dynamic_update_slice.3
  28.1 59.8 %all-reduce.5 = bf16[16,4096]{1,0:T(8,128)(2,1)S(1)} all-reduce(f32[16,4096]{1,0:T(8,128)S(1)} %dynamic_update_slice.3), channel_id=1, replica_groups=mesh['groups'=2,'rows'=16] {'rows'}, use_global_device_ids=true, to_apply=%region_3.4 | all-reduce | flops 65536 | bytes 393216 | tf_op jit(solution)/shard_map/psum | solution.py:53
  87.9 0.0 copy-done.5
  87.9 0.0 copy-start.1
  87.9 0.0 copy-start.6
  88.0 0.0 copy-start.4
  88.0 3.0 %fusion.6 = bf16[16,512]{1,0:T(8,128)(2,1)S(1)} fusion(bf16[4096,512]{1,0:T(8,128)(2,1)} %param.18, bf16[16,4096]{1,0:T(8,128)(2,1)S(1)} %all-reduce.5, f32[512]{0:T(512)S(1)} %copy-done.5, pred[512]{0:T(512)(128)(4,1)S(1)} %compare_reduce_fusion), kind=kOutput, calls=%fused_computation.8 | convolution fusion | flops 67141632 | bytes 4344320 | tf_op jit(solution)/shard_map/dot_general | solution.py:58
  91.0 0.4 copy-done.1
  91.4 1.4 fusion.17
  92.7 0.0 all-reduce.4.cloned.1.call-update
  92.8 0.7 dynamic-slice
  93.4 86.5 %all-reduce.4.cloned.1.call-done = f32[16,4096]{1,0:T(8,128)} async-done(((f32[16,4096]{1,0:T(8,128)}), f32[16,4096]{1,0:T(8,128)}) %all-reduce.4.cloned.1.call-update) | async-done | bytes 262160
  180.0 2.2 %fusion.11 = bf16[1,4096]{1,0:T(2,128)(2,1)} fusion(f32[1,4096]{1,0:T(1,128)S(1)} %bitcast.21, f32[16,4096]{1,0:T(8,128)} %all-reduce.4.cloned.1.call-done, u32[]{:T(128)} %bitcast.2), kind=kLoop, calls=%fused_computation.17 | loop fusion | flops 8192 | bytes 40964 | tf_op jit(solution)/shard_map/convert_element_type | solution.py:67
  (9 shorter events, 0.1 us)
Async XLA Ops:
  7.2 20.1 %copy-start = (bf16[256,4096]{1,0:T(8,128)(2,1)S(1)}, bf16[256,4096]{1,0:T(8,128)(2,1)}, u32[]{:S(2)}) copy-start(bf16[256,4096]{1,0:T(8,128)(2,1)} %param.16) | copy-start | bytes 6291460
  7.2 20.5 %copy-start.3 = (bf16[1,4096]{1,0:T(2,128)(2,1)S(1)}, bf16[1,4096]{1,0:T(2,128)(2,1)}, u32[]{:S(2)}) copy-start(bf16[1,4096]{1,0:T(2,128)(2,1)} %param.15) | copy-start | bytes 24580
  7.2 80.7 %copy-start.5 = (f32[512]{0:T(512)S(1)}, f32[512]{0:T(512)}, u32[]{:S(2)}) copy-start(f32[512]{0:T(512)} %param.19) | copy-start | bytes 6148
  13.5 13.8 %all-to-all-start = ((bf16[16,2,128]{2,1,0:T(2,128)(2,1)}), bf16[16,2,128]{2,1,0:T(2,128)(2,1)S(1)}, u32[]{:S(2)}, u32[]{:S(2)}) async-start(bf16[16,2,128]{2,1,0:T(2,128)(2,1)} %reshape.72), calls=%async_computation | async-start | bytes 16384 | tf_op jit(solution)/shard_map/all_to_all | solution.py:43
  20.9 159.1 %all-reduce.4.cloned.1.call-start = ((), (), s32[]{:S(2)}) async-start(), calls=%async_computation.1 | async-start | bytes 524288
  87.9 3.5 %copy-start.1 = (bf16[512,4096]{1,0:T(8,128)(2,1)S(1)}, bf16[512,4096]{1,0:T(8,128)(2,1)}, u32[]{:S(2)}) copy-start(bf16[512,4096]{1,0:T(8,128)(2,1)} %param.20) | copy-start | bytes 12582916
  87.9 4.8 %copy-start.6 = (u32[32]{0:T(128)S(1)}, u32[32]{0:T(128)}, u32[]{:S(2)}) copy-start(u32[32]{0:T(128)} %constant.28) | copy-start | bytes 388
  88.0 92.0 %copy-start.4 = (f32[4096]{0:T(1024)S(1)}, f32[4096]{0:T(1024)}, u32[]{:S(2)}) copy-start(f32[4096]{0:T(1024)} %param.21) | copy-start | bytes 49156
  91.4 90.8 %copy-start.2 = (bf16[16,512]{1,0:T(8,128)(2,1)}, bf16[16,512]{1,0:T(8,128)(2,1)S(1)}, u32[]{:S(2)}) copy-start(bf16[16,512]{1,0:T(8,128)(2,1)S(1)} %fusion.6) | copy-start | bytes 49156
Sparse Core Ops, SparseCore 0:
  92.9 87.0 all-reduce.3
where the time goes:
time: 189 us
  waiting for transfers between devices  92 us (49%)
  blocking collectives  59.8 us (32%)
  between operations  14.8 us (8%)
  starting transfers between devices  7.43 us (4%)
  matrix products  5.2 us (3%)
  local copies, waits for them, and re-layouts  5.01 us (3%)
  other arithmetic  4.74 us (3%)
    unnamed x2, waiting for transfers between devices  86.6 us
    psum x1, blocking collectives, shards(): hidden = lax.psum(partial_value, 'rows').astype(jnp.bfloat16)  59.8 us
    all_to_all x1, starting transfers between devices, shards(): lax.all_to_all(attended, 'rows', split_axis=1, concat_axis=0, tiled=True)  7.39 us
    all_to_all x1, waiting for transfers between devices, shards(): lax.all_to_all(attended, 'rows', split_axis=1, concat_axis=0, tiled=True)  5.46 us
  transfers between devices with their start and end apart: 2, of which 2 were waited for; matrix products, arithmetic and copies ran while one was open for 1% of the time, Pallas kernels for 0%

commit v1 on v0

--- a/solution.py
+++ b/solution.py
@@ -4,6 +4,16 @@
 from jax.sharding import PartitionSpec as P
 
 HEAD_DIM = 128
+
+
+def gather_rows(x, count):
+    copies = jnp.broadcast_to(x[None], (count,) + x.shape).reshape((count * x.shape[0],) + x.shape[1:])
+    return lax.all_to_all(copies, "rows", split_axis=0, concat_axis=0, tiled=True)
+
+
+def scatter_rows(x, count):
+    got = lax.all_to_all(x, "rows", split_axis=0, concat_axis=0, tiled=True)
+    return got.reshape((count, x.shape[0] // count) + x.shape[1:]).sum(axis=0)
 
 
 def shards(
@@ -19,6 +29,7 @@
     dec_weight,
     dec_bias,
 ):
+    count = lax.axis_size("rows")
     rows_here = queries.shape[0]
     cache_span = keys.shape[1]
     key_width = keys.shape[2]
@@ -42,15 +53,11 @@
     attended = attended.astype(jnp.bfloat16).reshape(rows_here, kv_count * group_size * HEAD_DIM)
     features = lax.all_to_all(attended, "rows", split_axis=1, concat_axis=0, tiled=True)
     partial_value = jnp.dot(features, out_weight, preferred_element_type=jnp.float32)
+    hidden_here = (scatter_rows(partial_value, count) + resid.astype(jnp.float32)).astype(jnp.bfloat16)
+    hidden = gather_rows(hidden_here, count)
     lat_here = enc_weight.shape[1]
     latent_ids = lax.axis_index("rows") * lat_here + lax.broadcasted_iota(jnp.int32, (lat_here,), 0)
     listed = jnp.any(chat_ids[:, None] == latent_ids[None, :], axis=0)
-    row_start = lax.axis_index("rows") * rows_here
-    own_rows = lax.dynamic_slice_in_dim(partial_value, row_start, rows_here, 0) + resid.astype(
-        jnp.float32
-    )
-    partial_value = lax.dynamic_update_slice_in_dim(partial_value, own_rows, row_start, 0)
-    hidden = lax.psum(partial_value, "rows").astype(jnp.bfloat16)
     activity = jnp.where(
         listed[None, :],
         0.0,
@@ -58,12 +65,7 @@
             jnp.dot(hidden, enc_weight, preferred_element_type=jnp.float32) + enc_bias[None, :]
         ),
     ).astype(jnp.bfloat16)
-    rebuilt = lax.psum_scatter(
-        jnp.dot(activity, dec_weight, preferred_element_type=jnp.float32),
-        "rows",
-        scatter_dimension=0,
-        tiled=True,
-    )
+    rebuilt = scatter_rows(jnp.dot(activity, dec_weight, preferred_element_type=jnp.float32), count)
     spliced = (rebuilt + dec_bias[None, :]).astype(jnp.bfloat16)
     return (spliced, activity)
 

time: 189 us -> 65.6 us (0.35)
  waiting for transfers between devices: 92 us -> 7.69 us
  blocking collectives: 59.8 us -> 38.9 us
  between operations: 14.8 us -> 1.61 us
  starting transfers between devices: 7.43 us -> 3.51 us
    unnamed x2 -> x0, waiting for transfers between devices: 86.6 us -> none
    psum x1 -> x0, blocking collectives: 59.8 us -> none  [shards(): hidden = lax.psum(partial_value, 'rows').astype(jnp.bfloat16)]
    all_to_all x0 -> x3, blocking collectives: none -> 38.9 us  [the longest x2 25.2 us: scatter_rows(): got = lax.all_to_all(x, 'rows', split_axis=0, concat_axis=0, tiled=True)]
    all_to_all x1, starting transfers between devices: 7.39 us -> 3.51 us  [gather_rows(): lax.all_to_all(copies, 'rows', split_axis=0, concat_axis=0, tiled=True)]
    all_to_all x1, waiting for transfers between devices: 5.46 us -> 7.69 us  [gather_rows(): lax.all_to_all(copies, 'rows', split_axis=0, concat_axis=0, tiled=True)]
    convert_element_type x1, other arithmetic: 2.22 us -> 0.01 us  [shards(): spliced = (rebuilt + dec_bias[None, :]).astype(jnp.bfloat16)]
  transfers between devices with their start and end apart: 2 -> 1, of which waited for: 2 -> 1; matrix products, arithmetic and copies ran while one was open for 1% -> 0% of each run, Pallas kernels for 0% -> 0%
where the time goes in v1:
time: 65.6 us; the launch traced here: 65.2 us
  blocking collectives  38.9 us (59%)
  waiting for transfers between devices  7.69 us (12%)
  local copies, waits for them, and re-layouts  5.41 us (8%)
  matrix products  4.51 us (7%)
  other arithmetic  3.61 us (6%)
  starting transfers between devices  3.51 us (5%)
  between operations  1.61 us (2%)
    all_to_all x2, blocking collectives, scatter_rows(): got = lax.all_to_all(x, 'rows', split_axis=0, concat_axis=0, tiled=True)  25.2 us
    all_to_all x1, blocking collectives, shards(): lax.all_to_all(attended, 'rows', split_axis=1, concat_axis=0, tiled=True)  13.6 us
    all_to_all x1, waiting for transfers between devices, gather_rows(): lax.all_to_all(copies, 'rows', split_axis=0, concat_axis=0, tiled=True)  7.69 us
    all_to_all x1, starting transfers between devices, gather_rows(): lax.all_to_all(copies, 'rows', split_axis=0, concat_axis=0, tiled=True)  3.51 us
    dot_general x1, matrix products, shards(): jnp.dot(hidden, enc_weight, preferred_element_type=jnp.float32)  2.99 us
    another operation x2, local copies, waits for them, and re-layouts  2.18 us
    unnamed x19, local copies, waits for them, and re-layouts  1.85 us
    unnamed x2, other arithmetic  1.46 us
  transfers between devices with their start and end apart: 1, of which 1 were waited for; matrix products, arithmetic and copies ran while one was open for 0% of the time, Pallas kernels for 0%

profile of v1, /device:TPU:0, one launch (start us, length us, event | category | flops | bytes accessed | tf_op | source)
XLA Modules:
  0.0 65.2 jit_solution(6879873016694861597)
XLA Ops:
  0.6 0.0 copy-start
  1.5 1.1 %reshape.92 = bf16[384,4,128]{2,1,0:T(4,128)(2,1)S(1)} reshape(bf16[1,384,512]{2,1,0:T(8,128)(2,1)} %param.12) | data formatting | bytes 786432 | tf_op jit(solution)/shard_map/reshape.3
  2.6 0.8 %reduce.10 = bf16[4096]{0:T(1024)(128)(2,1)S(1)} reduce(bf16[1,4096]{1,0:T(2,128)(2,1)} %param.11, bf16[]{:T(256)} %constant.22), dimensions={0}, to_apply=%param.11.reduce_sub_computation | reduce | bytes 16386 | tf_op args[0]
  3.3 0.2 fusion.3
  3.6 0.2 fusion.15
  3.8 1.1 %reshape.93 = bf16[384,4,128]{2,1,0:T(4,128)(2,1)S(1)} reshape(bf16[1,384,512]{2,1,0:T(8,128)(2,1)} %param.13) | data formatting | bytes 786432 | tf_op jit(solution)/shard_map/reshape.15
  4.9 0.2 convolution_convert_fusion
  5.1 0.5 broadcast.33
  5.7 0.7 %reduce.13 = bf16[16,256]{1,0:T(8,128)(2,1)S(1)} reduce(bf16[16,1,256]{2,1,0:T(2,128)(2,1)S(1)} %bitcast.25, bf16[]{:T(256)} %broadcast.33), dimensions={1}, to_apply=%bitcast.15.reduce_sub_computation | reduce | bytes 16386
  6.4 13.6 %all_to_all.44 = bf16[16,2,128]{2,1,0:T(2,128)(2,1)S(1)} all-to-all(bf16[16,2,128]{2,1,0:T(2,128)(2,1)S(1)} %reshape.97), channel_id=1, replica_groups=mesh['groups'=2,'rows'=16] {'rows'}, dimensions={0} | all-to-all | bytes 16384 | tf_op jit(solution)/shard_map/all_to_all | solution.py:54
  20.0 0.4 convolution_bitcast_fusion.1
  20.4 0.3 copy.30
  20.7 12.6 %all_to_all.45 = f32[16,1,4096]{2,1,0:T(1,128)S(1)} all-to-all(f32[16,1,4096]{2,1,0:T(1,128)S(1)} %copy.30), channel_id=1, replica_groups=mesh['groups'=2,'rows'=16] {'rows'}, dimensions={0} | all-to-all | bytes 524288 | tf_op jit(solution)/shard_map/all_to_all | solution.py:15
  33.3 0.2 reduce_sum.30
  33.5 0.0 copy-done.3
  33.5 0.1 convert_reduce_fusion
  33.5 0.2 reshape.94
  33.7 1.4 %reduce.14 = bf16[16,4096]{1,0:T(8,128)(2,1)S(1)} reduce(bf16[16,1,4096]{2,1,0:T(2,128)(2,1)S(1)} %reshape.94, bf16[]{:T(256)} %broadcast.33), dimensions={1}, to_apply=%reshape.94.reduce_sub_computation | reduce | bytes 262146 | tf_op jit(solution)/shard_map/reshape | solution.py:10
  35.1 0.7 %reshape.99 = bf16[16,2,2048]{2,1,0:T(2,128)(2,1)} reshape(bf16[16,4096]{1,0:T(8,128)(2,1)S(1)} %reduce.14) | data formatting | bytes 262144
  35.8 3.5 %all-to-all-start.2 = ((bf16[16,2,2048]{2,1,0:T(2,128)(2,1)}), bf16[16,2,2048]{2,1,0:T(2,128)(2,1)S(1)}, u32[]{:S(2)}, u32[]{:S(2)}) async-start(bf16[16,2,2048]{2,1,0:T(2,128)(2,1)} %reshape.99), calls=%async_computation.2 | async-start | bytes 262144 | tf_op jit(solution)/shard_map/all_to_all | solution.py:11
  39.4 0.2 compare_reduce_fusion
  39.5 7.7 %all-to-all-done.2 = bf16[16,2,2048]{2,1,0:T(2,128)(2,1)S(1)} async-done(((bf16[16,2,2048]{2,1,0:T(2,128)(2,1)}), bf16[16,2,2048]{2,1,0:T(2,128)(2,1)S(1)}, u32[]{:S(2)}, u32[]{:S(2)}) %all-to-all-start.2) | async-done | bytes 131104 | tf_op jit(solution)/shard_map/all_to_all | solution.py:11
  47.2 0.1 reshape.100
  47.4 0.0 copy-start.1
  47.4 0.0 copy-start.4
  47.4 3.0 %fusion.6 = bf16[16,512]{1,0:T(8,128)(2,1)S(1)} fusion(bf16[4096,512]{1,0:T(8,128)(2,1)} %param.18, bf16[16,1,4096]{2,1,0:T(2,128)(2,1)S(1)} %reshape.100, f32[512]{0:T(512)S(1)} %copy-done.5, pred[512]{0:T(512)(128)(4,1)S(1)} %compare_reduce_fusion), kind=kOutput, calls=%fused_computation.10 | convolution fusion | flops 67141632 | bytes 4344320 | tf_op jit(solution)/shard_map/dot_general | solution.py:65
  50.4 0.4 copy-done.1
  50.8 0.7 %convolution_bitcast_fusion = f32[16,1,4096]{2,0,1:T(8,128)S(1)} fusion(bf16[16,512]{1,0:T(8,128)(2,1)S(1)} %fusion.6, bf16[512,4096]{1,0:T(8,128)(2,1)S(1)} %copy-done.1), kind=kOutput, calls=%fused_computation.1 | convolution fusion | flops 67108864 | bytes 4472832 | tf_op jit(solution)/shard_map/dot_general | solution.py:68
  51.5 0.3 copy.31
  51.8 12.6 %all_to_all.46 = f32[16,1,4096]{2,1,0:T(1,128)S(1)} all-to-all(f32[16,1,4096]{2,1,0:T(1,128)S(1)} %copy.31), channel_id=1, replica_groups=mesh['groups'=2,'rows'=16] {'rows'}, dimensions={0} | all-to-all | bytes 524288 | tf_op jit(solution)/shard_map/all_to_all | solution.py:15
  64.4 0.2 reduce_sum.32
  64.6 0.6 convert_element_type.32
  (15 shorter events, 0.1 us)
Async XLA Ops:
  0.6 19.4 %copy-start = (bf16[256,4096]{1,0:T(8,128)(2,1)S(1)}, bf16[256,4096]{1,0:T(8,128)(2,1)}, u32[]{:S(2)}) copy-start(bf16[256,4096]{1,0:T(8,128)(2,1)} %param.16) | copy-start | bytes 6291460
  0.6 32.8 %copy-start.3 = (bf16[1,4096]{1,0:T(2,128)(2,1)S(1)}, bf16[1,4096]{1,0:T(2,128)(2,1)}, u32[]{:S(2)}) copy-start(bf16[1,4096]{1,0:T(2,128)(2,1)} %param.15) | copy-start | bytes 24580
  0.7 38.7 %copy-start.6 = (s32[256]{0:T(256)S(1)}, s32[256]{0:T(256)}, u32[]{:S(2)}) copy-start(s32[256]{0:T(256)} %param.17) | copy-start | bytes 3076
  0.7 46.7 %copy-start.5 = (f32[512]{0:T(512)S(1)}, f32[512]{0:T(512)}, u32[]{:S(2)}) copy-start(f32[512]{0:T(512)} %param.19) | copy-start | bytes 6148
  35.8 11.4 %all-to-all-start.2 = ((bf16[16,2,2048]{2,1,0:T(2,128)(2,1)}), bf16[16,2,2048]{2,1,0:T(2,128)(2,1)S(1)}, u32[]{:S(2)}, u32[]{:S(2)}) async-start(bf16[16,2,2048]{2,1,0:T(2,128)(2,1)} %reshape.99), calls=%async_computation.2 | async-start | bytes 262144 | tf_op jit(solution)/shard_map/all_to_all | solution.py:11
  47.4 3.5 %copy-start.1 = (bf16[512,4096]{1,0:T(8,128)(2,1)S(1)}, bf16[512,4096]{1,0:T(8,128)(2,1)}, u32[]{:S(2)}) copy-start(bf16[512,4096]{1,0:T(8,128)(2,1)} %param.20) | copy-start | bytes 12582916
  47.4 17.2 %copy-start.4 = (f32[4096]{0:T(1024)S(1)}, f32[4096]{0:T(1024)}, u32[]{:S(2)}) copy-start(f32[4096]{0:T(1024)} %param.21) | copy-start | bytes 49156
  50.8 14.4 %copy-start.2 = (bf16[16,512]{1,0:T(8,128)(2,1)}, bf16[16,512]{1,0:T(8,128)(2,1)S(1)}, u32[]{:S(2)}) copy-start(bf16[16,512]{1,0:T(8,128)(2,1)S(1)} %fusion.6) | copy-start | bytes 49156

commit v2 on v1

--- a/solution.py
+++ b/solution.py
@@ -1,13 +1,60 @@
+import math
+
 import jax
 import jax.numpy as jnp
 from jax import lax
+from jax.experimental import pallas as pl
+from jax.experimental.pallas import tpu as pltpu
 from jax.sharding import PartitionSpec as P
 
 HEAD_DIM = 128
 
 
+def attend_kernel(len_ref, q_ref, k_ref, v_ref, o_ref):
+    span = k_ref.shape[1]
+    kv_count = k_ref.shape[2] // HEAD_DIM
+    group_size = q_ref.shape[1] // kv_count
+    live = len_ref[pl.program_id(0)]
+    queries = q_ref[0].astype(jnp.float32)
+    scale = jnp.float32(math.sqrt(HEAD_DIM))
+    outs = []
+    for k in range(kv_count):
+        qk = queries[k * group_size:(k + 1) * group_size].astype(jnp.bfloat16)
+        kk = k_ref[0, :, k * HEAD_DIM:(k + 1) * HEAD_DIM]
+        s = lax.dot_general(qk, kk, (((1,), (1,)), ((), ())), preferred_element_type=jnp.float32)
+        s = s / scale
+        pos = lax.broadcasted_iota(jnp.int32, s.shape, 1)
+        s = jnp.where(pos < live, s, -jnp.inf)
+        e = jnp.exp(s - jnp.max(s, axis=-1, keepdims=True))
+        w = (e / jnp.sum(e, axis=-1, keepdims=True)).astype(jnp.bfloat16)
+        vk = v_ref[0, :, k * HEAD_DIM:(k + 1) * HEAD_DIM]
+        outs.append(jnp.dot(w, vk, preferred_element_type=jnp.float32))
+    o_ref[0] = jnp.concatenate(outs, axis=0).astype(o_ref.dtype)
+
+
+def attend(queries, keys, values, lengths):
+    rows_here, span, key_width = keys.shape
+    heads = queries.shape[1] // HEAD_DIM
+    q3 = queries.reshape(rows_here, heads, HEAD_DIM)
+    grid_spec = pltpu.PrefetchScalarGridSpec(
+        num_scalar_prefetch=1,
+        grid=(rows_here,),
+        in_specs=[
+            pl.BlockSpec((1, heads, HEAD_DIM), lambda i, n: (i, 0, 0)),
+            pl.BlockSpec((1, span, key_width), lambda i, n: (i, 0, 0)),
+            pl.BlockSpec((1, span, key_width), lambda i, n: (i, 0, 0)),
+        ],
+        out_specs=pl.BlockSpec((1, heads, HEAD_DIM), lambda i, n: (i, 0, 0)),
+    )
+    return pl.pallas_call(
+        attend_kernel,
+        grid_spec=grid_spec,
+        out_shape=jax.ShapeDtypeStruct((rows_here, heads, HEAD_DIM), jnp.bfloat16),
+    )(lengths, q3, keys, values)
+
+
 def gather_rows(x, count):
-    copies = jnp.broadcast_to(x[None], (count,) + x.shape).reshape((count * x.shape[0],) + x.shape[1:])
+    copies = jnp.tile(x, (count, 1))
     return lax.all_to_all(copies, "rows", split_axis=0, concat_axis=0, tiled=True)
 
 
@@ -31,26 +78,8 @@
 ):
     count = lax.axis_size("rows")
     rows_here = queries.shape[0]
-    cache_span = keys.shape[1]
-    key_width = keys.shape[2]
-    kv_count = key_width // HEAD_DIM
-    group_size = queries.shape[1] // key_width
-    query_heads = queries.reshape(rows_here, kv_count, group_size, HEAD_DIM)
-    key_heads = keys.reshape(rows_here, cache_span, kv_count, HEAD_DIM)
-    value_heads = values.reshape(rows_here, cache_span, kv_count, HEAD_DIM)
-    scores = jnp.einsum(
-        "rkgd,rskd->rkgs", query_heads, key_heads, preferred_element_type=jnp.float32
-    )
-    scores = scores / jnp.sqrt(jnp.float32(HEAD_DIM))
-    visible = lax.broadcasted_iota(jnp.int32, (rows_here, cache_span), 1) < lengths[:, None]
-    scores = jnp.where(visible[:, None, None, :], scores, -jnp.inf)
-    highest = jnp.max(scores, axis=-1, keepdims=True)
-    expo = jnp.exp(scores - highest)
-    weights = (expo / jnp.sum(expo, axis=-1, keepdims=True)).astype(jnp.bfloat16)
-    attended = jnp.einsum(
-        "rkgs,rskd->rkgd", weights, value_heads, preferred_element_type=jnp.float32
-    )
-    attended = attended.astype(jnp.bfloat16).reshape(rows_here, kv_count * group_size * HEAD_DIM)
+    attended = attend(queries, keys, values, lengths)
+    attended = attended.reshape(rows_here, attended.shape[1] * HEAD_DIM)
     features = lax.all_to_all(attended, "rows", split_axis=1, concat_axis=0, tiled=True)
     partial_value = jnp.dot(features, out_weight, preferred_element_type=jnp.float32)
     hidden_here = (scatter_rows(partial_value, count) + resid.astype(jnp.float32)).astype(jnp.bfloat16)

time: 65.6 us -> 67.2 us (1.024)
  Pallas kernels: 0 us -> 3.12 us
  local copies, waits for them, and re-layouts: 5.41 us -> 3.9 us
    pallas_call x0 -> x1, Pallas kernels: none -> 3.12 us  [attend(): pl.pallas_call(attend_kernel, grid_spec=grid_spec, out_shape=jax.ShapeDty...]
    another operation x2 -> x1, local copies, waits for them, and re-layouts: 2.18 us -> 0.2 us  [gather_rows(): copies = jnp.tile(x, (count, 1))]
    reshape x1 -> x0, other arithmetic: 1.38 us -> none  [gather_rows(): jnp.broadcast_to(x[None], (count,) + x.shape)]
    another operation x0 -> x1, other arithmetic: none -> 1.38 us  [gather_rows(): copies = jnp.tile(x, (count, 1))]
    all_to_all x1, local copies, waits for them, and re-layouts: 0.02 us -> 0.71 us  [shards(): lax.all_to_all(attended, 'rows', split_axis=1, concat_axis=0, tiled=True)]
where the time goes in v2:
time: 67.2 us; the launch traced here: 66.7 us
  blocking collectives  38.9 us (58%)
  waiting for transfers between devices  7.69 us (11%)
  matrix products  4.03 us (6%)
  other arithmetic  4.01 us (6%)
  local copies, waits for them, and re-layouts  3.9 us (6%)
  starting transfers between devices  3.51 us (5%)
  Pallas kernels  3.12 us (5%)
  between operations  1.58 us (2%)
    all_to_all x2, blocking collectives, scatter_rows(): got = lax.all_to_all(x, 'rows', split_axis=0, concat_axis=0, tiled=True)  25.2 us
    all_to_all x1, blocking collectives, shards(): lax.all_to_all(attended, 'rows', split_axis=1, concat_axis=0, tiled=True)  13.6 us
    all_to_all x1, waiting for transfers between devices, gather_rows(): lax.all_to_all(copies, 'rows', split_axis=0, concat_axis=0, tiled=True)  7.69 us
    all_to_all x1, starting transfers between devices, gather_rows(): lax.all_to_all(copies, 'rows', split_axis=0, concat_axis=0, tiled=True)  3.51 us
    pallas_call x1, Pallas kernels, attend(): pl.pallas_call(attend_kernel, grid_spec=grid_spec, out_shape=jax.ShapeDty...  3.12 us
    dot_general x1, matrix products, shards(): jnp.dot(hidden, enc_weight, preferred_element_type=jnp.float32)  2.99 us
    unnamed x2, other arithmetic  2.06 us
    unnamed x19, local copies, waits for them, and re-layouts  1.84 us
  transfers between devices with their start and end apart: 1, of which 1 were waited for; matrix products, arithmetic and copies ran while one was open for 0% of the time, Pallas kernels for 0%

profile of v2, /device:TPU:0, one launch (start us, length us, event | category | flops | bytes accessed | tf_op | source)
XLA Modules:
  0.0 66.7 jit_solution(11050109525276373732)
XLA Ops:
  0.6 0.0 copy-start
  1.5 1.4 %reduce.6 = bf16[4096]{0:T(1024)(128)(2,1)} reduce(bf16[1,4096]{1,0:T(2,128)(2,1)} %param.11, bf16[]{:T(256)} %constant.17), dimensions={0}, to_apply=%param.11.reduce_sub_computation | reduce | bytes 16386 | tf_op args[0]
  2.8 3.1 %shard_map.122 = bf16[1,32,128]{2,1,0:T(8,128)(2,1)} custom-call(s32[1]{0:T(128)S(6)} %copy.32.len_ref, bf16[1,32,128]{2,1,0:T(8,128)(2,1)} %bitcast.21, bf16[1,384,512]{2,1,0:T(8,128)(2,1)} %k_ref.1, bf16[1,384,512]{2,1,0:T(8,128)(2,1)} %v_ref.1), custom_call_target="tpu_custom_call" | custom-call | tf_op jit(solution)/shard_map/pallas_call | solution.py:49
  6.0 0.7 %all_to_all.39 = bf16[1,16,256]{2,0,1:T(2,128)(2,1)S(1)} reshape(bf16[1,32,128]{2,1,0:T(8,128)(2,1)} %shard_map.122) | data formatting | bytes 16384 | tf_op jit(solution)/shard_map/all_to_all | solution.py:83
  6.7 0.5 broadcast.15
  7.2 0.7 %reduce.9 = bf16[16,256]{1,0:T(8,128)(2,1)S(1)} reduce(bf16[16,1,256]{2,1,0:T(2,128)(2,1)S(1)} %bitcast.19, bf16[]{:T(256)} %broadcast.15), dimensions={1}, to_apply=%bitcast.12.reduce_sub_computation | reduce | bytes 16386
  7.9 13.6 %all_to_all.44 = bf16[16,2,128]{2,1,0:T(2,128)(2,1)S(1)} all-to-all(bf16[16,2,128]{2,1,0:T(2,128)(2,1)S(1)} %reshape.46), channel_id=1, replica_groups=mesh['groups'=2,'rows'=16] {'rows'}, dimensions={0} | all-to-all | bytes 16384 | tf_op jit(solution)/shard_map/all_to_all | solution.py:83
  21.5 0.0 copy-done
  21.5 0.4 convolution_bitcast_fusion.1
  21.9 0.3 copy.20
  22.2 12.6 %all_to_all.45 = f32[16,1,4096]{2,1,0:T(1,128)S(1)} all-to-all(f32[16,1,4096]{2,1,0:T(1,128)S(1)} %copy.20), channel_id=1, replica_groups=mesh['groups'=2,'rows'=16] {'rows'}, dimensions={0} | all-to-all | bytes 524288 | tf_op jit(solution)/shard_map/all_to_all | solution.py:62
  34.8 0.2 reduce_sum.20
  35.0 0.1 convert_reduce_fusion
  35.0 0.2 tile.2
  35.3 1.4 %reduce.10 = bf16[16,4096]{1,0:T(8,128)(2,1)S(1)} reduce(bf16[16,1,4096]{2,1,0:T(2,128)(2,1)S(1)} %tile.2, bf16[]{:T(256)} %broadcast.15), dimensions={1}, to_apply=%tile.2.reduce_sub_computation | reduce | bytes 262146 | tf_op jit(solution)/shard_map/tile | solution.py:57
  36.6 0.7 %reshape.48 = bf16[16,2,2048]{2,1,0:T(2,128)(2,1)} reshape(bf16[16,4096]{1,0:T(8,128)(2,1)S(1)} %reduce.10) | data formatting | bytes 262144
  37.4 3.5 %all-to-all-start.2 = ((bf16[16,2,2048]{2,1,0:T(2,128)(2,1)}), bf16[16,2,2048]{2,1,0:T(2,128)(2,1)S(1)}, u32[]{:S(2)}, u32[]{:S(2)}) async-start(bf16[16,2,2048]{2,1,0:T(2,128)(2,1)} %reshape.48), calls=%async_computation.2 | async-start | bytes 262144 | tf_op jit(solution)/shard_map/all_to_all | solution.py:58
  40.9 0.2 compare_reduce_fusion
  41.0 7.7 %all-to-all-done.2 = bf16[16,2,2048]{2,1,0:T(2,128)(2,1)S(1)} async-done(((bf16[16,2,2048]{2,1,0:T(2,128)(2,1)}), bf16[16,2,2048]{2,1,0:T(2,128)(2,1)S(1)}, u32[]{:S(2)}, u32[]{:S(2)}) %all-to-all-start.2) | async-done | bytes 131104 | tf_op jit(solution)/shard_map/all_to_all | solution.py:58
  48.7 0.1 reshape.49
  48.9 0.0 copy-done.5
  48.9 0.0 copy-start.1
  48.9 0.0 copy-start.4
  48.9 3.0 %fusion.2 = bf16[16,512]{1,0:T(8,128)(2,1)S(1)} fusion(bf16[4096,512]{1,0:T(8,128)(2,1)} %param.18, bf16[16,1,4096]{2,1,0:T(2,128)(2,1)S(1)} %reshape.49, f32[512]{0:T(512)S(1)} %copy-done.5, pred[512]{0:T(512)(128)(4,1)S(1)} %compare_reduce_fusion), kind=kOutput, calls=%fused_computation.5 | convolution fusion | flops 67141632 | bytes 4344320 | tf_op jit(solution)/shard_map/dot_general | solution.py:94
  51.9 0.4 copy-done.1
  52.3 0.7 convolution_bitcast_fusion
  53.0 0.3 copy.21
  53.3 12.6 %all_to_all.46 = f32[16,1,4096]{2,1,0:T(1,128)S(1)} all-to-all(f32[16,1,4096]{2,1,0:T(1,128)S(1)} %copy.21), channel_id=1, replica_groups=mesh['groups'=2,'rows'=16] {'rows'}, dimensions={0} | all-to-all | bytes 524288 | tf_op jit(solution)/shard_map/all_to_all | solution.py:62
  65.9 0.2 reduce_sum.22
  66.1 0.0 copy-done.4
  66.1 0.6 convert_element_type.22
  66.7 0.0 copy-done.2
  (10 shorter events, 0.0 us)
Async XLA Ops:
  0.6 20.9 %copy-start = (bf16[256,4096]{1,0:T(8,128)(2,1)S(1)}, bf16[256,4096]{1,0:T(8,128)(2,1)}, u32[]{:S(2)}) copy-start(bf16[256,4096]{1,0:T(8,128)(2,1)} %param.16) | copy-start | bytes 6291460
  0.6 34.3 %copy-start.3 = (bf16[1,4096]{1,0:T(2,128)(2,1)S(1)}, bf16[1,4096]{1,0:T(2,128)(2,1)}, u32[]{:S(2)}) copy-start(bf16[1,4096]{1,0:T(2,128)(2,1)} %param.15) | copy-start | bytes 24580
  0.7 40.2 %copy-start.6 = (s32[256]{0:T(256)S(1)}, s32[256]{0:T(256)}, u32[]{:S(2)}) copy-start(s32[256]{0:T(256)} %param.17) | copy-start | bytes 3076
  0.7 48.2 %copy-start.5 = (f32[512]{0:T(512)S(1)}, f32[512]{0:T(512)}, u32[]{:S(2)}) copy-start(f32[512]{0:T(512)} %param.19) | copy-start | bytes 6148
  37.4 11.4 %all-to-all-start.2 = ((bf16[16,2,2048]{2,1,0:T(2,128)(2,1)}), bf16[16,2,2048]{2,1,0:T(2,128)(2,1)S(1)}, u32[]{:S(2)}, u32[]{:S(2)}) async-start(bf16[16,2,2048]{2,1,0:T(2,128)(2,1)} %reshape.48), calls=%async_computation.2 | async-start | bytes 262144 | tf_op jit(solution)/shard_map/all_to_all | solution.py:58
  48.9 3.5 %copy-start.1 = (bf16[512,4096]{1,0:T(8,128)(2,1)S(1)}, bf16[512,4096]{1,0:T(8,128)(2,1)}, u32[]{:S(2)}) copy-start(bf16[512,4096]{1,0:T(8,128)(2,1)} %param.20) | copy-start | bytes 12582916
  48.9 17.2 %copy-start.4 = (f32[4096]{0:T(1024)S(1)}, f32[4096]{0:T(1024)}, u32[]{:S(2)}) copy-start(f32[4096]{0:T(1024)} %param.21) | copy-start | bytes 49156
  52.3 14.4 %copy-start.2 = (bf16[16,512]{1,0:T(8,128)(2,1)}, bf16[16,512]{1,0:T(8,128)(2,1)S(1)}, u32[]{:S(2)}) copy-start(bf16[16,512]{1,0:T(8,128)(2,1)S(1)} %fusion.2) | copy-start | bytes 49156

commit v3 on v1

--- a/solution.py
+++ b/solution.py
@@ -7,8 +7,10 @@
 
 
 def gather_rows(x, count):
-    copies = jnp.broadcast_to(x[None], (count,) + x.shape).reshape((count * x.shape[0],) + x.shape[1:])
-    return lax.all_to_all(copies, "rows", split_axis=0, concat_axis=0, tiled=True)
+    halves = x.reshape(2 * x.shape[0], x.shape[1] // 2)
+    copies = jnp.broadcast_to(halves[None], (count,) + halves.shape).reshape((count * halves.shape[0], halves.shape[1]))
+    got = lax.all_to_all(copies, "rows", split_axis=0, concat_axis=0, tiled=True)
+    return got.reshape(count * x.shape[0], x.shape[1])
 
 
 def scatter_rows(x, count):

time: 65.6 us -> 63.9 us (0.974)
  other arithmetic: 3.61 us -> 2.23 us
    reshape x1 -> x0, other arithmetic: 1.38 us -> none  [gather_rows(): jnp.broadcast_to(x[None], (count,) + x.shape)]
    unnamed x19 -> x18, local copies, waits for them, and re-layouts: 1.85 us -> 1.01 us
    broadcast_in_dim x0 -> x2, local copies, waits for them, and re-layouts: none -> 0.72 us  [gather_rows(): jnp.broadcast_to(halves[None], (count,) + halves.shape)]
where the time goes in v3:
time: 63.9 us; the launch traced here: 63.5 us
  blocking collectives  38.9 us (61%)
  waiting for transfers between devices  7.69 us (12%)
  local copies, waits for them, and re-layouts  5.1 us (8%)
  matrix products  4.5 us (7%)
  starting transfers between devices  3.51 us (5%)
  other arithmetic  2.23 us (3%)
  between operations  1.59 us (2%)
    all_to_all x2, blocking collectives, scatter_rows(): got = lax.all_to_all(x, 'rows', split_axis=0, concat_axis=0, tiled=True)  25.2 us
    all_to_all x1, blocking collectives, shards(): lax.all_to_all(attended, 'rows', split_axis=1, concat_axis=0, tiled=True)  13.6 us
    all_to_all x1, waiting for transfers between devices, gather_rows(): lax.all_to_all(copies, 'rows', split_axis=0, concat_axis=0, tiled=True)  7.69 us
    all_to_all x1, starting transfers between devices, gather_rows(): lax.all_to_all(copies, 'rows', split_axis=0, concat_axis=0, tiled=True)  3.51 us
    dot_general x1, matrix products, shards(): jnp.dot(hidden, enc_weight, preferred_element_type=jnp.float32)  2.98 us
    another operation x2, local copies, waits for them, and re-layouts  2.18 us
    unnamed x2, other arithmetic  1.46 us
  transfers between devices with their start and end apart: 1, of which 1 were waited for; matrix products, arithmetic and copies ran while one was open for 0% of the time, Pallas kernels for 0%

profile of v3, /device:TPU:0, one launch (start us, length us, event | category | flops | bytes accessed | tf_op | source)
XLA Modules:
  0.0 63.5 jit_solution(4677439299859494948)
XLA Ops:
  0.6 0.0 copy-start
  0.6 0.0 copy-start.3
  0.7 0.0 copy-start.6
  0.7 0.0 copy-start.5
  1.5 1.1 %reshape.89 = bf16[384,4,128]{2,1,0:T(4,128)(2,1)S(1)} reshape(bf16[1,384,512]{2,1,0:T(8,128)(2,1)} %param.12) | data formatting | bytes 786432 | tf_op jit(solution)/shard_map/reshape.3
  2.6 0.8 %reduce.10 = bf16[4096]{0:T(1024)(128)(2,1)S(1)} reduce(bf16[1,4096]{1,0:T(2,128)(2,1)} %param.11, bf16[]{:T(256)} %constant.22), dimensions={0}, to_apply=%param.11.reduce_sub_computation | reduce | bytes 16386 | tf_op args[0]
  3.3 0.2 fusion.3
  3.6 0.2 fusion.13
  3.8 1.1 %reshape.90 = bf16[384,4,128]{2,1,0:T(4,128)(2,1)S(1)} reshape(bf16[1,384,512]{2,1,0:T(8,128)(2,1)} %param.13) | data formatting | bytes 786432 | tf_op jit(solution)/shard_map/reshape.16
  4.9 0.2 convolution_convert_fusion
  5.1 0.5 broadcast.27
  5.7 0.7 %reduce.13 = bf16[16,256]{1,0:T(8,128)(2,1)S(1)} reduce(bf16[16,1,256]{2,1,0:T(2,128)(2,1)S(1)} %bitcast.27, bf16[]{:T(256)} %broadcast.27), dimensions={1}, to_apply=%bitcast.14.reduce_sub_computation | reduce | bytes 16386
  6.4 13.6 %all_to_all.41 = bf16[16,2,128]{2,1,0:T(2,128)(2,1)S(1)} all-to-all(bf16[16,2,128]{2,1,0:T(2,128)(2,1)S(1)} %reshape.94), channel_id=1, replica_groups=mesh['groups'=2,'rows'=16] {'rows'}, dimensions={0} | all-to-all | bytes 16384 | tf_op jit(solution)/shard_map/all_to_all | solution.py:56
  20.0 0.0 copy-done
  20.0 0.4 convolution_bitcast_fusion.1
  20.4 0.3 copy.28
  20.7 12.6 %all_to_all.42 = f32[16,1,4096]{2,1,0:T(1,128)S(1)} all-to-all(f32[16,1,4096]{2,1,0:T(1,128)S(1)} %copy.28), channel_id=1, replica_groups=mesh['groups'=2,'rows'=16] {'rows'}, dimensions={0} | all-to-all | bytes 524288 | tf_op jit(solution)/shard_map/all_to_all | solution.py:17
  33.3 0.2 reduce_sum.30
  33.5 0.0 copy-done.3
  33.5 0.1 convert_reduce_fusion
  33.5 0.7 %broadcast_in_dim.45 = bf16[16,2,2048]{2,1,0:T(2,128)(2,1)} broadcast(bf16[2,2048]{1,0:T(2,128)(2,1)S(1)} %broadcast_in_dim.44), dimensions={1,2} | broadcast | bytes 139264 | tf_op jit(solution)/shard_map/broadcast_in_dim | solution.py:11
  34.3 3.5 %all-to-all-start.2 = ((bf16[16,2,2048]{2,1,0:T(2,128)(2,1)}), bf16[16,2,2048]{2,1,0:T(2,128)(2,1)S(1)}, u32[]{:S(2)}, u32[]{:S(2)}) async-start(bf16[16,2,2048]{2,1,0:T(2,128)(2,1)} %broadcast_in_dim.45), calls=%async_computation.2 | async-start | bytes 262144 | tf_op jit(solution)/shard_map/all_to_all | solution.py:12
  37.8 0.2 compare_reduce_fusion
  38.0 7.7 %all-to-all-done.2 = bf16[16,2,2048]{2,1,0:T(2,128)(2,1)S(1)} async-done(((bf16[16,2,2048]{2,1,0:T(2,128)(2,1)}), bf16[16,2,2048]{2,1,0:T(2,128)(2,1)S(1)}, u32[]{:S(2)}, u32[]{:S(2)}) %all-to-all-start.2) | async-done | bytes 131104 | tf_op jit(solution)/shard_map/all_to_all | solution.py:12
  45.7 0.0 copy-start.4
  45.7 3.0 %fusion.6 = bf16[16,512]{1,0:T(8,128)(2,1)S(1)} fusion(bf16[16,4096]{1,0:T(8,128)(2,1)S(1)} %bitcast.24, bf16[4096,512]{1,0:T(8,128)(2,1)} %param.18, f32[512]{0:T(512)S(1)} %copy-done.5, pred[512]{0:T(512)(128)(4,1)S(1)} %compare_reduce_fusion), kind=kOutput, calls=%fused_computation.10 | convolution fusion | flops 67141632 | bytes 4344320 | tf_op jit(solution)/shard_map/dot_general | solution.py:67
  48.7 0.4 copy-done.1
  49.1 0.7 %convolution_bitcast_fusion = f32[16,1,4096]{2,0,1:T(8,128)S(1)} fusion(bf16[16,512]{1,0:T(8,128)(2,1)S(1)} %fusion.6, bf16[512,4096]{1,0:T(8,128)(2,1)S(1)} %copy-done.1), kind=kOutput, calls=%fused_computation.1 | convolution fusion | flops 67108864 | bytes 4472832 | tf_op jit(solution)/shard_map/dot_general | solution.py:70
  49.8 0.3 copy.29
  50.0 12.6 %all_to_all.43 = f32[16,1,4096]{2,1,0:T(1,128)S(1)} all-to-all(f32[16,1,4096]{2,1,0:T(1,128)S(1)} %copy.29), channel_id=1, replica_groups=mesh['groups'=2,'rows'=16] {'rows'}, dimensions={0} | all-to-all | bytes 524288 | tf_op jit(solution)/shard_map/all_to_all | solution.py:17
  62.6 0.2 reduce_sum.32
  62.9 0.6 convert_element_type.29
  (14 shorter events, 0.1 us)
Async XLA Ops:
  0.6 19.4 %copy-start = (bf16[256,4096]{1,0:T(8,128)(2,1)S(1)}, bf16[256,4096]{1,0:T(8,128)(2,1)}, u32[]{:S(2)}) copy-start(bf16[256,4096]{1,0:T(8,128)(2,1)} %param.16) | copy-start | bytes 6291460
  0.6 32.8 %copy-start.3 = (bf16[1,4096]{1,0:T(2,128)(2,1)S(1)}, bf16[1,4096]{1,0:T(2,128)(2,1)}, u32[]{:S(2)}) copy-start(bf16[1,4096]{1,0:T(2,128)(2,1)} %param.15) | copy-start | bytes 24580
  0.7 37.1 %copy-start.6 = (s32[256]{0:T(256)S(1)}, s32[256]{0:T(256)}, u32[]{:S(2)}) copy-start(s32[256]{0:T(256)} %param.17) | copy-start | bytes 3076
  0.7 45.0 %copy-start.5 = (f32[512]{0:T(512)S(1)}, f32[512]{0:T(512)}, u32[]{:S(2)}) copy-start(f32[512]{0:T(512)} %param.19) | copy-start | bytes 6148
  34.3 11.4 %all-to-all-start.2 = ((bf16[16,2,2048]{2,1,0:T(2,128)(2,1)}), bf16[16,2,2048]{2,1,0:T(2,128)(2,1)S(1)}, u32[]{:S(2)}, u32[]{:S(2)}) async-start(bf16[16,2,2048]{2,1,0:T(2,128)(2,1)} %broadcast_in_dim.45), calls=%async_computation.2 | async-start | bytes 262144 | tf_op jit(solution)/shard_map/all_to_all | solution.py:12
  45.6 3.4 %copy-start.1 = (bf16[512,4096]{1,0:T(8,128)(2,1)S(1)}, bf16[512,4096]{1,0:T(8,128)(2,1)}, u32[]{:S(2)}) copy-start(bf16[512,4096]{1,0:T(8,128)(2,1)} %param.20) | copy-start | bytes 12582916
  45.7 17.1 %copy-start.4 = (f32[4096]{0:T(1024)S(1)}, f32[4096]{0:T(1024)}, u32[]{:S(2)}) copy-start(f32[4096]{0:T(1024)} %param.21) | copy-start | bytes 49156
  49.1 14.4 %copy-start.2 = (bf16[16,512]{1,0:T(8,128)(2,1)}, bf16[16,512]{1,0:T(8,128)(2,1)S(1)}, u32[]{:S(2)}) copy-start(bf16[16,512]{1,0:T(8,128)(2,1)S(1)} %fusion.6) | copy-start | bytes 49156

commit v4 on v3

--- a/solution.py
+++ b/solution.py
@@ -33,26 +33,26 @@
 ):
     count = lax.axis_size("rows")
     rows_here = queries.shape[0]
-    cache_span = keys.shape[1]
     key_width = keys.shape[2]
     kv_count = key_width // HEAD_DIM
-    group_size = queries.shape[1] // key_width
-    query_heads = queries.reshape(rows_here, kv_count, group_size, HEAD_DIM)
-    key_heads = keys.reshape(rows_here, cache_span, kv_count, HEAD_DIM)
-    value_heads = values.reshape(rows_here, cache_span, kv_count, HEAD_DIM)
-    scores = jnp.einsum(
-        "rkgd,rskd->rkgs", query_heads, key_heads, preferred_element_type=jnp.float32
-    )
+    heads = queries.shape[1] // HEAD_DIM
+    group_size = heads // kv_count
+    head_of = lax.broadcasted_iota(jnp.int32, (heads, kv_count), 0) // group_size
+    block_of = lax.broadcasted_iota(jnp.int32, (heads, kv_count), 1)
+    onehot = (head_of == block_of).astype(jnp.bfloat16)
+    query_heads = queries.reshape(rows_here, heads, 1, HEAD_DIM)
+    spread = (query_heads * onehot[None, :, :, None]).reshape(rows_here, heads, key_width)
+    scores = jnp.einsum("rhc,rsc->rhs", spread, keys, preferred_element_type=jnp.float32)
     scores = scores / jnp.sqrt(jnp.float32(HEAD_DIM))
+    cache_span = keys.shape[1]
     visible = lax.broadcasted_iota(jnp.int32, (rows_here, cache_span), 1) < lengths[:, None]
-    scores = jnp.where(visible[:, None, None, :], scores, -jnp.inf)
+    scores = jnp.where(visible[:, None, :], scores, -jnp.inf)
     highest = jnp.max(scores, axis=-1, keepdims=True)
     expo = jnp.exp(scores - highest)
     weights = (expo / jnp.sum(expo, axis=-1, keepdims=True)).astype(jnp.bfloat16)
-    attended = jnp.einsum(
-        "rkgs,rskd->rkgd", weights, value_heads, preferred_element_type=jnp.float32
-    )
-    attended = attended.astype(jnp.bfloat16).reshape(rows_here, kv_count * group_size * HEAD_DIM)
+    mixed = jnp.einsum("rhs,rsc->rhc", weights, values, preferred_element_type=jnp.float32)
+    mixed = mixed.reshape(rows_here, heads, kv_count, HEAD_DIM) * onehot.astype(jnp.float32)[None, :, :, None]
+    attended = mixed.sum(axis=2).astype(jnp.bfloat16).reshape(rows_here, heads * HEAD_DIM)
     features = lax.all_to_all(attended, "rows", split_axis=1, concat_axis=0, tiled=True)
     partial_value = jnp.dot(features, out_weight, preferred_element_type=jnp.float32)
     hidden_here = (scatter_rows(partial_value, count) + resid.astype(jnp.float32)).astype(jnp.bfloat16)

time: 63.9 us -> 64.3 us (level)
  matrix products: 4.5 us -> 5.61 us
  local copies, waits for them, and re-layouts: 5.1 us -> 4.24 us
    another operation x2 -> x0, local copies, waits for them, and re-layouts: 2.18 us -> none
    dot_general x0 -> x1, local copies, waits for them, and re-layouts: none -> 1.21 us  [shards(): jnp.einsum('rhs,rsc->rhc', weights, values, preferred_element_type=jnp.fl...]
    dot_general x2, matrix products: 0.48 us -> 1.59 us  [the longest x1 1.36 us: shards(): jnp.einsum('rhc,rsc->rhs', spread, keys, preferred_element_type=jnp.float32)]
where the time goes in v4:
time: 64.3 us; the launch traced here: 63.9 us
  blocking collectives  38.9 us (60%)
  waiting for transfers between devices  7.69 us (12%)
  matrix products  5.61 us (9%)
  local copies, waits for them, and re-layouts  4.24 us (7%)
  starting transfers between devices  3.51 us (5%)
  other arithmetic  2.36 us (4%)
  between operations  1.6 us (2%)
    all_to_all x2, blocking collectives, scatter_rows(): got = lax.all_to_all(x, 'rows', split_axis=0, concat_axis=0, tiled=True)  25.2 us
    all_to_all x1, blocking collectives, shards(): lax.all_to_all(attended, 'rows', split_axis=1, concat_axis=0, tiled=True)  13.6 us
    all_to_all x1, waiting for transfers between devices, gather_rows(): lax.all_to_all(copies, 'rows', split_axis=0, concat_axis=0, tiled=True)  7.69 us
    all_to_all x1, starting transfers between devices, gather_rows(): lax.all_to_all(copies, 'rows', split_axis=0, concat_axis=0, tiled=True)  3.51 us
    dot_general x1, matrix products, shards(): jnp.dot(hidden, enc_weight, preferred_element_type=jnp.float32)  2.98 us
    unnamed x2, other arithmetic  1.46 us
    dot_general x1, matrix products, shards(): jnp.einsum('rhc,rsc->rhs', spread, keys, preferred_element_type=jnp.float32)  1.36 us
  transfers between devices with their start and end apart: 1, of which 1 were waited for; matrix products, arithmetic and copies ran while one was open for 0% of the time, Pallas kernels for 0%

profile of v4, /device:TPU:0, one launch (start us, length us, event | category | flops | bytes accessed | tf_op | source)
XLA Modules:
  0.0 63.9 jit_solution(3316854374985393514)
XLA Ops:
  0.6 0.0 copy-start
  0.6 0.0 copy-start.3
  0.7 0.0 copy-start.6
  1.5 0.1 copy.24
  1.6 1.2 %copy.29 = bf16[512,384]{1,0:T(8,128)(2,1)S(1)} copy(bf16[512,384]{0,1:T(8,128)(2,1)} %bitcast.41) | data formatting | bytes 786432 | tf_op jit(solution)/shard_map/rhs,rsc->rhc/dot_general | solution.py:53
  2.8 0.8 %reduce.12 = bf16[4096]{0:T(1024)(128)(2,1)S(1)} reduce(bf16[1,4096]{1,0:T(2,128)(2,1)} %param.11, bf16[]{:T(256)} %constant.42), dimensions={0}, to_apply=%param.11.reduce_sub_computation | reduce | bytes 16386 | tf_op args[0]
  3.6 0.1 broadcast_multiply_fusion
  3.7 1.4 %fusion.16 = (f32[32]{0:T(128)S(1)}, f32[32,384]{1,0:T(8,128)S(1)}) fusion(bf16[1,384,512]{2,1,0:T(8,128)(2,1)} %param.12, bf16[4,8,4,128]{3,2,1,0:T(4,128)(2,1)S(1)} %bitcast.43, pred[384]{0:T(512)(128)(4,1)S(1)} %iota_compare_fusion.1), kind=kOutput, calls=%fused_computation.34 | convolution fusion | flops 12619744 | bytes 475648 | tf_op jit(solution)/shard_map/rhc,rsc->rhs/dot_general | solution.py:45
  5.1 0.2 fusion.6
  5.3 0.2 fusion.1
  5.5 0.5 broadcast.143
  6.1 0.7 %reduce.15 = bf16[16,256]{1,0:T(8,128)(2,1)S(1)} reduce(bf16[16,1,256]{2,1,0:T(2,128)(2,1)S(1)} %bitcast.45, bf16[]{:T(256)} %broadcast.143), dimensions={1}, to_apply=%bitcast.26.reduce_sub_computation | reduce | bytes 16386
  6.8 13.6 %all_to_all.37 = bf16[16,2,128]{2,1,0:T(2,128)(2,1)S(1)} all-to-all(bf16[16,2,128]{2,1,0:T(2,128)(2,1)S(1)} %reshape.217), channel_id=1, replica_groups=mesh['groups'=2,'rows'=16] {'rows'}, dimensions={0} | all-to-all | bytes 16384 | tf_op jit(solution)/shard_map/all_to_all | solution.py:56
  20.4 0.4 convolution_bitcast_fusion.1
  20.8 0.3 copy.27
  21.1 12.6 %all_to_all.38 = f32[16,1,4096]{2,1,0:T(1,128)S(1)} all-to-all(f32[16,1,4096]{2,1,0:T(1,128)S(1)} %copy.27), channel_id=1, replica_groups=mesh['groups'=2,'rows'=16] {'rows'}, dimensions={0} | all-to-all | bytes 524288 | tf_op jit(solution)/shard_map/all_to_all | solution.py:17
  33.7 0.2 reduce_sum.40
  33.9 0.0 copy-done.3
  33.9 0.1 convert_reduce_fusion
  33.9 0.7 %broadcast_in_dim.47 = bf16[16,2,2048]{2,1,0:T(2,128)(2,1)} broadcast(bf16[2,2048]{1,0:T(2,128)(2,1)S(1)} %broadcast_in_dim.46), dimensions={1,2} | broadcast | bytes 139264 | tf_op jit(solution)/shard_map/broadcast_in_dim | solution.py:11
  34.7 3.5 %all-to-all-start.2 = ((bf16[16,2,2048]{2,1,0:T(2,128)(2,1)}), bf16[16,2,2048]{2,1,0:T(2,128)(2,1)S(1)}, u32[]{:S(2)}, u32[]{:S(2)}) async-start(bf16[16,2,2048]{2,1,0:T(2,128)(2,1)} %broadcast_in_dim.47), calls=%async_computation.2 | async-start | bytes 262144 | tf_op jit(solution)/shard_map/all_to_all | solution.py:12
  38.2 0.2 compare_reduce_fusion
  38.4 7.7 %all-to-all-done.2 = bf16[16,2,2048]{2,1,0:T(2,128)(2,1)S(1)} async-done(((bf16[16,2,2048]{2,1,0:T(2,128)(2,1)}), bf16[16,2,2048]{2,1,0:T(2,128)(2,1)S(1)}, u32[]{:S(2)}, u32[]{:S(2)}) %all-to-all-start.2) | async-done | bytes 131104 | tf_op jit(solution)/shard_map/all_to_all | solution.py:12
  46.1 0.0 copy-done.5
  46.1 0.0 copy-start.4
  46.1 3.0 %fusion.4 = bf16[16,512]{1,0:T(8,128)(2,1)S(1)} fusion(bf16[16,4096]{1,0:T(8,128)(2,1)S(1)} %bitcast.39, bf16[4096,512]{1,0:T(8,128)(2,1)} %param.18, f32[512]{0:T(512)S(1)} %copy-done.5, pred[512]{0:T(512)(128)(4,1)S(1)} %compare_reduce_fusion), kind=kOutput, calls=%fused_computation.9 | convolution fusion | flops 67141632 | bytes 4344320 | tf_op jit(solution)/shard_map/dot_general | solution.py:67
  49.1 0.4 copy-done.1
  49.5 0.7 %convolution_bitcast_fusion = f32[16,1,4096]{2,0,1:T(8,128)S(1)} fusion(bf16[16,512]{1,0:T(8,128)(2,1)S(1)} %fusion.4, bf16[512,4096]{1,0:T(8,128)(2,1)S(1)} %copy-done.1), kind=kOutput, calls=%fused_computation | convolution fusion | flops 67108864 | bytes 4472832 | tf_op jit(solution)/shard_map/dot_general | solution.py:70
  50.2 0.3 copy.28
  50.4 12.6 %all_to_all.39 = f32[16,1,4096]{2,1,0:T(1,128)S(1)} all-to-all(f32[16,1,4096]{2,1,0:T(1,128)S(1)} %copy.28), channel_id=1, replica_groups=mesh['groups'=2,'rows'=16] {'rows'}, dimensions={0} | all-to-all | bytes 524288 | tf_op jit(solution)/shard_map/all_to_all | solution.py:17
  63.1 0.2 reduce_sum.42
  63.3 0.6 convert_element_type.63
  (18 shorter events, 0.2 us)
Async XLA Ops:
  0.6 19.8 %copy-start = (bf16[256,4096]{1,0:T(8,128)(2,1)S(1)}, bf16[256,4096]{1,0:T(8,128)(2,1)}, u32[]{:S(2)}) copy-start(bf16[256,4096]{1,0:T(8,128)(2,1)} %param.16) | copy-start | bytes 6291460
  0.6 33.2 %copy-start.3 = (bf16[1,4096]{1,0:T(2,128)(2,1)S(1)}, bf16[1,4096]{1,0:T(2,128)(2,1)}, u32[]{:S(2)}) copy-start(bf16[1,4096]{1,0:T(2,128)(2,1)} %param.15) | copy-start | bytes 24580
  0.7 37.5 %copy-start.6 = (s32[256]{0:T(256)S(1)}, s32[256]{0:T(256)}, u32[]{:S(2)}) copy-start(s32[256]{0:T(256)} %param.17) | copy-start | bytes 3076
  0.7 45.4 %copy-start.5 = (f32[512]{0:T(512)S(1)}, f32[512]{0:T(512)}, u32[]{:S(2)}) copy-start(f32[512]{0:T(512)} %param.19) | copy-start | bytes 6148
  34.7 11.4 %all-to-all-start.2 = ((bf16[16,2,2048]{2,1,0:T(2,128)(2,1)}), bf16[16,2,2048]{2,1,0:T(2,128)(2,1)S(1)}, u32[]{:S(2)}, u32[]{:S(2)}) async-start(bf16[16,2,2048]{2,1,0:T(2,128)(2,1)} %broadcast_in_dim.47), calls=%async_computation.2 | async-start | bytes 262144 | tf_op jit(solution)/shard_map/all_to_all | solution.py:12
  46.0 3.4 %copy-start.1 = (bf16[512,4096]{1,0:T(8,128)(2,1)S(1)}, bf16[512,4096]{1,0:T(8,128)(2,1)}, u32[]{:S(2)}) copy-start(bf16[512,4096]{1,0:T(8,128)(2,1)} %param.20) | copy-start | bytes 12582916
  46.1 17.1 %copy-start.4 = (f32[4096]{0:T(1024)S(1)}, f32[4096]{0:T(1024)}, u32[]{:S(2)}) copy-start(f32[4096]{0:T(1024)} %param.21) | copy-start | bytes 49156
  49.5 14.4 %copy-start.2 = (bf16[16,512]{1,0:T(8,128)(2,1)}, bf16[16,512]{1,0:T(8,128)(2,1)S(1)}, u32[]{:S(2)}) copy-start(bf16[16,512]{1,0:T(8,128)(2,1)S(1)} %fusion.4) | copy-start | bytes 49156

commit v5 on v4

--- a/solution.py
+++ b/solution.py
@@ -51,7 +51,7 @@
     expo = jnp.exp(scores - highest)
     weights = (expo / jnp.sum(expo, axis=-1, keepdims=True)).astype(jnp.bfloat16)
     mixed = jnp.einsum("rhs,rsc->rhc", weights, values, preferred_element_type=jnp.float32)
-    mixed = mixed.reshape(rows_here, heads, kv_count, HEAD_DIM) * onehot.astype(jnp.float32)[None, :, :, None]
+    mixed = lax.optimization_barrier(mixed).reshape(rows_here, heads, kv_count, HEAD_DIM) * onehot.astype(jnp.float32)[None, :, :, None]
     attended = mixed.sum(axis=2).astype(jnp.bfloat16).reshape(rows_here, heads * HEAD_DIM)
     features = lax.all_to_all(attended, "rows", split_axis=1, concat_axis=0, tiled=True)
     partial_value = jnp.dot(features, out_weight, preferred_element_type=jnp.float32)

time: 64.3 us -> 64.2 us (level)
  local copies, waits for them, and re-layouts: 4.24 us -> 2.95 us
  matrix products: 5.61 us -> 6.59 us
    dot_general x1 -> x0, local copies, waits for them, and re-layouts: 1.21 us -> none  [shards(): jnp.einsum('rhs,rsc->rhc', weights, values, preferred_element_type=jnp.fl...]
    dot_general x1, matrix products: 0.23 us -> 1.21 us  [shards(): jnp.einsum('rhs,rsc->rhc', weights, values, preferred_element_type=jnp.fl...]
where the time goes in v5:
time: 64.2 us; the launch traced here: 63.7 us
  blocking collectives  38.9 us (61%)
  waiting for transfers between devices  7.69 us (12%)
  matrix products  6.59 us (10%)
  starting transfers between devices  3.51 us (5%)
  local copies, waits for them, and re-layouts  2.95 us (5%)
  other arithmetic  2.55 us (4%)
  between operations  1.6 us (2%)
    all_to_all x2, blocking collectives, scatter_rows(): got = lax.all_to_all(x, 'rows', split_axis=0, concat_axis=0, tiled=True)  25.2 us
    all_to_all x1, blocking collectives, shards(): lax.all_to_all(attended, 'rows', split_axis=1, concat_axis=0, tiled=True)  13.6 us
    all_to_all x1, waiting for transfers between devices, gather_rows(): lax.all_to_all(copies, 'rows', split_axis=0, concat_axis=0, tiled=True)  7.69 us
    all_to_all x1, starting transfers between devices, gather_rows(): lax.all_to_all(copies, 'rows', split_axis=0, concat_axis=0, tiled=True)  3.51 us
    dot_general x1, matrix products, shards(): jnp.dot(hidden, enc_weight, preferred_element_type=jnp.float32)  2.98 us
    unnamed x2, other arithmetic  1.46 us
    dot_general x1, matrix products, shards(): jnp.einsum('rhc,rsc->rhs', spread, keys, preferred_element_type=jnp.float32)  1.36 us
  transfers between devices with their start and end apart: 1, of which 1 were waited for; matrix products, arithmetic and copies ran while one was open for 0% of the time, Pallas kernels for 0%

profile of v5, /device:TPU:0, one launch (start us, length us, event | category | flops | bytes accessed | tf_op | source)
XLA Modules:
  0.0 63.7 jit_solution(14130270072609564917)
XLA Ops:
  0.6 0.0 copy-start
  0.6 0.0 copy-start.3
  0.7 0.0 copy-start.6
  0.7 0.0 copy-start.5
  1.5 0.8 %reduce.11 = bf16[4096]{0:T(1024)(128)(2,1)S(1)} reduce(bf16[1,4096]{1,0:T(2,128)(2,1)} %param.11, bf16[]{:T(256)} %constant.42), dimensions={0}, to_apply=%param.11.reduce_sub_computation | reduce | bytes 16386 | tf_op args[0]
  2.3 0.1 fusion.14
  2.4 0.1 broadcast_multiply_fusion
  2.5 1.4 %fusion.15 = (f32[32]{0:T(128)S(1)}, f32[32,384]{1,0:T(8,128)S(1)}) fusion(bf16[1,384,512]{2,1,0:T(8,128)(2,1)} %param.12, bf16[4,8,4,128]{3,2,1,0:T(4,128)(2,1)S(1)} %bitcast.38, pred[384]{0:T(512)(128)(4,1)S(1)} %iota_compare_fusion.1), kind=kOutput, calls=%fused_computation.35 | convolution fusion | flops 12619744 | bytes 475648 | tf_op jit(solution)/shard_map/rhc,rsc->rhs/dot_general | solution.py:45
  3.8 0.2 fusion.6
  4.0 1.2 %convolution_bitcast_fusion.2 = f32[1,32,512]{2,1,0:T(8,128)S(1)} fusion(bf16[1,384,512]{2,1,0:T(8,128)(2,1)} %param.13, f32[32,384]{1,0:T(8,128)S(1)} %get-tuple-element.5, f32[32]{0:T(128)S(1)} %fusion.6, f32[32]{0:T(128)S(1)} %get-tuple-element.4), kind=kOutput, calls=%fused_computation.2 | convolution fusion | flops 12619776 | bytes 508160 | tf_op jit(solution)/shard_map/rhs,rsc->rhc/dot_general | solution.py:53
  5.3 0.1 multiply_reduce_fusion
  5.4 0.5 broadcast.156
  5.9 0.7 %reduce.14 = bf16[16,256]{1,0:T(8,128)(2,1)S(1)} reduce(bf16[16,1,256]{2,1,0:T(2,128)(2,1)S(1)} %bitcast.40, bf16[]{:T(256)} %broadcast.156), dimensions={1}, to_apply=%bitcast.24.reduce_sub_computation | reduce | bytes 16386
  6.6 13.6 %all_to_all.37 = bf16[16,2,128]{2,1,0:T(2,128)(2,1)S(1)} all-to-all(bf16[16,2,128]{2,1,0:T(2,128)(2,1)S(1)} %reshape.230), channel_id=1, replica_groups=mesh['groups'=2,'rows'=16] {'rows'}, dimensions={0} | all-to-all | bytes 16384 | tf_op jit(solution)/shard_map/all_to_all | solution.py:56
  20.3 0.4 convolution_bitcast_fusion.1
  20.7 0.3 copy.19
  20.9 12.6 %all_to_all.38 = f32[16,1,4096]{2,1,0:T(1,128)S(1)} all-to-all(f32[16,1,4096]{2,1,0:T(1,128)S(1)} %copy.19), channel_id=1, replica_groups=mesh['groups'=2,'rows'=16] {'rows'}, dimensions={0} | all-to-all | bytes 524288 | tf_op jit(solution)/shard_map/all_to_all | solution.py:17
  33.6 0.2 reduce_sum.40
  33.7 0.1 convert_reduce_fusion
  33.8 0.7 %broadcast_in_dim.47 = bf16[16,2,2048]{2,1,0:T(2,128)(2,1)} broadcast(bf16[2,2048]{1,0:T(2,128)(2,1)S(1)} %broadcast_in_dim.46), dimensions={1,2} | broadcast | bytes 139264 | tf_op jit(solution)/shard_map/broadcast_in_dim | solution.py:11
  34.5 3.5 %all-to-all-start.2 = ((bf16[16,2,2048]{2,1,0:T(2,128)(2,1)}), bf16[16,2,2048]{2,1,0:T(2,128)(2,1)S(1)}, u32[]{:S(2)}, u32[]{:S(2)}) async-start(bf16[16,2,2048]{2,1,0:T(2,128)(2,1)} %broadcast_in_dim.47), calls=%async_computation.2 | async-start | bytes 262144 | tf_op jit(solution)/shard_map/all_to_all | solution.py:12
  38.1 0.0 copy-done.6
  38.1 0.2 compare_reduce_fusion
  38.2 7.7 %all-to-all-done.2 = bf16[16,2,2048]{2,1,0:T(2,128)(2,1)S(1)} async-done(((bf16[16,2,2048]{2,1,0:T(2,128)(2,1)}), bf16[16,2,2048]{2,1,0:T(2,128)(2,1)S(1)}, u32[]{:S(2)}, u32[]{:S(2)}) %all-to-all-start.2) | async-done | bytes 131104 | tf_op jit(solution)/shard_map/all_to_all | solution.py:12
  46.0 0.0 copy-start.4
  46.0 3.0 %fusion.3 = bf16[16,512]{1,0:T(8,128)(2,1)S(1)} fusion(bf16[16,4096]{1,0:T(8,128)(2,1)S(1)} %bitcast.36, bf16[4096,512]{1,0:T(8,128)(2,1)} %param.18, f32[512]{0:T(512)S(1)} %copy-done.5, pred[512]{0:T(512)(128)(4,1)S(1)} %compare_reduce_fusion), kind=kOutput, calls=%fused_computation.8 | convolution fusion | flops 67141632 | bytes 4344320 | tf_op jit(solution)/shard_map/dot_general | solution.py:67
  49.0 0.4 copy-done.1
  49.4 0.7 %convolution_bitcast_fusion = f32[16,1,4096]{2,0,1:T(8,128)S(1)} fusion(bf16[16,512]{1,0:T(8,128)(2,1)S(1)} %fusion.3, bf16[512,4096]{1,0:T(8,128)(2,1)S(1)} %copy-done.1), kind=kOutput, calls=%fused_computation | convolution fusion | flops 67108864 | bytes 4472832 | tf_op jit(solution)/shard_map/dot_general | solution.py:70
  50.0 0.3 copy.20
  50.3 12.6 %all_to_all.39 = f32[16,1,4096]{2,1,0:T(1,128)S(1)} all-to-all(f32[16,1,4096]{2,1,0:T(1,128)S(1)} %copy.20), channel_id=1, replica_groups=mesh['groups'=2,'rows'=16] {'rows'}, dimensions={0} | all-to-all | bytes 524288 | tf_op jit(solution)/shard_map/all_to_all | solution.py:17
  62.9 0.2 reduce_sum.42
  63.1 0.6 convert_element_type.63
  (18 shorter events, 0.2 us)
Async XLA Ops:
  0.6 19.7 %copy-start = (bf16[256,4096]{1,0:T(8,128)(2,1)S(1)}, bf16[256,4096]{1,0:T(8,128)(2,1)}, u32[]{:S(2)}) copy-start(bf16[256,4096]{1,0:T(8,128)(2,1)} %param.16) | copy-start | bytes 6291460
  0.6 33.1 %copy-start.3 = (bf16[1,4096]{1,0:T(2,128)(2,1)S(1)}, bf16[1,4096]{1,0:T(2,128)(2,1)}, u32[]{:S(2)}) copy-start(bf16[1,4096]{1,0:T(2,128)(2,1)} %param.15) | copy-start | bytes 24580
  0.7 37.4 %copy-start.6 = (s32[256]{0:T(256)S(1)}, s32[256]{0:T(256)}, u32[]{:S(2)}) copy-start(s32[256]{0:T(256)} %param.17) | copy-start | bytes 3076
  0.7 45.3 %copy-start.5 = (f32[512]{0:T(512)S(1)}, f32[512]{0:T(512)}, u32[]{:S(2)}) copy-start(f32[512]{0:T(512)} %param.19) | copy-start | bytes 6148
  34.5 11.4 %all-to-all-start.2 = ((bf16[16,2,2048]{2,1,0:T(2,128)(2,1)}), bf16[16,2,2048]{2,1,0:T(2,128)(2,1)S(1)}, u32[]{:S(2)}, u32[]{:S(2)}) async-start(bf16[16,2,2048]{2,1,0:T(2,128)(2,1)} %broadcast_in_dim.47), calls=%async_computation.2 | async-start | bytes 262144 | tf_op jit(solution)/shard_map/all_to_all | solution.py:12
  45.9 3.4 %copy-start.1 = (bf16[512,4096]{1,0:T(8,128)(2,1)S(1)}, bf16[512,4096]{1,0:T(8,128)(2,1)}, u32[]{:S(2)}) copy-start(bf16[512,4096]{1,0:T(8,128)(2,1)} %param.20) | copy-start | bytes 12582916
  46.0 17.1 %copy-start.4 = (f32[4096]{0:T(1024)S(1)}, f32[4096]{0:T(1024)}, u32[]{:S(2)}) copy-start(f32[4096]{0:T(1024)} %param.21) | copy-start | bytes 49156
  49.4 14.4 %copy-start.2 = (bf16[16,512]{1,0:T(8,128)(2,1)}, bf16[16,512]{1,0:T(8,128)(2,1)S(1)}, u32[]{:S(2)}) copy-start(bf16[16,512]{1,0:T(8,128)(2,1)S(1)} %fusion.3) | copy-start | bytes 49156

commit v6 on v5

v6 whole, which is shorter than its diff:
```python
import jax
import jax.numpy as jnp
from jax import lax
from jax.sharding import Mesh, PartitionSpec as P

HEAD_DIM = 128


ROWS = ("chip", "core")


def pick(pair, first):
    return jnp.where(lax.axis_index("core") == first, pair[0], pair[1])


def gather_rows(x, chips):
    halves = x.reshape(2 * x.shape[0], x.shape[1] // 2)
    copies = jnp.broadcast_to(halves[None], (chips,) + halves.shape).reshape((chips * halves.shape[0], halves.shape[1]))
    mine = lax.all_to_all(copies, "chip", split_axis=0, concat_axis=0, tiled=True)
    mine = mine.reshape(chips, x.shape[0], x.shape[1])
    mate = lax.ppermute(mine, "core", [(0, 1), (1, 0)])
    first = pick((mine, mate), 0)
    second = pick((mate, mine), 0)
    return jnp.stack([first, second], axis=1).reshape(chips * 2 * x.shape[0], x.shape[1])


def scatter_rows(x, chips):
    per = x.shape[0] // (2 * chips)
    split = x.reshape(chips, 2, per, x.shape[1])
    keep = pick((split[:, 0], split[:, 1]), 0)
    give = pick((split[:, 1], split[:, 0]), 0)
    summed = keep + lax.ppermute(give, "core", [(0, 1), (1, 0)])
    got = lax.all_to_all(summed.reshape(chips * per, x.shape[1]), "chip", split_axis=0, concat_axis=0, tiled=True)
    return got.reshape(chips, per, x.shape[1]).sum(axis=0)


def shards(
    queries,
    keys,
    values,
    lengths,
    resid,
    out_weight,
    chat_ids,
    enc_weight,
    enc_bias,
    dec_weight,
    dec_bias,
):
    chips = lax.axis_size("chip")
    rows_here = queries.shape[0]
    key_width = keys.shape[2]
    kv_count = key_width // HEAD_DIM
    heads = queries.shape[1] // HEAD_DIM
    group_size = heads // kv_count
    head_of = lax.broadcasted_iota(jnp.int32, (heads, kv_count), 0) // group_size
    block_of = lax.broadcasted_iota(jnp.int32, (heads, kv_count), 1)
    onehot = (head_of == block_of).astype(jnp.bfloat16)
    query_heads = queries.reshape(rows_here, heads, 1, HEAD_DIM)
    spread = (query_heads * onehot[None, :, :, None]).reshape(rows_here, heads, key_width)
    scores = jnp.einsum("rhc,rsc->rhs", spread, keys, preferred_element_type=jnp.float32)
    scores = scores / jnp.sqrt(jnp.float32(HEAD_DIM))
    cache_span = keys.shape[1]
    visible = lax.broadcasted_iota(jnp.int32, (rows_here, cache_span), 1) < lengths[:, None]
    scores = jnp.where(visible[:, None, :], scores, -jnp.inf)
    highest = jnp.max(scores, axis=-1, keepdims=True)
    expo = jnp.exp(scores - highest)
    weights = (expo / jnp.sum(expo, axis=-1, keepdims=True)).astype(jnp.bfloat16)
    mixed = jnp.einsum("rhs,rsc->rhc", weights, values, preferred_element_type=jnp.float32)
    mixed = lax.optimization_barrier(mixed).reshape(rows_here, heads, kv_count, HEAD_DIM) * onehot.astype(jnp.float32)[None, :, :, None]
    attended = mixed.sum(axis=2).astype(jnp.bfloat16).reshape(rows_here, heads * HEAD_DIM)
    features = lax.all_to_all(attended, ROWS, split_axis=1, concat_axis=0, tiled=True)
    partial_value = jnp.dot(features, out_weight, preferred_element_type=jnp.float32)
    hidden_here = (scatter_rows(partial_value, chips) + resid.astype(jnp.float32)).astype(jnp.bfloat16)
    hidden = gather_rows(hidden_here, chips)
    lat_here = enc_weight.shape[1]
    latent_ids = lax.axis_index(ROWS) * lat_here + lax.broadcasted_iota(jnp.int32, (lat_here,), 0)
    listed = jnp.any(chat_ids[:, None] == latent_ids[None, :], axis=0)
    activity = jnp.where(
        listed[None, :],
        0.0,
        jax.nn.relu(
            jnp.dot(hidden, enc_weight, preferred_element_type=jnp.float32) + enc_bias[None, :]
        ),
    ).astype(jnp.bfloat16)
    rebuilt = scatter_rows(jnp.dot(activity, dec_weight, preferred_element_type=jnp.float32), chips)
    spliced = (rebuilt + dec_bias[None, :]).astype(jnp.bfloat16)
    return (spliced, activity)


def solution(mesh):
    groups, count = mesh.devices.shape
    paired = Mesh(mesh.devices.reshape(groups, count // 2, 2), ("groups",) + ROWS)
    lead = ("groups",) + ROWS
    placed = (
        P(lead, None),
        P(lead, None, None),
        P(lead, None, None),
        P(lead),
        P(lead, None),
        P(ROWS, None),
        P(),
        P(None, ROWS),
        P(ROWS),
        P(ROWS, None),
        P(),
    )
    return jax.shard_map(
        shards,
        mesh=paired,
        in_specs=placed,
        out_specs=(P(lead, None), P("groups", ROWS)),
        check_vma=False,
    )
```

time: 64.2 us -> 63.3 us (0.986)
  blocking collectives: 38.9 us -> 19.9 us
  waiting for transfers between devices: 7.69 us -> 16.8 us
  starting transfers between devices: 3.51 us -> 11.1 us
  local copies, waits for them, and re-layouts: 2.95 us -> 3.93 us
    all_to_all x3 -> x2, blocking collectives: 38.9 us -> 19.9 us  [scatter_rows(): lax.all_to_all(summed.reshape(chips * per, x.shape[1]), 'chip', split_axi...]
    all_to_all x1 -> x2, starting transfers between devices: 3.51 us -> 10.7 us  [the longest x1 7.39 us: shards(): lax.all_to_all(attended, ROWS, split_axis=1, concat_axis=0, tiled=True)]
    all_to_all x1 -> x2, waiting for transfers between devices: 7.69 us -> 13.2 us  [the longest x1 6.82 us: gather_rows(): lax.all_to_all(copies, 'chip', split_axis=0, concat_axis=0, tiled=True)]
    ppermute x0 -> x3, waiting for transfers between devices: none -> 3.6 us  [the longest x2 2.53 us: scatter_rows(): summed = keep + lax.ppermute(give, 'core', [(0, 1), (1, 0)])]
    unnamed x18 -> x17, local copies, waits for them, and re-layouts: 1.01 us -> 1.62 us
  transfers between devices with their start and end apart: 1 -> 5, of which waited for: 1 -> 5; matrix products, arithmetic and copies ran while one was open for 0% -> 0% of each run, Pallas kernels for 0% -> 0%
where the time goes in v6:
time: 63.3 us; the launch traced here: 62.8 us
  blocking collectives  19.9 us (31%)
  waiting for transfers between devices  16.8 us (27%)
  starting transfers between devices  11.1 us (18%)
  matrix products  6.59 us (10%)
  local copies, waits for them, and re-layouts  3.93 us (6%)
  other arithmetic  2.78 us (4%)
  between operations  1.7 us (3%)
    all_to_all x2, blocking collectives, scatter_rows(): lax.all_to_all(summed.reshape(chips * per, x.shape[1]), 'chip', split_axi...  19.9 us
    all_to_all x1, starting transfers between devices, shards(): lax.all_to_all(attended, ROWS, split_axis=1, concat_axis=0, tiled=True)  7.39 us
    all_to_all x1, waiting for transfers between devices, gather_rows(): lax.all_to_all(copies, 'chip', split_axis=0, concat_axis=0, tiled=True)  6.82 us
    all_to_all x1, waiting for transfers between devices, shards(): lax.all_to_all(attended, ROWS, split_axis=1, concat_axis=0, tiled=True)  6.35 us
    all_to_all x1, starting transfers between devices, gather_rows(): lax.all_to_all(copies, 'chip', split_axis=0, concat_axis=0, tiled=True)  3.35 us
    dot_general x1, matrix products, shards(): jnp.dot(hidden, enc_weight, preferred_element_type=jnp.float32)  2.98 us
    ppermute x2, waiting for transfers between devices, scatter_rows(): summed = keep + lax.ppermute(give, 'core', [(0, 1), (1, 0)])  2.53 us
    unnamed x17, local copies, waits for them, and re-layouts  1.62 us
  transfers between devices with their start and end apart: 5, of which 5 were waited for; matrix products, arithmetic and copies ran while one was open for 0% of the time, Pallas kernels for 0%

profile of v6, /device:TPU:0, one launch (start us, length us, event | category | flops | bytes accessed | tf_op | source)
XLA Modules:
  0.0 62.8 jit_solution(3191771778950367434)
XLA Ops:
  1.5 0.8 %reduce.11 = bf16[4096]{0:T(1024)(128)(2,1)S(1)} reduce(bf16[1,4096]{1,0:T(2,128)(2,1)} %param.11, bf16[]{:T(256)} %constant.49), dimensions={0}, to_apply=%param.11.reduce_sub_computation | reduce | bytes 16386 | tf_op args[0]
  2.5 1.4 %fusion.18 = (f32[32]{0:T(128)S(1)}, f32[32,384]{1,0:T(8,128)S(1)}) fusion(bf16[1,384,512]{2,1,0:T(8,128)(2,1)} %param.12, bf16[4,8,4,128]{3,2,1,0:T(4,128)(2,1)S(1)} %bitcast.60, pred[384]{0:T(512)(128)(4,1)S(1)} %iota_compare_fusion.1), kind=kOutput, calls=%fused_computation.44 | convolution fusion | flops 12619744 | bytes 475648 | tf_op jit(solution)/shard_map/rhc,rsc->rhs/dot_general | solution.py:61
  3.8 0.2 fusion.9
  4.0 1.2 %convolution_bitcast_fusion = f32[1,32,512]{2,1,0:T(8,128)S(1)} fusion(bf16[1,384,512]{2,1,0:T(8,128)(2,1)} %param.13, f32[32,384]{1,0:T(8,128)S(1)} %get-tuple-element.9, f32[32]{0:T(128)S(1)} %fusion.9, f32[32]{0:T(128)S(1)} %get-tuple-element.8), kind=kOutput, calls=%fused_computation.2 | convolution fusion | flops 12619776 | bytes 508160 | tf_op jit(solution)/shard_map/rhs,rsc->rhc/dot_general | solution.py:69
  5.3 0.1 multiply_reduce_fusion
  5.4 0.5 broadcast.196
  5.9 0.7 %reduce.16 = bf16[16,256]{1,0:T(8,128)(2,1)S(1)} reduce(bf16[16,1,256]{2,1,0:T(2,128)(2,1)S(1)} %bitcast.62, bf16[]{:T(256)} %broadcast.196), dimensions={1}, to_apply=%bitcast.44.reduce_sub_computation | reduce | bytes 16386
  6.6 0.6 reshape.339
  7.2 7.4 %all-to-all-start = ((bf16[16,2,128]{2,1,0:T(2,128)(2,1)}), bf16[16,2,128]{2,1,0:T(2,128)(2,1)S(1)}, u32[]{:S(2)}, u32[]{:S(2)}) async-start(bf16[16,2,128]{2,1,0:T(2,128)(2,1)} %reshape.339), calls=%async_computation | async-start | bytes 16384 | tf_op jit(solution)/shard_map/all_to_all | solution.py:72
  14.6 6.4 %all-to-all-done = bf16[16,2,128]{2,1,0:T(2,128)(2,1)S(1)} async-done(((bf16[16,2,128]{2,1,0:T(2,128)(2,1)}), bf16[16,2,128]{2,1,0:T(2,128)(2,1)S(1)}, u32[]{:S(2)}, u32[]{:S(2)}) %all-to-all-start) | async-done | bytes 8224 | tf_op jit(solution)/shard_map/all_to_all | solution.py:72
  21.1 0.4 fusion
  21.6 1.3 %collective-permute-done = f32[8,1,4096]{2,0,1:T(8,128)S(1)} collective-permute-done((f32[8,1,4096]{2,0,1:T(8,128)S(1)}, f32[8,1,4096]{2,0,1:T(8,128)S(1)}, u32[]{:S(2)}, u32[]{:S(2)}) %collective-permute-start) | collective-permute-done | bytes 131104 | tf_op jit(solution)/shard_map/ppermute | solution.py:32
  22.9 0.1 copy.55
  23.1 10.0 %all_to_all.28 = f32[8,1,4096]{2,1,0:T(1,128)S(1)} all-to-all(f32[8,1,4096]{2,1,0:T(1,128)S(1)} %copy.55), channel_id=1, replica_groups=mesh['groups'=2,'chip'=8,'core'=2] {'chip'}, dimensions={0} | all-to-all | bytes 262144 | tf_op jit(solution)/shard_map/all_to_all | solution.py:33
  33.2 0.7 %broadcast_in_dim.47 = bf16[8,2,2048]{2,1,0:T(2,128)(2,1)} broadcast(bf16[2,2048]{1,0:T(2,128)(2,1)S(1)} %broadcast_in_dim.46), dimensions={1,2} | broadcast | bytes 73728 | tf_op jit(solution)/shard_map/broadcast_in_dim | solution.py:18
  33.9 3.3 %all-to-all-start.2 = ((bf16[8,2,2048]{2,1,0:T(2,128)(2,1)}), bf16[8,2,2048]{2,1,0:T(2,128)(2,1)S(1)}, u32[]{:S(2)}, u32[]{:S(2)}) async-start(bf16[8,2,2048]{2,1,0:T(2,128)(2,1)} %broadcast_in_dim.47), calls=%async_computation.2 | async-start | bytes 131072 | tf_op jit(solution)/shard_map/all_to_all | solution.py:19
  37.3 6.8 %all-to-all-done.2 = bf16[8,2,2048]{2,1,0:T(2,128)(2,1)S(1)} async-done(((bf16[8,2,2048]{2,1,0:T(2,128)(2,1)}), bf16[8,2,2048]{2,1,0:T(2,128)(2,1)S(1)}, u32[]{:S(2)}, u32[]{:S(2)}) %all-to-all-start.2) | async-done | bytes 65568 | tf_op jit(solution)/shard_map/all_to_all | solution.py:19
  44.2 0.2 compare_reduce_fusion
  44.4 1.1 %collective-permute-done.1 = bf16[8,1,4096]{2,0,1:T(8,128)(2,1)S(1)} collective-permute-done((bf16[8,1,4096]{2,0,1:T(8,128)(2,1)S(1)}, bf16[8,1,4096]{2,0,1:T(8,128)(2,1)S(1)}, u32[]{:S(2)}, u32[]{:S(2)}) %collective-permute-start.1) | collective-permute-done | bytes 65568 | tf_op jit(solution)/shard_map/ppermute | solution.py:21
  45.5 0.1 copy.56
  45.7 3.0 %fusion.5 = bf16[16,512]{1,0:T(8,128)(2,1)S(1)} fusion(bf16[16,4096]{1,0:T(8,128)(2,1)S(1)} %reshape.333, bf16[4096,512]{1,0:T(8,128)(2,1)} %param.18, f32[512]{0:T(512)S(1)} %copy-done.5, pred[512]{0:T(512)(128)(4,1)S(1)} %compare_reduce_fusion), kind=kOutput, calls=%fused_computation.8 | convolution fusion | flops 67141632 | bytes 4344320 | tf_op jit(solution)/shard_map/dot_general | solution.py:83
  48.7 0.5 copy-done.1
  49.2 0.7 %fusion.19 = f32[16,4096]{1,0:T(8,128)S(1)} fusion(bf16[16,512]{1,0:T(8,128)(2,1)S(1)} %fusion.5, bf16[512,4096]{1,0:T(8,128)(2,1)S(1)} %copy-done.1), kind=kOutput, calls=%fused_computation.46 | convolution fusion | flops 67108864 | bytes 4472832 | tf_op jit(solution)/shard_map/dot_general | solution.py:86
  49.8 0.2 reshape.334
  50.0 0.2 fusion.17
  50.2 0.2 select_bitcast_fusion
  50.4 0.2 collective-permute-start.2
  50.6 1.2 %collective-permute-done.2 = f32[8,1,4096]{2,0,1:T(8,128)S(1)} collective-permute-done((f32[8,1,4096]{2,0,1:T(8,128)S(1)}, f32[8,1,4096]{2,0,1:T(8,128)S(1)}, u32[]{:S(2)}, u32[]{:S(2)}) %collective-permute-start.2) | collective-permute-done | bytes 131104 | tf_op jit(solution)/shard_map/ppermute | solution.py:32
  51.8 0.2 bitcast_add_fusion
  52.0 0.1 copy.59
  52.1 10.0 %all_to_all.29 = f32[8,1,4096]{2,1,0:T(1,128)S(1)} all-to-all(f32[8,1,4096]{2,1,0:T(1,128)S(1)} %copy.59), channel_id=1, replica_groups=mesh['groups'=2,'chip'=8,'core'=2] {'chip'}, dimensions={0} | all-to-all | bytes 262144 | tf_op jit(solution)/shard_map/all_to_all | solution.py:33
  62.2 0.6 convert_element_type.63
  (37 shorter events, 1.0 us)
Async XLA Ops:
  0.6 20.4 %copy-start = (bf16[256,4096]{1,0:T(8,128)(2,1)S(1)}, bf16[256,4096]{1,0:T(8,128)(2,1)}, u32[]{:S(2)}) copy-start(bf16[256,4096]{1,0:T(8,128)(2,1)} %param.16) | copy-start | bytes 6291460
  0.6 32.5 %copy-start.3 = (bf16[1,4096]{1,0:T(2,128)(2,1)S(1)}, bf16[1,4096]{1,0:T(2,128)(2,1)}, u32[]{:S(2)}) copy-start(bf16[1,4096]{1,0:T(2,128)(2,1)} %param.15) | copy-start | bytes 24580
  0.7 43.6 %copy-start.6 = (s32[256]{0:T(256)S(1)}, s32[256]{0:T(256)}, u32[]{:S(2)}) copy-start(s32[256]{0:T(256)} %param.17) | copy-start | bytes 3076
  0.7 45.0 %copy-start.5 = (f32[512]{0:T(512)S(1)}, f32[512]{0:T(512)}, u32[]{:S(2)}) copy-start(f32[512]{0:T(512)} %param.19) | copy-start | bytes 6148
  7.2 13.8 %all-to-all-start = ((bf16[16,2,128]{2,1,0:T(2,128)(2,1)}), bf16[16,2,128]{2,1,0:T(2,128)(2,1)S(1)}, u32[]{:S(2)}, u32[]{:S(2)}) async-start(bf16[16,2,128]{2,1,0:T(2,128)(2,1)} %reshape.339), calls=%async_computation | async-start | bytes 16384 | tf_op jit(solution)/shard_map/all_to_all | solution.py:72
  21.5 1.4 %collective-permute-start = (f32[8,1,4096]{2,0,1:T(8,128)S(1)}, f32[8,1,4096]{2,0,1:T(8,128)S(1)}, u32[]{:S(2)}, u32[]{:S(2)}) collective-permute-start(f32[8,1,4096]{2,0,1:T(8,128)S(1)} %fusion.8), channel_id=1, source_target_pairs={{0,1},{1,0},{2,3},{3,2},{4,5},{5,4},{6,7},{7,6},{8,9},{9,8},{10,11... | collective-permute-start | bytes 393224 | tf_op jit(solution)/shard_map/ppermute | solution.py:32
  33.9 10.2 %all-to-all-start.2 = ((bf16[8,2,2048]{2,1,0:T(2,128)(2,1)}), bf16[8,2,2048]{2,1,0:T(2,128)(2,1)S(1)}, u32[]{:S(2)}, u32[]{:S(2)}) async-start(bf16[8,2,2048]{2,1,0:T(2,128)(2,1)} %broadcast_in_dim.47), calls=%async_computation.2 | async-start | bytes 131072 | tf_op jit(solution)/shard_map/all_to_all | solution.py:19
  44.1 1.3 %collective-permute-start.1 = (bf16[8,1,4096]{2,0,1:T(8,128)(2,1)S(1)}, bf16[8,1,4096]{2,0,1:T(8,128)(2,1)S(1)}, u32[]{:S(2)}, u32[]{:S(2)}) collective-permute-start(bf16[8,1,4096]{2,0,1:T(8,128)(2,1)S(1)} %reshape.332), channel_id=1, source_target_pairs={{0,1},{1,0},{2,3},{3,2},{4,5},{5,4},{6,7},{7,6},{8,9},{9,8},{10,11... | collective-permute-start | bytes 196616 | tf_op jit(solution)/shard_map/ppermute | solution.py:21
  45.7 3.5 %copy-start.1 = (bf16[512,4096]{1,0:T(8,128)(2,1)S(1)}, bf16[512,4096]{1,0:T(8,128)(2,1)}, u32[]{:S(2)}) copy-start(bf16[512,4096]{1,0:T(8,128)(2,1)} %param.20) | copy-start | bytes 12582916
  49.2 13.7 %copy-start.2 = (bf16[16,512]{1,0:T(8,128)(2,1)}, bf16[16,512]{1,0:T(8,128)(2,1)S(1)}, u32[]{:S(2)}) copy-start(bf16[16,512]{1,0:T(8,128)(2,1)S(1)} %fusion.5) | copy-start | bytes 49156
  49.2 13.0 %copy-start.4 = (f32[4096]{0:T(1024)S(1)}, f32[4096]{0:T(1024)}, u32[]{:S(2)}) copy-start(f32[4096]{0:T(1024)} %param.21) | copy-start | bytes 49156
  50.4 1.4 %collective-permute-start.2 = (f32[8,1,4096]{2,0,1:T(8,128)S(1)}, f32[8,1,4096]{2,0,1:T(8,128)S(1)}, u32[]{:S(2)}, u32[]{:S(2)}) collective-permute-start(f32[8,1,4096]{2,0,1:T(8,128)S(1)} %select_bitcast_fusion), channel_id=1, source_target_pairs={{0,1},{1,0},{2,3},{3,2},{4,5},{5,4},{6,7},{7,6},{8,9},{9,8},{10,11... | collective-permute-start | bytes 393224 | tf_op jit(solution)/shard_map/ppermute | solution.py:32

commit v7 on v6

--- a/solution.py
+++ b/solution.py
@@ -68,8 +68,15 @@
     weights = (expo / jnp.sum(expo, axis=-1, keepdims=True)).astype(jnp.bfloat16)
     mixed = jnp.einsum("rhs,rsc->rhc", weights, values, preferred_element_type=jnp.float32)
     mixed = lax.optimization_barrier(mixed).reshape(rows_here, heads, kv_count, HEAD_DIM) * onehot.astype(jnp.float32)[None, :, :, None]
-    attended = mixed.sum(axis=2).astype(jnp.bfloat16).reshape(rows_here, heads * HEAD_DIM)
-    features = lax.all_to_all(attended, ROWS, split_axis=1, concat_axis=0, tiled=True)
+    attended = mixed.sum(axis=2).astype(jnp.bfloat16)
+    count = 2 * chips
+    if heads % count == 0:
+        blocks = attended.reshape(rows_here * count, heads // count, HEAD_DIM)
+        got = lax.all_to_all(blocks, ROWS, split_axis=0, concat_axis=0, tiled=True)
+        features = got.reshape(count * rows_here, (heads // count) * HEAD_DIM)
+    else:
+        attended = attended.reshape(rows_here, heads * HEAD_DIM)
+        features = lax.all_to_all(attended, ROWS, split_axis=1, concat_axis=0, tiled=True)
     partial_value = jnp.dot(features, out_weight, preferred_element_type=jnp.float32)
     hidden_here = (scatter_rows(partial_value, chips) + resid.astype(jnp.float32)).astype(jnp.bfloat16)
     hidden = gather_rows(hidden_here, chips)

time: 63.3 us -> 62 us (0.979)
  local copies, waits for them, and re-layouts: 3.93 us -> 2.73 us
    unnamed x17 -> x14, local copies, waits for them, and re-layouts: 1.62 us -> 0.49 us
    unnamed x2 -> x1, other arithmetic: 1.46 us -> 0.77 us
where the time goes in v7:
time: 62 us; the launch traced here: 61.5 us
  blocking collectives  19.9 us (32%)
  waiting for transfers between devices  16.8 us (27%)
  starting transfers between devices  11.1 us (18%)
  matrix products  6.59 us (11%)
  local copies, waits for them, and re-layouts  2.73 us (4%)
  other arithmetic  2.69 us (4%)
  between operations  1.69 us (3%)
    all_to_all x2, blocking collectives, scatter_rows(): lax.all_to_all(summed.reshape(chips * per, x.shape[1]), 'chip', split_axi...  19.9 us
    all_to_all x1, starting transfers between devices, shards(): got = lax.all_to_all(blocks, ROWS, split_axis=0, concat_axis=0, tiled=True)  7.39 us
    all_to_all x1, waiting for transfers between devices, gather_rows(): lax.all_to_all(copies, 'chip', split_axis=0, concat_axis=0, tiled=True)  6.82 us
    all_to_all x1, waiting for transfers between devices, shards(): got = lax.all_to_all(blocks, ROWS, split_axis=0, concat_axis=0, tiled=True)  6.35 us
    all_to_all x1, starting transfers between devices, gather_rows(): lax.all_to_all(copies, 'chip', split_axis=0, concat_axis=0, tiled=True)  3.35 us
    dot_general x1, matrix products, shards(): jnp.dot(hidden, enc_weight, preferred_element_type=jnp.float32)  2.98 us
    ppermute x2, waiting for transfers between devices, scatter_rows(): summed = keep + lax.ppermute(give, 'core', [(0, 1), (1, 0)])  2.53 us
    dot_general x1, matrix products, shards(): jnp.einsum('rhc,rsc->rhs', spread, keys, preferred_element_type=jnp.float32)  1.36 us
  transfers between devices with their start and end apart: 5, of which 5 were waited for; matrix products, arithmetic and copies ran while one was open for 0% of the time, Pallas kernels for 0%

profile of v7, /device:TPU:0, one launch (start us, length us, event | category | flops | bytes accessed | tf_op | source)
XLA Modules:
  0.0 61.5 jit_solution(6527646060870336461)
XLA Ops:
  1.5 0.8 %reduce.11 = bf16[4096]{0:T(1024)(128)(2,1)S(1)} reduce(bf16[1,4096]{1,0:T(2,128)(2,1)} %param.11, bf16[]{:T(256)} %constant.49), dimensions={0}, to_apply=%param.11.reduce_sub_computation | reduce | bytes 16386 | tf_op args[0]
  2.4 0.1 broadcast_multiply_fusion
  2.5 1.4 %fusion.18 = (f32[32]{0:T(128)S(1)}, f32[32,384]{1,0:T(8,128)S(1)}) fusion(bf16[1,384,512]{2,1,0:T(8,128)(2,1)} %param.12, bf16[4,8,4,128]{3,2,1,0:T(4,128)(2,1)S(1)} %bitcast.58, pred[384]{0:T(512)(128)(4,1)S(1)} %iota_compare_fusion.1), kind=kOutput, calls=%fused_computation.44 | convolution fusion | flops 12619744 | bytes 475648 | tf_op jit(solution)/shard_map/rhc,rsc->rhs/dot_general | solution.py:61
  3.8 0.2 fusion.9
  4.0 1.2 %convolution_bitcast_fusion = f32[1,32,512]{2,1,0:T(8,128)S(1)} fusion(bf16[1,384,512]{2,1,0:T(8,128)(2,1)} %param.13, f32[32,384]{1,0:T(8,128)S(1)} %get-tuple-element.9, f32[32]{0:T(128)S(1)} %fusion.9, f32[32]{0:T(128)S(1)} %get-tuple-element.8), kind=kOutput, calls=%fused_computation.2 | convolution fusion | flops 12619776 | bytes 508160 | tf_op jit(solution)/shard_map/rhs,rsc->rhc/dot_general | solution.py:69
  5.3 0.7 %multiply_reduce_fusion = bf16[32,128]{1,0:T(8,128)(2,1)} fusion(f32[1,32,4,128]{3,2,1,0:T(4,128)S(1)} %reshape.316, f32[32,4]{1,0:T(8,128)S(1)} %get-tuple-element.6), kind=kLoop, calls=%fused_computation.21 | loop fusion | flops 28672 | bytes 74240 | tf_op jit(solution)/shard_map/reduce_sum | solution.py:71
  6.0 7.4 %all-to-all-start = ((bf16[16,2,128]{2,1,0:T(2,128)(2,1)}), bf16[16,2,128]{2,1,0:T(2,128)(2,1)S(1)}, u32[]{:S(2)}, u32[]{:S(2)}) async-start(bf16[16,2,128]{2,1,0:T(2,128)(2,1)} %bitcast.4), calls=%async_computation | async-start | bytes 16384 | tf_op jit(solution)/shard_map/all_to_all | solution.py:75
  13.4 6.4 %all-to-all-done = bf16[16,2,128]{2,1,0:T(2,128)(2,1)S(1)} async-done(((bf16[16,2,128]{2,1,0:T(2,128)(2,1)}), bf16[16,2,128]{2,1,0:T(2,128)(2,1)S(1)}, u32[]{:S(2)}, u32[]{:S(2)}) %all-to-all-start) | async-done | bytes 8224 | tf_op jit(solution)/shard_map/all_to_all | solution.py:75
  19.8 0.4 fusion
  20.3 1.3 %collective-permute-done = f32[8,1,4096]{2,0,1:T(8,128)S(1)} collective-permute-done((f32[8,1,4096]{2,0,1:T(8,128)S(1)}, f32[8,1,4096]{2,0,1:T(8,128)S(1)}, u32[]{:S(2)}, u32[]{:S(2)}) %collective-permute-start) | collective-permute-done | bytes 131104 | tf_op jit(solution)/shard_map/ppermute | solution.py:32
  21.6 0.1 copy.43
  21.8 10.0 %all_to_all.23 = f32[8,1,4096]{2,1,0:T(1,128)S(1)} all-to-all(f32[8,1,4096]{2,1,0:T(1,128)S(1)} %copy.43), channel_id=1, replica_groups=mesh['groups'=2,'chip'=8,'core'=2] {'chip'}, dimensions={0} | all-to-all | bytes 262144 | tf_op jit(solution)/shard_map/all_to_all | solution.py:33
  31.7 0.1 reduce_sum.40
  31.9 0.7 %broadcast_in_dim.47 = bf16[8,2,2048]{2,1,0:T(2,128)(2,1)} broadcast(bf16[2,2048]{1,0:T(2,128)(2,1)S(1)} %broadcast_in_dim.46), dimensions={1,2} | broadcast | bytes 73728 | tf_op jit(solution)/shard_map/broadcast_in_dim | solution.py:18
  32.6 3.3 %all-to-all-start.2 = ((bf16[8,2,2048]{2,1,0:T(2,128)(2,1)}), bf16[8,2,2048]{2,1,0:T(2,128)(2,1)S(1)}, u32[]{:S(2)}, u32[]{:S(2)}) async-start(bf16[8,2,2048]{2,1,0:T(2,128)(2,1)} %broadcast_in_dim.47), calls=%async_computation.2 | async-start | bytes 131072 | tf_op jit(solution)/shard_map/all_to_all | solution.py:19
  36.0 6.8 %all-to-all-done.2 = bf16[8,2,2048]{2,1,0:T(2,128)(2,1)S(1)} async-done(((bf16[8,2,2048]{2,1,0:T(2,128)(2,1)}), bf16[8,2,2048]{2,1,0:T(2,128)(2,1)S(1)}, u32[]{:S(2)}, u32[]{:S(2)}) %all-to-all-start.2) | async-done | bytes 65568 | tf_op jit(solution)/shard_map/all_to_all | solution.py:19
  42.9 0.2 compare_reduce_fusion
  43.1 1.1 %collective-permute-done.1 = bf16[8,1,4096]{2,0,1:T(8,128)(2,1)S(1)} collective-permute-done((bf16[8,1,4096]{2,0,1:T(8,128)(2,1)S(1)}, bf16[8,1,4096]{2,0,1:T(8,128)(2,1)S(1)}, u32[]{:S(2)}, u32[]{:S(2)}) %collective-permute-start.1) | collective-permute-done | bytes 65568 | tf_op jit(solution)/shard_map/ppermute | solution.py:21
  44.2 0.1 copy.44
  44.4 3.0 %fusion.5 = bf16[16,512]{1,0:T(8,128)(2,1)S(1)} fusion(bf16[16,4096]{1,0:T(8,128)(2,1)S(1)} %reshape.318, bf16[4096,512]{1,0:T(8,128)(2,1)} %param.18, f32[512]{0:T(512)S(1)} %copy-done.5, pred[512]{0:T(512)(128)(4,1)S(1)} %compare_reduce_fusion), kind=kOutput, calls=%fused_computation.8 | convolution fusion | flops 67141632 | bytes 4344320 | tf_op jit(solution)/shard_map/dot_general | solution.py:90
  47.4 0.5 copy-done.1
  47.9 0.7 %fusion.19 = f32[16,4096]{1,0:T(8,128)S(1)} fusion(bf16[16,512]{1,0:T(8,128)(2,1)S(1)} %fusion.5, bf16[512,4096]{1,0:T(8,128)(2,1)S(1)} %copy-done.1), kind=kOutput, calls=%fused_computation.45 | convolution fusion | flops 67108864 | bytes 4472832 | tf_op jit(solution)/shard_map/dot_general | solution.py:93
  48.5 0.2 reshape.319
  48.7 0.2 fusion.17
  48.9 0.2 select_bitcast_fusion
  49.1 0.2 collective-permute-start.2
  49.3 1.2 %collective-permute-done.2 = f32[8,1,4096]{2,0,1:T(8,128)S(1)} collective-permute-done((f32[8,1,4096]{2,0,1:T(8,128)S(1)}, f32[8,1,4096]{2,0,1:T(8,128)S(1)}, u32[]{:S(2)}, u32[]{:S(2)}) %collective-permute-start.2) | collective-permute-done | bytes 131104 | tf_op jit(solution)/shard_map/ppermute | solution.py:32
  50.5 0.2 bitcast_add_fusion
  50.7 0.1 copy.47
  50.8 10.0 %all_to_all.24 = f32[8,1,4096]{2,1,0:T(1,128)S(1)} all-to-all(f32[8,1,4096]{2,1,0:T(1,128)S(1)} %copy.47), channel_id=1, replica_groups=mesh['groups'=2,'chip'=8,'core'=2] {'chip'}, dimensions={0} | all-to-all | bytes 262144 | tf_op jit(solution)/shard_map/all_to_all | solution.py:33
  60.8 0.1 reduce_sum.42
  60.9 0.6 %convert_element_type.56 = bf16[1,4096]{1,0:T(2,128)(2,1)} reshape(bf16[4096]{0:T(1024)(128)(2,1)S(1)} %add_convert_fusion) | data formatting | bytes 16384 | tf_op jit(solution)/shard_map/convert_element_type | solution.py:94
  (31 shorter events, 0.6 us)
Async XLA Ops:
  0.6 19.1 %copy-start = (bf16[256,4096]{1,0:T(8,128)(2,1)S(1)}, bf16[256,4096]{1,0:T(8,128)(2,1)}, u32[]{:S(2)}) copy-start(bf16[256,4096]{1,0:T(8,128)(2,1)} %param.16) | copy-start | bytes 6291460
  0.6 31.2 %copy-start.3 = (bf16[1,4096]{1,0:T(2,128)(2,1)S(1)}, bf16[1,4096]{1,0:T(2,128)(2,1)}, u32[]{:S(2)}) copy-start(bf16[1,4096]{1,0:T(2,128)(2,1)} %param.15) | copy-start | bytes 24580
  0.7 42.3 %copy-start.6 = (s32[256]{0:T(256)S(1)}, s32[256]{0:T(256)}, u32[]{:S(2)}) copy-start(s32[256]{0:T(256)} %param.17) | copy-start | bytes 3076
  0.7 43.7 %copy-start.5 = (f32[512]{0:T(512)S(1)}, f32[512]{0:T(512)}, u32[]{:S(2)}) copy-start(f32[512]{0:T(512)} %param.19) | copy-start | bytes 6148
  6.0 13.8 %all-to-all-start = ((bf16[16,2,128]{2,1,0:T(2,128)(2,1)}), bf16[16,2,128]{2,1,0:T(2,128)(2,1)S(1)}, u32[]{:S(2)}, u32[]{:S(2)}) async-start(bf16[16,2,128]{2,1,0:T(2,128)(2,1)} %bitcast.4), calls=%async_computation | async-start | bytes 16384 | tf_op jit(solution)/shard_map/all_to_all | solution.py:75
  20.2 1.4 %collective-permute-start = (f32[8,1,4096]{2,0,1:T(8,128)S(1)}, f32[8,1,4096]{2,0,1:T(8,128)S(1)}, u32[]{:S(2)}, u32[]{:S(2)}) collective-permute-start(f32[8,1,4096]{2,0,1:T(8,128)S(1)} %fusion.8), channel_id=1, source_target_pairs={{0,1},{1,0},{2,3},{3,2},{4,5},{5,4},{6,7},{7,6},{8,9},{9,8},{10,11... | collective-permute-start | bytes 393224 | tf_op jit(solution)/shard_map/ppermute | solution.py:32
  32.6 10.2 %all-to-all-start.2 = ((bf16[8,2,2048]{2,1,0:T(2,128)(2,1)}), bf16[8,2,2048]{2,1,0:T(2,128)(2,1)S(1)}, u32[]{:S(2)}, u32[]{:S(2)}) async-start(bf16[8,2,2048]{2,1,0:T(2,128)(2,1)} %broadcast_in_dim.47), calls=%async_computation.2 | async-start | bytes 131072 | tf_op jit(solution)/shard_map/all_to_all | solution.py:19
  42.8 1.3 %collective-permute-start.1 = (bf16[8,1,4096]{2,0,1:T(8,128)(2,1)S(1)}, bf16[8,1,4096]{2,0,1:T(8,128)(2,1)S(1)}, u32[]{:S(2)}, u32[]{:S(2)}) collective-permute-start(bf16[8,1,4096]{2,0,1:T(8,128)(2,1)S(1)} %reshape.317), channel_id=1, source_target_pairs={{0,1},{1,0},{2,3},{3,2},{4,5},{5,4},{6,7},{7,6},{8,9},{9,8},{10,11... | collective-permute-start | bytes 196616 | tf_op jit(solution)/shard_map/ppermute | solution.py:21
  44.4 3.5 %copy-start.1 = (bf16[512,4096]{1,0:T(8,128)(2,1)S(1)}, bf16[512,4096]{1,0:T(8,128)(2,1)}, u32[]{:S(2)}) copy-start(bf16[512,4096]{1,0:T(8,128)(2,1)} %param.20) | copy-start | bytes 12582916
  47.9 13.7 %copy-start.2 = (bf16[16,512]{1,0:T(8,128)(2,1)}, bf16[16,512]{1,0:T(8,128)(2,1)S(1)}, u32[]{:S(2)}) copy-start(bf16[16,512]{1,0:T(8,128)(2,1)S(1)} %fusion.5) | copy-start | bytes 49156
  47.9 13.0 %copy-start.4 = (f32[4096]{0:T(1024)S(1)}, f32[4096]{0:T(1024)}, u32[]{:S(2)}) copy-start(f32[4096]{0:T(1024)} %param.21) | copy-start | bytes 49156
  49.1 1.4 %collective-permute-start.2 = (f32[8,1,4096]{2,0,1:T(8,128)S(1)}, f32[8,1,4096]{2,0,1:T(8,128)S(1)}, u32[]{:S(2)}, u32[]{:S(2)}) collective-permute-start(f32[8,1,4096]{2,0,1:T(8,128)S(1)} %select_bitcast_fusion), channel_id=1, source_target_pairs={{0,1},{1,0},{2,3},{3,2},{4,5},{5,4},{6,7},{7,6},{8,9},{9,8},{10,11... | collective-permute-start | bytes 393224 | tf_op jit(solution)/shard_map/ppermute | solution.py:32

commit v8 on v7

--- a/solution.py
+++ b/solution.py
@@ -24,12 +24,16 @@
     return jnp.stack([first, second], axis=1).reshape(chips * 2 * x.shape[0], x.shape[1])
 
 
-def scatter_rows(x, chips):
+def scatter_rows(x, chips, narrow=False):
     per = x.shape[0] // (2 * chips)
     split = x.reshape(chips, 2, per, x.shape[1])
     keep = pick((split[:, 0], split[:, 1]), 0)
     give = pick((split[:, 1], split[:, 0]), 0)
     summed = keep + lax.ppermute(give, "core", [(0, 1), (1, 0)])
+    if narrow:
+        sent = summed.astype(jnp.bfloat16).reshape(chips * per * 2, x.shape[1] // 2)
+        got = lax.all_to_all(sent, "chip", split_axis=0, concat_axis=0, tiled=True)
+        return got.astype(jnp.float32).reshape(chips, per, x.shape[1]).sum(axis=0)
     got = lax.all_to_all(summed.reshape(chips * per, x.shape[1]), "chip", split_axis=0, concat_axis=0, tiled=True)
     return got.reshape(chips, per, x.shape[1]).sum(axis=0)
 
@@ -90,7 +94,7 @@
             jnp.dot(hidden, enc_weight, preferred_element_type=jnp.float32) + enc_bias[None, :]
         ),
     ).astype(jnp.bfloat16)
-    rebuilt = scatter_rows(jnp.dot(activity, dec_weight, preferred_element_type=jnp.float32), chips)
+    rebuilt = scatter_rows(jnp.dot(activity, dec_weight, preferred_element_type=jnp.float32), chips, narrow=True)
     spliced = (rebuilt + dec_bias[None, :]).astype(jnp.bfloat16)
     return (spliced, activity)
 

time: 62 us -> 61.2 us (0.987)
    all_to_all x2 -> x1, blocking collectives: 19.9 us -> 9.97 us  [scatter_rows(): lax.all_to_all(summed.reshape(chips * per, x.shape[1]), 'chip', split_axi...]
    all_to_all x0 -> x1, blocking collectives: none -> 9.29 us  [scatter_rows(): got = lax.all_to_all(sent, 'chip', split_axis=0, concat_axis=0, tiled=True)]
where the time goes in v8:
time: 61.2 us; the launch traced here: 60.7 us
  blocking collectives  19.3 us (32%)
  waiting for transfers between devices  16.8 us (27%)
  starting transfers between devices  11.1 us (18%)
  matrix products  6.59 us (11%)
  local copies, waits for them, and re-layouts  2.67 us (4%)
  other arithmetic  2.65 us (4%)
  between operations  1.69 us (3%)
    all_to_all x1, blocking collectives, scatter_rows(): lax.all_to_all(summed.reshape(chips * per, x.shape[1]), 'chip', split_axi...  9.97 us
    all_to_all x1, blocking collectives, scatter_rows(): got = lax.all_to_all(sent, 'chip', split_axis=0, concat_axis=0, tiled=True)  9.29 us
    all_to_all x1, starting transfers between devices, shards(): got = lax.all_to_all(blocks, ROWS, split_axis=0, concat_axis=0, tiled=True)  7.39 us
    all_to_all x1, waiting for transfers between devices, gather_rows(): lax.all_to_all(copies, 'chip', split_axis=0, concat_axis=0, tiled=True)  6.82 us
    all_to_all x1, waiting for transfers between devices, shards(): got = lax.all_to_all(blocks, ROWS, split_axis=0, concat_axis=0, tiled=True)  6.35 us
    all_to_all x1, starting transfers between devices, gather_rows(): lax.all_to_all(copies, 'chip', split_axis=0, concat_axis=0, tiled=True)  3.35 us
    dot_general x1, matrix products, shards(): jnp.dot(hidden, enc_weight, preferred_element_type=jnp.float32)  2.98 us
    ppermute x2, waiting for transfers between devices, scatter_rows(): summed = keep + lax.ppermute(give, 'core', [(0, 1), (1, 0)])  2.53 us
  transfers between devices with their start and end apart: 5, of which 5 were waited for; matrix products, arithmetic and copies ran while one was open for 0% of the time, Pallas kernels for 0%

profile of v8, /device:TPU:0, one launch (start us, length us, event | category | flops | bytes accessed | tf_op | source)
XLA Modules:
  0.0 60.7 jit_solution(3949510141494745603)
XLA Ops:
  1.5 0.8 %reduce.9 = bf16[4096]{0:T(1024)(128)(2,1)S(1)} reduce(bf16[1,4096]{1,0:T(2,128)(2,1)} %param.11, bf16[]{:T(256)} %constant.49), dimensions={0}, to_apply=%param.11.reduce_sub_computation | reduce | bytes 16386 | tf_op args[0]
  2.3 0.1 fusion.17
  2.4 0.1 broadcast_multiply_fusion
  2.5 1.4 %fusion.19 = (f32[32]{0:T(128)S(1)}, f32[32,384]{1,0:T(8,128)S(1)}) fusion(bf16[1,384,512]{2,1,0:T(8,128)(2,1)} %param.12, bf16[4,8,4,128]{3,2,1,0:T(4,128)(2,1)S(1)} %bitcast.64, pred[384]{0:T(512)(128)(4,1)S(1)} %iota_compare_fusion.1), kind=kOutput, calls=%fused_computation.46 | convolution fusion | flops 12619744 | bytes 475648 | tf_op jit(solution)/shard_map/rhc,rsc->rhs/dot_general | solution.py:65
  3.8 0.2 fusion.10
  4.0 1.2 %convolution_bitcast_fusion = f32[1,32,512]{2,1,0:T(8,128)S(1)} fusion(bf16[1,384,512]{2,1,0:T(8,128)(2,1)} %param.13, f32[32,384]{1,0:T(8,128)S(1)} %get-tuple-element.9, f32[32]{0:T(128)S(1)} %fusion.10, f32[32]{0:T(128)S(1)} %get-tuple-element.8), kind=kOutput, calls=%fused_computation.2 | convolution fusion | flops 12619776 | bytes 508160 | tf_op jit(solution)/shard_map/rhs,rsc->rhc/dot_general | solution.py:73
  5.3 0.7 %multiply_reduce_fusion = bf16[32,128]{1,0:T(8,128)(2,1)} fusion(f32[1,32,4,128]{3,2,1,0:T(4,128)S(1)} %reshape.317, f32[32,4]{1,0:T(8,128)S(1)} %get-tuple-element.6), kind=kLoop, calls=%fused_computation.23 | loop fusion | flops 28672 | bytes 74240 | tf_op jit(solution)/shard_map/reduce_sum | solution.py:75
  6.0 7.4 %all-to-all-start = ((bf16[16,2,128]{2,1,0:T(2,128)(2,1)}), bf16[16,2,128]{2,1,0:T(2,128)(2,1)S(1)}, u32[]{:S(2)}, u32[]{:S(2)}) async-start(bf16[16,2,128]{2,1,0:T(2,128)(2,1)} %bitcast.4), calls=%async_computation | async-start | bytes 16384 | tf_op jit(solution)/shard_map/all_to_all | solution.py:79
  13.4 6.4 %all-to-all-done = bf16[16,2,128]{2,1,0:T(2,128)(2,1)S(1)} async-done(((bf16[16,2,128]{2,1,0:T(2,128)(2,1)}), bf16[16,2,128]{2,1,0:T(2,128)(2,1)S(1)}, u32[]{:S(2)}, u32[]{:S(2)}) %all-to-all-start) | async-done | bytes 8224 | tf_op jit(solution)/shard_map/all_to_all | solution.py:79
  19.8 0.4 fusion
  20.2 0.1 collective-permute-start
  20.3 1.3 %collective-permute-done = f32[8,1,4096]{2,0,1:T(8,128)S(1)} collective-permute-done((f32[8,1,4096]{2,0,1:T(8,128)S(1)}, f32[8,1,4096]{2,0,1:T(8,128)S(1)}, u32[]{:S(2)}, u32[]{:S(2)}) %collective-permute-start) | collective-permute-done | bytes 131104 | tf_op jit(solution)/shard_map/ppermute | solution.py:32
  21.6 0.1 copy.43
  21.8 10.0 %all_to_all.26 = f32[8,1,4096]{2,1,0:T(1,128)S(1)} all-to-all(f32[8,1,4096]{2,1,0:T(1,128)S(1)} %copy.43), channel_id=1, replica_groups=mesh['groups'=2,'chip'=8,'core'=2] {'chip'}, dimensions={0} | all-to-all | bytes 262144 | tf_op jit(solution)/shard_map/all_to_all | solution.py:37
  31.7 0.1 reduce_sum.42
  31.9 0.7 %broadcast_in_dim.47 = bf16[8,2,2048]{2,1,0:T(2,128)(2,1)} broadcast(bf16[2,2048]{1,0:T(2,128)(2,1)S(1)} %broadcast_in_dim.46), dimensions={1,2} | broadcast | bytes 73728 | tf_op jit(solution)/shard_map/broadcast_in_dim | solution.py:18
  32.6 3.3 %all-to-all-start.2 = ((bf16[8,2,2048]{2,1,0:T(2,128)(2,1)}), bf16[8,2,2048]{2,1,0:T(2,128)(2,1)S(1)}, u32[]{:S(2)}, u32[]{:S(2)}) async-start(bf16[8,2,2048]{2,1,0:T(2,128)(2,1)} %broadcast_in_dim.47), calls=%async_computation.2 | async-start | bytes 131072 | tf_op jit(solution)/shard_map/all_to_all | solution.py:19
  36.0 6.8 %all-to-all-done.2 = bf16[8,2,2048]{2,1,0:T(2,128)(2,1)S(1)} async-done(((bf16[8,2,2048]{2,1,0:T(2,128)(2,1)}), bf16[8,2,2048]{2,1,0:T(2,128)(2,1)S(1)}, u32[]{:S(2)}, u32[]{:S(2)}) %all-to-all-start.2) | async-done | bytes 65568 | tf_op jit(solution)/shard_map/all_to_all | solution.py:19
  42.9 0.2 compare_reduce_fusion
  43.1 1.1 %collective-permute-done.1 = bf16[8,1,4096]{2,0,1:T(8,128)(2,1)S(1)} collective-permute-done((bf16[8,1,4096]{2,0,1:T(8,128)(2,1)S(1)}, bf16[8,1,4096]{2,0,1:T(8,128)(2,1)S(1)}, u32[]{:S(2)}, u32[]{:S(2)}) %collective-permute-start.1) | collective-permute-done | bytes 65568 | tf_op jit(solution)/shard_map/ppermute | solution.py:21
  44.2 0.1 copy.44
  44.4 3.0 %fusion.5 = bf16[16,512]{1,0:T(8,128)(2,1)S(1)} fusion(bf16[16,4096]{1,0:T(8,128)(2,1)S(1)} %reshape.319, bf16[4096,512]{1,0:T(8,128)(2,1)} %param.18, f32[512]{0:T(512)S(1)} %copy-done.5, pred[512]{0:T(512)(128)(4,1)S(1)} %compare_reduce_fusion), kind=kOutput, calls=%fused_computation.8 | convolution fusion | flops 67141632 | bytes 4344320 | tf_op jit(solution)/shard_map/dot_general | solution.py:94
  47.4 0.5 copy-done.1
  47.9 0.7 %fusion.20 = f32[16,4096]{1,0:T(8,128)S(1)} fusion(bf16[16,512]{1,0:T(8,128)(2,1)S(1)} %fusion.5, bf16[512,4096]{1,0:T(8,128)(2,1)S(1)} %copy-done.1), kind=kOutput, calls=%fused_computation.47 | convolution fusion | flops 67108864 | bytes 4472832 | tf_op jit(solution)/shard_map/dot_general | solution.py:97
  48.5 0.2 reshape.320
  48.7 0.2 fusion.18
  48.9 0.2 select_bitcast_fusion
  49.1 0.2 collective-permute-start.2
  49.3 1.2 %collective-permute-done.2 = f32[8,1,4096]{2,0,1:T(8,128)S(1)} collective-permute-done((f32[8,1,4096]{2,0,1:T(8,128)S(1)}, f32[8,1,4096]{2,0,1:T(8,128)S(1)}, u32[]{:S(2)}, u32[]{:S(2)}) %collective-permute-start.2) | collective-permute-done | bytes 131104 | tf_op jit(solution)/shard_map/ppermute | solution.py:32
  50.5 0.1 fusion.8
  50.7 9.3 %all_to_all.27 = bf16[8,2,2048]{2,1,0:T(2,128)(2,1)S(1)} all-to-all(bf16[8,2,2048]{2,1,0:T(2,128)(2,1)S(1)} %copy.47), channel_id=1, replica_groups=mesh['groups'=2,'chip'=8,'core'=2] {'chip'}, dimensions={0} | all-to-all | bytes 131072 | tf_op jit(solution)/shard_map/all_to_all | solution.py:35
  60.1 0.6 %convert_element_type.66 = bf16[1,4096]{1,0:T(2,128)(2,1)} reshape(bf16[4096]{0:T(1024)(128)(2,1)S(1)} %add_convert_fusion) | data formatting | bytes 16384 | tf_op jit(solution)/shard_map/convert_element_type | solution.py:98
  (32 shorter events, 0.6 us)
Async XLA Ops:
  0.6 19.1 %copy-start = (bf16[256,4096]{1,0:T(8,128)(2,1)S(1)}, bf16[256,4096]{1,0:T(8,128)(2,1)}, u32[]{:S(2)}) copy-start(bf16[256,4096]{1,0:T(8,128)(2,1)} %param.16) | copy-start | bytes 6291460
  0.6 31.2 %copy-start.3 = (bf16[1,4096]{1,0:T(2,128)(2,1)S(1)}, bf16[1,4096]{1,0:T(2,128)(2,1)}, u32[]{:S(2)}) copy-start(bf16[1,4096]{1,0:T(2,128)(2,1)} %param.15) | copy-start | bytes 24580
  0.7 42.3 %copy-start.6 = (s32[256]{0:T(256)S(1)}, s32[256]{0:T(256)}, u32[]{:S(2)}) copy-start(s32[256]{0:T(256)} %param.17) | copy-start | bytes 3076
  0.7 43.7 %copy-start.5 = (f32[512]{0:T(512)S(1)}, f32[512]{0:T(512)}, u32[]{:S(2)}) copy-start(f32[512]{0:T(512)} %param.19) | copy-start | bytes 6148
  6.0 13.8 %all-to-all-start = ((bf16[16,2,128]{2,1,0:T(2,128)(2,1)}), bf16[16,2,128]{2,1,0:T(2,128)(2,1)S(1)}, u32[]{:S(2)}, u32[]{:S(2)}) async-start(bf16[16,2,128]{2,1,0:T(2,128)(2,1)} %bitcast.4), calls=%async_computation | async-start | bytes 16384 | tf_op jit(solution)/shard_map/all_to_all | solution.py:79
  20.2 1.4 %collective-permute-start = (f32[8,1,4096]{2,0,1:T(8,128)S(1)}, f32[8,1,4096]{2,0,1:T(8,128)S(1)}, u32[]{:S(2)}, u32[]{:S(2)}) collective-permute-start(f32[8,1,4096]{2,0,1:T(8,128)S(1)} %fusion.9), channel_id=1, source_target_pairs={{0,1},{1,0},{2,3},{3,2},{4,5},{5,4},{6,7},{7,6},{8,9},{9,8},{10,11... | collective-permute-start | bytes 393224 | tf_op jit(solution)/shard_map/ppermute | solution.py:32
  32.6 10.2 %all-to-all-start.2 = ((bf16[8,2,2048]{2,1,0:T(2,128)(2,1)}), bf16[8,2,2048]{2,1,0:T(2,128)(2,1)S(1)}, u32[]{:S(2)}, u32[]{:S(2)}) async-start(bf16[8,2,2048]{2,1,0:T(2,128)(2,1)} %broadcast_in_dim.47), calls=%async_computation.2 | async-start | bytes 131072 | tf_op jit(solution)/shard_map/all_to_all | solution.py:19
  42.8 1.3 %collective-permute-start.1 = (bf16[8,1,4096]{2,0,1:T(8,128)(2,1)S(1)}, bf16[8,1,4096]{2,0,1:T(8,128)(2,1)S(1)}, u32[]{:S(2)}, u32[]{:S(2)}) collective-permute-start(bf16[8,1,4096]{2,0,1:T(8,128)(2,1)S(1)} %reshape.318), channel_id=1, source_target_pairs={{0,1},{1,0},{2,3},{3,2},{4,5},{5,4},{6,7},{7,6},{8,9},{9,8},{10,11... | collective-permute-start | bytes 196616 | tf_op jit(solution)/shard_map/ppermute | solution.py:21
  44.4 3.5 %copy-start.1 = (bf16[512,4096]{1,0:T(8,128)(2,1)S(1)}, bf16[512,4096]{1,0:T(8,128)(2,1)}, u32[]{:S(2)}) copy-start(bf16[512,4096]{1,0:T(8,128)(2,1)} %param.20) | copy-start | bytes 12582916
  47.9 12.9 %copy-start.2 = (bf16[16,512]{1,0:T(8,128)(2,1)}, bf16[16,512]{1,0:T(8,128)(2,1)S(1)}, u32[]{:S(2)}) copy-start(bf16[16,512]{1,0:T(8,128)(2,1)S(1)} %fusion.5) | copy-start | bytes 49156
  47.9 12.2 %copy-start.4 = (f32[4096]{0:T(1024)S(1)}, f32[4096]{0:T(1024)}, u32[]{:S(2)}) copy-start(f32[4096]{0:T(1024)} %param.21) | copy-start | bytes 49156
  49.1 1.4 %collective-permute-start.2 = (f32[8,1,4096]{2,0,1:T(8,128)S(1)}, f32[8,1,4096]{2,0,1:T(8,128)S(1)}, u32[]{:S(2)}, u32[]{:S(2)}) collective-permute-start(f32[8,1,4096]{2,0,1:T(8,128)S(1)} %select_bitcast_fusion), channel_id=1, source_target_pairs={{0,1},{1,0},{2,3},{3,2},{4,5},{5,4},{6,7},{7,6},{8,9},{9,8},{10,11... | collective-permute-start | bytes 393224 | tf_op jit(solution)/shard_map/ppermute | solution.py:32

commit v9 on v8

--- a/solution.py
+++ b/solution.py
@@ -82,7 +82,7 @@
         attended = attended.reshape(rows_here, heads * HEAD_DIM)
         features = lax.all_to_all(attended, ROWS, split_axis=1, concat_axis=0, tiled=True)
     partial_value = jnp.dot(features, out_weight, preferred_element_type=jnp.float32)
-    hidden_here = (scatter_rows(partial_value, chips) + resid.astype(jnp.float32)).astype(jnp.bfloat16)
+    hidden_here = (scatter_rows(partial_value, chips, narrow=True) + resid.astype(jnp.float32)).astype(jnp.bfloat16)
     hidden = gather_rows(hidden_here, chips)
     lat_here = enc_weight.shape[1]
     latent_ids = lax.axis_index(ROWS) * lat_here + lax.broadcasted_iota(jnp.int32, (lat_here,), 0)

time: 61.2 us -> 60.4 us (0.987)
  blocking collectives: 19.3 us -> 18.6 us
    all_to_all x1 -> x0, blocking collectives: 9.97 us -> none  [scatter_rows(): lax.all_to_all(summed.reshape(chips * per, x.shape[1]), 'chip', split_axi...]
    all_to_all x1 -> x2, blocking collectives: 9.29 us -> 18.6 us  [scatter_rows(): got = lax.all_to_all(sent, 'chip', split_axis=0, concat_axis=0, tiled=True)]
where the time goes in v9:
time: 60.4 us; the launch traced here: 60 us
  blocking collectives  18.6 us (31%)
  waiting for transfers between devices  16.8 us (28%)
  starting transfers between devices  11.1 us (18%)
  matrix products  6.59 us (11%)
  local copies, waits for them, and re-layouts  2.62 us (4%)
  other arithmetic  2.61 us (4%)
  between operations  1.7 us (3%)
    all_to_all x2, blocking collectives, scatter_rows(): got = lax.all_to_all(sent, 'chip', split_axis=0, concat_axis=0, tiled=True)  18.6 us
    all_to_all x1, starting transfers between devices, shards(): got = lax.all_to_all(blocks, ROWS, split_axis=0, concat_axis=0, tiled=True)  7.39 us
    all_to_all x1, waiting for transfers between devices, gather_rows(): lax.all_to_all(copies, 'chip', split_axis=0, concat_axis=0, tiled=True)  6.82 us
    all_to_all x1, waiting for transfers between devices, shards(): got = lax.all_to_all(blocks, ROWS, split_axis=0, concat_axis=0, tiled=True)  6.35 us
    all_to_all x1, starting transfers between devices, gather_rows(): lax.all_to_all(copies, 'chip', split_axis=0, concat_axis=0, tiled=True)  3.35 us
    dot_general x1, matrix products, shards(): jnp.dot(hidden, enc_weight, preferred_element_type=jnp.float32)  2.98 us
    ppermute x2, waiting for transfers between devices, scatter_rows(): summed = keep + lax.ppermute(give, 'core', [(0, 1), (1, 0)])  2.53 us
    dot_general x1, matrix products, shards(): jnp.einsum('rhc,rsc->rhs', spread, keys, preferred_element_type=jnp.float32)  1.36 us
  transfers between devices with their start and end apart: 5, of which 5 were waited for; matrix products, arithmetic and copies ran while one was open for 0% of the time, Pallas kernels for 0%

profile of v9, /device:TPU:0, one launch (start us, length us, event | category | flops | bytes accessed | tf_op | source)
XLA Modules:
  0.0 60.0 jit_solution(754856860108556983)
XLA Ops:
  1.5 0.8 %reduce.7 = bf16[4096]{0:T(1024)(128)(2,1)S(1)} reduce(bf16[1,4096]{1,0:T(2,128)(2,1)} %param.11, bf16[]{:T(256)} %constant.49), dimensions={0}, to_apply=%param.11.reduce_sub_computation | reduce | bytes 16386 | tf_op args[0]
  2.3 0.1 fusion.18
  2.4 0.1 broadcast_multiply_fusion
  2.5 1.4 %fusion.20 = (f32[32]{0:T(128)S(1)}, f32[32,384]{1,0:T(8,128)S(1)}) fusion(bf16[1,384,512]{2,1,0:T(8,128)(2,1)} %param.12, bf16[4,8,4,128]{3,2,1,0:T(4,128)(2,1)S(1)} %bitcast.70, pred[384]{0:T(512)(128)(4,1)S(1)} %iota_compare_fusion.1), kind=kOutput, calls=%fused_computation.48 | convolution fusion | flops 12619744 | bytes 475648 | tf_op jit(solution)/shard_map/rhc,rsc->rhs/dot_general | solution.py:65
  3.8 0.2 fusion.11
  4.0 1.2 %convolution_bitcast_fusion = f32[1,32,512]{2,1,0:T(8,128)S(1)} fusion(bf16[1,384,512]{2,1,0:T(8,128)(2,1)} %param.13, f32[32,384]{1,0:T(8,128)S(1)} %get-tuple-element.9, f32[32]{0:T(128)S(1)} %fusion.11, f32[32]{0:T(128)S(1)} %get-tuple-element.8), kind=kOutput, calls=%fused_computation.2 | convolution fusion | flops 12619776 | bytes 508160 | tf_op jit(solution)/shard_map/rhs,rsc->rhc/dot_general | solution.py:73
  5.3 0.7 %multiply_reduce_fusion = bf16[32,128]{1,0:T(8,128)(2,1)} fusion(f32[1,32,4,128]{3,2,1,0:T(4,128)S(1)} %reshape.318, f32[32,4]{1,0:T(8,128)S(1)} %get-tuple-element.6), kind=kLoop, calls=%fused_computation.25 | loop fusion | flops 28672 | bytes 74240 | tf_op jit(solution)/shard_map/reduce_sum | solution.py:75
  6.0 7.4 %all-to-all-start = ((bf16[16,2,128]{2,1,0:T(2,128)(2,1)}), bf16[16,2,128]{2,1,0:T(2,128)(2,1)S(1)}, u32[]{:S(2)}, u32[]{:S(2)}) async-start(bf16[16,2,128]{2,1,0:T(2,128)(2,1)} %bitcast.4), calls=%async_computation | async-start | bytes 16384 | tf_op jit(solution)/shard_map/all_to_all | solution.py:79
  13.4 6.4 %all-to-all-done = bf16[16,2,128]{2,1,0:T(2,128)(2,1)S(1)} async-done(((bf16[16,2,128]{2,1,0:T(2,128)(2,1)}), bf16[16,2,128]{2,1,0:T(2,128)(2,1)S(1)}, u32[]{:S(2)}, u32[]{:S(2)}) %all-to-all-start) | async-done | bytes 8224 | tf_op jit(solution)/shard_map/all_to_all | solution.py:79
  19.8 0.4 fusion
  20.2 0.1 collective-permute-start
  20.3 1.3 %collective-permute-done = f32[8,1,4096]{2,0,1:T(8,128)S(1)} collective-permute-done((f32[8,1,4096]{2,0,1:T(8,128)S(1)}, f32[8,1,4096]{2,0,1:T(8,128)S(1)}, u32[]{:S(2)}, u32[]{:S(2)}) %collective-permute-start) | collective-permute-done | bytes 131104 | tf_op jit(solution)/shard_map/ppermute | solution.py:32
  21.7 9.3 %all_to_all.29 = bf16[8,2,2048]{2,1,0:T(2,128)(2,1)S(1)} all-to-all(bf16[8,2,2048]{2,1,0:T(2,128)(2,1)S(1)} %copy.43), channel_id=1, replica_groups=mesh['groups'=2,'chip'=8,'core'=2] {'chip'}, dimensions={0} | all-to-all | bytes 131072 | tf_op jit(solution)/shard_map/all_to_all | solution.py:35
  31.2 0.7 %broadcast_in_dim.47 = bf16[8,2,2048]{2,1,0:T(2,128)(2,1)} broadcast(bf16[2,2048]{1,0:T(2,128)(2,1)S(1)} %broadcast_in_dim.46), dimensions={1,2} | broadcast | bytes 73728 | tf_op jit(solution)/shard_map/broadcast_in_dim | solution.py:18
  31.8 3.3 %all-to-all-start.2 = ((bf16[8,2,2048]{2,1,0:T(2,128)(2,1)}), bf16[8,2,2048]{2,1,0:T(2,128)(2,1)S(1)}, u32[]{:S(2)}, u32[]{:S(2)}) async-start(bf16[8,2,2048]{2,1,0:T(2,128)(2,1)} %broadcast_in_dim.47), calls=%async_computation.2 | async-start | bytes 131072 | tf_op jit(solution)/shard_map/all_to_all | solution.py:19
  35.2 6.8 %all-to-all-done.2 = bf16[8,2,2048]{2,1,0:T(2,128)(2,1)S(1)} async-done(((bf16[8,2,2048]{2,1,0:T(2,128)(2,1)}), bf16[8,2,2048]{2,1,0:T(2,128)(2,1)S(1)}, u32[]{:S(2)}, u32[]{:S(2)}) %all-to-all-start.2) | async-done | bytes 65568 | tf_op jit(solution)/shard_map/all_to_all | solution.py:19
  42.1 0.1 collective-permute-start.1
  42.1 0.2 compare_reduce_fusion
  42.3 1.1 %collective-permute-done.1 = bf16[8,1,4096]{2,0,1:T(8,128)(2,1)S(1)} collective-permute-done((bf16[8,1,4096]{2,0,1:T(8,128)(2,1)S(1)}, bf16[8,1,4096]{2,0,1:T(8,128)(2,1)S(1)}, u32[]{:S(2)}, u32[]{:S(2)}) %collective-permute-start.1) | collective-permute-done | bytes 65568 | tf_op jit(solution)/shard_map/ppermute | solution.py:21
  43.4 0.1 copy.44
  43.6 3.0 %fusion.5 = bf16[16,512]{1,0:T(8,128)(2,1)S(1)} fusion(bf16[16,4096]{1,0:T(8,128)(2,1)S(1)} %reshape.320, bf16[4096,512]{1,0:T(8,128)(2,1)} %param.18, f32[512]{0:T(512)S(1)} %copy-done.5, pred[512]{0:T(512)(128)(4,1)S(1)} %compare_reduce_fusion), kind=kOutput, calls=%fused_computation.8 | convolution fusion | flops 67141632 | bytes 4344320 | tf_op jit(solution)/shard_map/dot_general | solution.py:94
  46.6 0.5 copy-done.1
  47.1 0.7 %fusion.21 = f32[16,4096]{1,0:T(8,128)S(1)} fusion(bf16[16,512]{1,0:T(8,128)(2,1)S(1)} %fusion.5, bf16[512,4096]{1,0:T(8,128)(2,1)S(1)} %copy-done.1), kind=kOutput, calls=%fused_computation.49 | convolution fusion | flops 67108864 | bytes 4472832 | tf_op jit(solution)/shard_map/dot_general | solution.py:97
  47.7 0.2 reshape.321
  47.9 0.2 fusion.19
  48.2 0.2 select_bitcast_fusion
  48.3 0.2 collective-permute-start.2
  48.5 1.2 %collective-permute-done.2 = f32[8,1,4096]{2,0,1:T(8,128)S(1)} collective-permute-done((f32[8,1,4096]{2,0,1:T(8,128)S(1)}, f32[8,1,4096]{2,0,1:T(8,128)S(1)}, u32[]{:S(2)}, u32[]{:S(2)}) %collective-permute-start.2) | collective-permute-done | bytes 131104 | tf_op jit(solution)/shard_map/ppermute | solution.py:32
  49.7 0.1 fusion.8
  49.9 0.1 copy.47
  50.0 9.3 %all_to_all.30 = bf16[8,2,2048]{2,1,0:T(2,128)(2,1)S(1)} all-to-all(bf16[8,2,2048]{2,1,0:T(2,128)(2,1)S(1)} %copy.47), channel_id=1, replica_groups=mesh['groups'=2,'chip'=8,'core'=2] {'chip'}, dimensions={0} | all-to-all | bytes 131072 | tf_op jit(solution)/shard_map/all_to_all | solution.py:35
  59.3 0.6 %convert_element_type.76 = bf16[1,4096]{1,0:T(2,128)(2,1)} reshape(bf16[4096]{0:T(1024)(128)(2,1)S(1)} %add_convert_fusion) | data formatting | bytes 16384 | tf_op jit(solution)/shard_map/convert_element_type | solution.py:98
  (33 shorter events, 0.6 us)
Async XLA Ops:
  0.6 19.1 %copy-start = (bf16[256,4096]{1,0:T(8,128)(2,1)S(1)}, bf16[256,4096]{1,0:T(8,128)(2,1)}, u32[]{:S(2)}) copy-start(bf16[256,4096]{1,0:T(8,128)(2,1)} %param.16) | copy-start | bytes 6291460
  0.6 30.4 %copy-start.3 = (bf16[1,4096]{1,0:T(2,128)(2,1)S(1)}, bf16[1,4096]{1,0:T(2,128)(2,1)}, u32[]{:S(2)}) copy-start(bf16[1,4096]{1,0:T(2,128)(2,1)} %param.15) | copy-start | bytes 24580
  0.7 41.5 %copy-start.6 = (s32[256]{0:T(256)S(1)}, s32[256]{0:T(256)}, u32[]{:S(2)}) copy-start(s32[256]{0:T(256)} %param.17) | copy-start | bytes 3076
  0.7 43.0 %copy-start.5 = (f32[512]{0:T(512)S(1)}, f32[512]{0:T(512)}, u32[]{:S(2)}) copy-start(f32[512]{0:T(512)} %param.19) | copy-start | bytes 6148
  6.0 13.8 %all-to-all-start = ((bf16[16,2,128]{2,1,0:T(2,128)(2,1)}), bf16[16,2,128]{2,1,0:T(2,128)(2,1)S(1)}, u32[]{:S(2)}, u32[]{:S(2)}) async-start(bf16[16,2,128]{2,1,0:T(2,128)(2,1)} %bitcast.4), calls=%async_computation | async-start | bytes 16384 | tf_op jit(solution)/shard_map/all_to_all | solution.py:79
  20.2 1.4 %collective-permute-start = (f32[8,1,4096]{2,0,1:T(8,128)S(1)}, f32[8,1,4096]{2,0,1:T(8,128)S(1)}, u32[]{:S(2)}, u32[]{:S(2)}) collective-permute-start(f32[8,1,4096]{2,0,1:T(8,128)S(1)} %fusion.9), channel_id=1, source_target_pairs={{0,1},{1,0},{2,3},{3,2},{4,5},{5,4},{6,7},{7,6},{8,9},{9,8},{10,11... | collective-permute-start | bytes 393224 | tf_op jit(solution)/shard_map/ppermute | solution.py:32
  31.8 10.2 %all-to-all-start.2 = ((bf16[8,2,2048]{2,1,0:T(2,128)(2,1)}), bf16[8,2,2048]{2,1,0:T(2,128)(2,1)S(1)}, u32[]{:S(2)}, u32[]{:S(2)}) async-start(bf16[8,2,2048]{2,1,0:T(2,128)(2,1)} %broadcast_in_dim.47), calls=%async_computation.2 | async-start | bytes 131072 | tf_op jit(solution)/shard_map/all_to_all | solution.py:19
  42.1 1.3 %collective-permute-start.1 = (bf16[8,1,4096]{2,0,1:T(8,128)(2,1)S(1)}, bf16[8,1,4096]{2,0,1:T(8,128)(2,1)S(1)}, u32[]{:S(2)}, u32[]{:S(2)}) collective-permute-start(bf16[8,1,4096]{2,0,1:T(8,128)(2,1)S(1)} %reshape.319), channel_id=1, source_target_pairs={{0,1},{1,0},{2,3},{3,2},{4,5},{5,4},{6,7},{7,6},{8,9},{9,8},{10,11... | collective-permute-start | bytes 196616 | tf_op jit(solution)/shard_map/ppermute | solution.py:21
  43.6 3.5 %copy-start.1 = (bf16[512,4096]{1,0:T(8,128)(2,1)S(1)}, bf16[512,4096]{1,0:T(8,128)(2,1)}, u32[]{:S(2)}) copy-start(bf16[512,4096]{1,0:T(8,128)(2,1)} %param.20) | copy-start | bytes 12582916
  47.1 12.9 %copy-start.2 = (bf16[16,512]{1,0:T(8,128)(2,1)}, bf16[16,512]{1,0:T(8,128)(2,1)S(1)}, u32[]{:S(2)}) copy-start(bf16[16,512]{1,0:T(8,128)(2,1)S(1)} %fusion.5) | copy-start | bytes 49156
  47.1 12.2 %copy-start.4 = (f32[4096]{0:T(1024)S(1)}, f32[4096]{0:T(1024)}, u32[]{:S(2)}) copy-start(f32[4096]{0:T(1024)} %param.21) | copy-start | bytes 49156
  48.3 1.4 %collective-permute-start.2 = (f32[8,1,4096]{2,0,1:T(8,128)S(1)}, f32[8,1,4096]{2,0,1:T(8,128)S(1)}, u32[]{:S(2)}, u32[]{:S(2)}) collective-permute-start(f32[8,1,4096]{2,0,1:T(8,128)S(1)} %select_bitcast_fusion), channel_id=1, source_target_pairs={{0,1},{1,0},{2,3},{3,2},{4,5},{5,4},{6,7},{7,6},{8,9},{9,8},{10,11... | collective-permute-start | bytes 393224 | tf_op jit(solution)/shard_map/ppermute | solution.py:32

commit v10 on v9

--- a/solution.py
+++ b/solution.py
@@ -1,9 +1,45 @@
 import jax
+from jax.experimental import pallas as pl
+from jax.experimental.pallas import tpu as pltpu
 import jax.numpy as jnp
 from jax import lax
 from jax.sharding import Mesh, PartitionSpec as P
 
 HEAD_DIM = 128
+
+
+def attend_kernel(len_ref, q_ref, k_ref, v_ref, o_ref):
+    live = len_ref[pl.program_id(0)]
+    s = lax.dot_general(q_ref[...], k_ref[0], (((1,), (1,)), ((), ())), preferred_element_type=jnp.float32)
+    s = s / jnp.sqrt(jnp.float32(HEAD_DIM))
+    pos = lax.broadcasted_iota(jnp.int32, s.shape, 1)
+    s = jnp.where(pos < live, s, -jnp.inf)
+    e = jnp.exp(s - jnp.max(s, axis=-1, keepdims=True))
+    w = (e / jnp.sum(e, axis=-1, keepdims=True)).astype(jnp.bfloat16)
+    o_ref[...] = jnp.dot(w, v_ref[0], preferred_element_type=jnp.float32).astype(o_ref.dtype)
+
+
+def attend(queries, keys, values, lengths):
+    rows_here, span, key_width = keys.shape
+    kv_count = key_width // HEAD_DIM
+    heads = queries.shape[1] // HEAD_DIM
+    group_size = heads // kv_count
+    q2 = queries.reshape(rows_here * heads, HEAD_DIM)
+    grid_spec = pltpu.PrefetchScalarGridSpec(
+        num_scalar_prefetch=1,
+        grid=(rows_here, kv_count),
+        in_specs=[
+            pl.BlockSpec((group_size, HEAD_DIM), lambda i, k, n: (i * kv_count + k, 0)),
+            pl.BlockSpec((1, span, HEAD_DIM), lambda i, k, n: (i, 0, k)),
+            pl.BlockSpec((1, span, HEAD_DIM), lambda i, k, n: (i, 0, k)),
+        ],
+        out_specs=pl.BlockSpec((group_size, HEAD_DIM), lambda i, k, n: (i * kv_count + k, 0)),
+    )
+    return pl.pallas_call(
+        attend_kernel,
+        grid_spec=grid_spec,
+        out_shape=jax.ShapeDtypeStruct((rows_here * heads, HEAD_DIM), jnp.bfloat16),
+    )(lengths, q2, keys, values)
 
 
 ROWS = ("chip", "core")
@@ -57,22 +93,7 @@
     kv_count = key_width // HEAD_DIM
     heads = queries.shape[1] // HEAD_DIM
     group_size = heads // kv_count
-    head_of = lax.broadcasted_iota(jnp.int32, (heads, kv_count), 0) // group_size
-    block_of = lax.broadcasted_iota(jnp.int32, (heads, kv_count), 1)
-    onehot = (head_of == block_of).astype(jnp.bfloat16)
-    query_heads = queries.reshape(rows_here, heads, 1, HEAD_DIM)
-    spread = (query_heads * onehot[None, :, :, None]).reshape(rows_here, heads, key_width)
-    scores = jnp.einsum("rhc,rsc->rhs", spread, keys, preferred_element_type=jnp.float32)
-    scores = scores / jnp.sqrt(jnp.float32(HEAD_DIM))
-    cache_span = keys.shape[1]
-    visible = lax.broadcasted_iota(jnp.int32, (rows_here, cache_span), 1) < lengths[:, None]
-    scores = jnp.where(visible[:, None, :], scores, -jnp.inf)
-    highest = jnp.max(scores, axis=-1, keepdims=True)
-    expo = jnp.exp(scores - highest)
-    weights = (expo / jnp.sum(expo, axis=-1, keepdims=True)).astype(jnp.bfloat16)
-    mixed = jnp.einsum("rhs,rsc->rhc", weights, values, preferred_element_type=jnp.float32)
-    mixed = lax.optimization_barrier(mixed).reshape(rows_here, heads, kv_count, HEAD_DIM) * onehot.astype(jnp.float32)[None, :, :, None]
-    attended = mixed.sum(axis=2).astype(jnp.bfloat16)
+    attended = attend(queries, keys, values, lengths)
     count = 2 * chips
     if heads % count == 0:
         blocks = attended.reshape(rows_here * count, heads // count, HEAD_DIM)

time: 60.4 us -> 61.2 us (1.013)
  Pallas kernels: 0 us -> 3.97 us
  matrix products: 6.59 us -> 4.02 us
    pallas_call x0 -> x1, Pallas kernels: none -> 3.97 us  [attend(): pl.pallas_call(attend_kernel, grid_spec=grid_spec, out_shape=jax.ShapeDty...]
    dot_general x2 -> x0, matrix products: 2.57 us -> none  [the longest x1 1.36 us: shards(): jnp.einsum('rhc,rsc->rhs', spread, keys, preferred_element_type=jnp.float32)]
    reduce_sum x2 -> x0, other arithmetic: 0.92 us -> none  [the longest x1 0.72 us: shards(): attended = mixed.sum(axis=2).astype(jnp.bfloat16)]
where the time goes in v10:
time: 61.2 us; the launch traced here: 60.8 us
  blocking collectives  18.6 us (30%)
  waiting for transfers between devices  16.8 us (27%)
  starting transfers between devices  11.1 us (18%)
  matrix products  4.02 us (7%)
  Pallas kernels  3.97 us (6%)
  local copies, waits for them, and re-layouts  2.57 us (4%)
  other arithmetic  2.09 us (3%)
  between operations  1.66 us (3%)
    all_to_all x2, blocking collectives, scatter_rows(): got = lax.all_to_all(sent, 'chip', split_axis=0, concat_axis=0, tiled=True)  18.6 us
    all_to_all x1, starting transfers between devices, shards(): got = lax.all_to_all(blocks, ROWS, split_axis=0, concat_axis=0, tiled=True)  7.39 us
    all_to_all x1, waiting for transfers between devices, gather_rows(): lax.all_to_all(copies, 'chip', split_axis=0, concat_axis=0, tiled=True)  6.82 us
    all_to_all x1, waiting for transfers between devices, shards(): got = lax.all_to_all(blocks, ROWS, split_axis=0, concat_axis=0, tiled=True)  6.35 us
    pallas_call x1, Pallas kernels, attend(): pl.pallas_call(attend_kernel, grid_spec=grid_spec, out_shape=jax.ShapeDty...  3.97 us
    all_to_all x1, starting transfers between devices, gather_rows(): lax.all_to_all(copies, 'chip', split_axis=0, concat_axis=0, tiled=True)  3.35 us
    dot_general x1, matrix products, shards(): jnp.dot(hidden, enc_weight, preferred_element_type=jnp.float32)  2.98 us
    ppermute x2, waiting for transfers between devices, scatter_rows(): summed = keep + lax.ppermute(give, 'core', [(0, 1), (1, 0)])  2.53 us
  transfers between devices with their start and end apart: 5, of which 5 were waited for; matrix products, arithmetic and copies ran while one was open for 0% of the time, Pallas kernels for 0%

profile of v10, /device:TPU:0, one launch (start us, length us, event | category | flops | bytes accessed | tf_op | source)
XLA Modules:
  0.0 60.8 jit_solution(3155644155246653846)
XLA Ops:
  1.5 1.4 %reduce.2 = bf16[4096]{0:T(1024)(128)(2,1)} reduce(bf16[1,4096]{1,0:T(2,128)(2,1)} %param.11, bf16[]{:T(256)} %constant.25), dimensions={0}, to_apply=%param.11.reduce_sub_computation | reduce | bytes 16386 | tf_op args[0]
  2.8 4.0 %shard_map.122 = bf16[32,128]{1,0:T(8,128)(2,1)} custom-call(s32[1]{0:T(128)S(6)} %copy.58.len_ref, bf16[32,128]{1,0:T(8,128)(2,1)} %bitcast.56, bf16[1,384,512]{2,1,0:T(8,128)(2,1)} %k_ref.1, bf16[1,384,512]{2,1,0:T(8,128)(2,1)} %v_ref.1), custom_call_target="tpu_custom_call" | custom-call | tf_op jit(solution)/shard_map/pallas_call | solution.py:38
  6.8 7.4 %all-to-all-start = ((bf16[16,2,128]{2,1,0:T(2,128)(2,1)}), bf16[16,2,128]{2,1,0:T(2,128)(2,1)S(1)}, u32[]{:S(2)}, u32[]{:S(2)}) async-start(bf16[16,2,128]{2,1,0:T(2,128)(2,1)} %bitcast.57), calls=%async_computation | async-start | bytes 16384 | tf_op jit(solution)/shard_map/all_to_all | solution.py:100
  14.2 6.4 %all-to-all-done = bf16[16,2,128]{2,1,0:T(2,128)(2,1)S(1)} async-done(((bf16[16,2,128]{2,1,0:T(2,128)(2,1)}), bf16[16,2,128]{2,1,0:T(2,128)(2,1)S(1)}, u32[]{:S(2)}, u32[]{:S(2)}) %all-to-all-start) | async-done | bytes 8224 | tf_op jit(solution)/shard_map/all_to_all | solution.py:100
  20.6 0.4 fusion
  21.0 0.1 collective-permute-start
  21.1 1.3 %collective-permute-done = f32[8,1,4096]{2,0,1:T(8,128)S(1)} collective-permute-done((f32[8,1,4096]{2,0,1:T(8,128)S(1)}, f32[8,1,4096]{2,0,1:T(8,128)S(1)}, u32[]{:S(2)}, u32[]{:S(2)}) %collective-permute-start) | collective-permute-done | bytes 131104 | tf_op jit(solution)/shard_map/ppermute | solution.py:68
  22.4 0.1 copy.43
  22.5 9.3 %all_to_all.29 = bf16[8,2,2048]{2,1,0:T(2,128)(2,1)S(1)} all-to-all(bf16[8,2,2048]{2,1,0:T(2,128)(2,1)S(1)} %copy.43), channel_id=1, replica_groups=mesh['groups'=2,'chip'=8,'core'=2] {'chip'}, dimensions={0} | all-to-all | bytes 131072 | tf_op jit(solution)/shard_map/all_to_all | solution.py:71
  31.8 0.1 convert_reduce_fusion.1
  31.9 0.1 convert_reduce_fusion.2
  32.0 0.7 %broadcast_in_dim.27 = bf16[8,2,2048]{2,1,0:T(2,128)(2,1)} broadcast(bf16[2,2048]{1,0:T(2,128)(2,1)S(1)} %broadcast_in_dim.26), dimensions={1,2} | broadcast | bytes 73728 | tf_op jit(solution)/shard_map/broadcast_in_dim | solution.py:54
  32.6 3.3 %all-to-all-start.2 = ((bf16[8,2,2048]{2,1,0:T(2,128)(2,1)}), bf16[8,2,2048]{2,1,0:T(2,128)(2,1)S(1)}, u32[]{:S(2)}, u32[]{:S(2)}) async-start(bf16[8,2,2048]{2,1,0:T(2,128)(2,1)} %broadcast_in_dim.27), calls=%async_computation.2 | async-start | bytes 131072 | tf_op jit(solution)/shard_map/all_to_all | solution.py:55
  36.0 6.8 %all-to-all-done.2 = bf16[8,2,2048]{2,1,0:T(2,128)(2,1)S(1)} async-done(((bf16[8,2,2048]{2,1,0:T(2,128)(2,1)}), bf16[8,2,2048]{2,1,0:T(2,128)(2,1)S(1)}, u32[]{:S(2)}, u32[]{:S(2)}) %all-to-all-start.2) | async-done | bytes 65568 | tf_op jit(solution)/shard_map/all_to_all | solution.py:55
  42.9 0.1 collective-permute-start.1
  42.9 0.2 compare_reduce_fusion
  43.1 1.1 %collective-permute-done.1 = bf16[8,1,4096]{2,0,1:T(8,128)(2,1)S(1)} collective-permute-done((bf16[8,1,4096]{2,0,1:T(8,128)(2,1)S(1)}, bf16[8,1,4096]{2,0,1:T(8,128)(2,1)S(1)}, u32[]{:S(2)}, u32[]{:S(2)}) %collective-permute-start.1) | collective-permute-done | bytes 65568 | tf_op jit(solution)/shard_map/ppermute | solution.py:57
  44.2 0.1 copy.44
  44.4 0.1 reshape.149
  44.4 3.0 %fusion.4 = bf16[16,512]{1,0:T(8,128)(2,1)S(1)} fusion(bf16[16,4096]{1,0:T(8,128)(2,1)S(1)} %reshape.149, bf16[4096,512]{1,0:T(8,128)(2,1)} %param.18, f32[512]{0:T(512)S(1)} %copy-done.5, pred[512]{0:T(512)(128)(4,1)S(1)} %compare_reduce_fusion), kind=kOutput, calls=%fused_computation.5 | convolution fusion | flops 67141632 | bytes 4344320 | tf_op jit(solution)/shard_map/dot_general | solution.py:115
  47.4 0.5 copy-done.1
  47.9 0.7 %fusion.10 = f32[16,4096]{1,0:T(8,128)S(1)} fusion(bf16[16,512]{1,0:T(8,128)(2,1)S(1)} %fusion.4, bf16[512,4096]{1,0:T(8,128)(2,1)S(1)} %copy-done.1), kind=kOutput, calls=%fused_computation.25 | convolution fusion | flops 67108864 | bytes 4472832 | tf_op jit(solution)/shard_map/dot_general | solution.py:118
  48.5 0.2 reshape.150
  48.7 0.2 fusion.9
  49.0 0.2 select_bitcast_fusion
  49.1 0.2 collective-permute-start.2
  49.3 1.2 %collective-permute-done.2 = f32[8,1,4096]{2,0,1:T(8,128)S(1)} collective-permute-done((f32[8,1,4096]{2,0,1:T(8,128)S(1)}, f32[8,1,4096]{2,0,1:T(8,128)S(1)}, u32[]{:S(2)}, u32[]{:S(2)}) %collective-permute-start.2) | collective-permute-done | bytes 131104 | tf_op jit(solution)/shard_map/ppermute | solution.py:68
  50.5 0.1 fusion.5
  50.7 0.1 copy.47
  50.8 9.3 %all_to_all.30 = bf16[8,2,2048]{2,1,0:T(2,128)(2,1)S(1)} all-to-all(bf16[8,2,2048]{2,1,0:T(2,128)(2,1)S(1)} %copy.47), channel_id=1, replica_groups=mesh['groups'=2,'chip'=8,'core'=2] {'chip'}, dimensions={0} | all-to-all | bytes 131072 | tf_op jit(solution)/shard_map/all_to_all | solution.py:71
  60.0 0.1 convert_reduce_fusion
  60.1 0.6 %convert_element_type.39 = bf16[1,4096]{1,0:T(2,128)(2,1)} reshape(bf16[4096]{0:T(1024)(128)(2,1)S(1)} %add_convert_fusion) | data formatting | bytes 16384 | tf_op jit(solution)/shard_map/convert_element_type | solution.py:119
  (24 shorter events, 0.2 us)
Async XLA Ops:
  0.6 19.9 %copy-start = (bf16[256,4096]{1,0:T(8,128)(2,1)S(1)}, bf16[256,4096]{1,0:T(8,128)(2,1)}, u32[]{:S(2)}) copy-start(bf16[256,4096]{1,0:T(8,128)(2,1)} %param.16) | copy-start | bytes 6291460
  0.6 31.2 %copy-start.3 = (bf16[1,4096]{1,0:T(2,128)(2,1)S(1)}, bf16[1,4096]{1,0:T(2,128)(2,1)}, u32[]{:S(2)}) copy-start(bf16[1,4096]{1,0:T(2,128)(2,1)} %param.15) | copy-start | bytes 24580
  0.7 42.3 %copy-start.6 = (s32[256]{0:T(256)S(1)}, s32[256]{0:T(256)}, u32[]{:S(2)}) copy-start(s32[256]{0:T(256)} %param.17) | copy-start | bytes 3076
  0.7 43.8 %copy-start.5 = (f32[512]{0:T(512)S(1)}, f32[512]{0:T(512)}, u32[]{:S(2)}) copy-start(f32[512]{0:T(512)} %param.19) | copy-start | bytes 6148
  6.8 13.8 %all-to-all-start = ((bf16[16,2,128]{2,1,0:T(2,128)(2,1)}), bf16[16,2,128]{2,1,0:T(2,128)(2,1)S(1)}, u32[]{:S(2)}, u32[]{:S(2)}) async-start(bf16[16,2,128]{2,1,0:T(2,128)(2,1)} %bitcast.57), calls=%async_computation | async-start | bytes 16384 | tf_op jit(solution)/shard_map/all_to_all | solution.py:100
  21.0 1.4 %collective-permute-start = (f32[8,1,4096]{2,0,1:T(8,128)S(1)}, f32[8,1,4096]{2,0,1:T(8,128)S(1)}, u32[]{:S(2)}, u32[]{:S(2)}) collective-permute-start(f32[8,1,4096]{2,0,1:T(8,128)S(1)} %fusion.6), channel_id=1, source_target_pairs={{0,1},{1,0},{2,3},{3,2},{4,5},{5,4},{6,7},{7,6},{8,9},{9,8},{10,11... | collective-permute-start | bytes 393224 | tf_op jit(solution)/shard_map/ppermute | solution.py:68
  32.6 10.2 %all-to-all-start.2 = ((bf16[8,2,2048]{2,1,0:T(2,128)(2,1)}), bf16[8,2,2048]{2,1,0:T(2,128)(2,1)S(1)}, u32[]{:S(2)}, u32[]{:S(2)}) async-start(bf16[8,2,2048]{2,1,0:T(2,128)(2,1)} %broadcast_in_dim.27), calls=%async_computation.2 | async-start | bytes 131072 | tf_op jit(solution)/shard_map/all_to_all | solution.py:55
  42.9 1.3 %collective-permute-start.1 = (bf16[8,1,4096]{2,0,1:T(8,128)(2,1)S(1)}, bf16[8,1,4096]{2,0,1:T(8,128)(2,1)S(1)}, u32[]{:S(2)}, u32[]{:S(2)}) collective-permute-start(bf16[8,1,4096]{2,0,1:T(8,128)(2,1)S(1)} %reshape.148), channel_id=1, source_target_pairs={{0,1},{1,0},{2,3},{3,2},{4,5},{5,4},{6,7},{7,6},{8,9},{9,8},{10,11... | collective-permute-start | bytes 196616 | tf_op jit(solution)/shard_map/ppermute | solution.py:57
  44.4 3.5 %copy-start.1 = (bf16[512,4096]{1,0:T(8,128)(2,1)S(1)}, bf16[512,4096]{1,0:T(8,128)(2,1)}, u32[]{:S(2)}) copy-start(bf16[512,4096]{1,0:T(8,128)(2,1)} %param.20) | copy-start | bytes 12582916
  47.9 12.9 %copy-start.2 = (bf16[16,512]{1,0:T(8,128)(2,1)}, bf16[16,512]{1,0:T(8,128)(2,1)S(1)}, u32[]{:S(2)}) copy-start(bf16[16,512]{1,0:T(8,128)(2,1)S(1)} %fusion.4) | copy-start | bytes 49156
  47.9 12.2 %copy-start.4 = (f32[4096]{0:T(1024)S(1)}, f32[4096]{0:T(1024)}, u32[]{:S(2)}) copy-start(f32[4096]{0:T(1024)} %param.21) | copy-start | bytes 49156
  49.1 1.4 %collective-permute-start.2 = (f32[8,1,4096]{2,0,1:T(8,128)S(1)}, f32[8,1,4096]{2,0,1:T(8,128)S(1)}, u32[]{:S(2)}, u32[]{:S(2)}) collective-permute-start(f32[8,1,4096]{2,0,1:T(8,128)S(1)} %select_bitcast_fusion), channel_id=1, source_target_pairs={{0,1},{1,0},{2,3},{3,2},{4,5},{5,4},{6,7},{7,6},{8,9},{9,8},{10,11... | collective-permute-start | bytes 393224 | tf_op jit(solution)/shard_map/ppermute | solution.py:68

commit v11 on v9

--- a/solution.py
+++ b/solution.py
@@ -22,6 +22,25 @@
     first = pick((mine, mate), 0)
     second = pick((mate, mine), 0)
     return jnp.stack([first, second], axis=1).reshape(chips * 2 * x.shape[0], x.shape[1])
+
+
+def reduce_gather_rows(x, resid, chips):
+    per = x.shape[0] // (2 * chips)
+    width = x.shape[1]
+    split = x.reshape(chips, 2, per, width)
+    keep = pick((split[:, 0], split[:, 1]), 0)
+    give = pick((split[:, 1], split[:, 0]), 0)
+    summed = keep + lax.ppermute(give, "core", [(0, 1), (1, 0)])
+    payload = jnp.concatenate([summed.astype(jnp.bfloat16).reshape(chips * per, width), resid], axis=0)
+    halves = payload.reshape(2 * (chips + 1) * per, width // 2)
+    copies = jnp.broadcast_to(halves[None], (chips,) + halves.shape).reshape(chips * halves.shape[0], width // 2)
+    got = lax.all_to_all(copies, "chip", split_axis=0, concat_axis=0, tiled=True)
+    got = got.reshape(chips, chips + 1, per, width).astype(jnp.float32)
+    mine = (got[:, :chips].sum(axis=0) + got[:, chips]).astype(jnp.bfloat16)
+    mate = lax.ppermute(mine, "core", [(0, 1), (1, 0)])
+    first = pick((mine, mate), 0)
+    second = pick((mate, mine), 0)
+    return jnp.stack([first, second], axis=1).reshape(chips * 2 * per, width)
 
 
 def scatter_rows(x, chips, narrow=False):
@@ -82,8 +101,11 @@
         attended = attended.reshape(rows_here, heads * HEAD_DIM)
         features = lax.all_to_all(attended, ROWS, split_axis=1, concat_axis=0, tiled=True)
     partial_value = jnp.dot(features, out_weight, preferred_element_type=jnp.float32)
-    hidden_here = (scatter_rows(partial_value, chips, narrow=True) + resid.astype(jnp.float32)).astype(jnp.bfloat16)
-    hidden = gather_rows(hidden_here, chips)
+    if chips <= 8:
+        hidden = reduce_gather_rows(partial_value, resid, chips)
+    else:
+        hidden_here = (scatter_rows(partial_value, chips, narrow=True) + resid.astype(jnp.float32)).astype(jnp.bfloat16)
+        hidden = gather_rows(hidden_here, chips)
     lat_here = enc_weight.shape[1]
     latent_ids = lax.axis_index(ROWS) * lat_here + lax.broadcasted_iota(jnp.int32, (lat_here,), 0)
     listed = jnp.any(chat_ids[:, None] == latent_ids[None, :], axis=0)

time: 60.4 us -> 66.9 us (1.11)
  waiting for transfers between devices: 16.8 us -> 30.6 us
  blocking collectives: 18.6 us -> 10.3 us
    all_to_all x1, waiting for transfers between devices: 6.82 us -> 20.6 us  [reduce_gather_rows(): lax.all_to_all(copies, 'chip', split_axis=0, concat_axis=0, tiled=True)]
    all_to_all x2 -> x1, blocking collectives: 18.6 us -> 10.3 us  [scatter_rows(): got = lax.all_to_all(sent, 'chip', split_axis=0, concat_axis=0, tiled=True)]
    ppermute x2 -> x1, waiting for transfers between devices: 2.53 us -> 1.19 us  [scatter_rows(): summed = keep + lax.ppermute(give, 'core', [(0, 1), (1, 0)])]
    ppermute x1 -> x2, waiting for transfers between devices: 1.08 us -> 2.41 us  [the longest x1 1.33 us: reduce_gather_rows(): summed = keep + lax.ppermute(give, 'core', [(0, 1), (1, 0)])]
where the time goes in v11:
time: 66.9 us; the launch traced here: 66.5 us
  waiting for transfers between devices  30.6 us (46%)
  starting transfers between devices  11.3 us (17%)
  blocking collectives  10.3 us (15%)
  matrix products  6.59 us (10%)
  local copies, waits for them, and re-layouts  3.16 us (5%)
  other arithmetic  2.86 us (4%)
  between operations  1.71 us (3%)
    all_to_all x1, waiting for transfers between devices, reduce_gather_rows(): lax.all_to_all(copies, 'chip', split_axis=0, concat_axis=0, tiled=True)  20.6 us
    all_to_all x1, blocking collectives, scatter_rows(): got = lax.all_to_all(sent, 'chip', split_axis=0, concat_axis=0, tiled=True)  10.3 us
    all_to_all x1, starting transfers between devices, shards(): got = lax.all_to_all(blocks, ROWS, split_axis=0, concat_axis=0, tiled=True)  7.39 us
    all_to_all x1, waiting for transfers between devices, shards(): got = lax.all_to_all(blocks, ROWS, split_axis=0, concat_axis=0, tiled=True)  6.35 us
    all_to_all x1, starting transfers between devices, reduce_gather_rows(): lax.all_to_all(copies, 'chip', split_axis=0, concat_axis=0, tiled=True)  3.55 us
    dot_general x1, matrix products, shards(): jnp.dot(hidden, enc_weight, preferred_element_type=jnp.float32)  2.98 us
    dot_general x1, matrix products, shards(): jnp.einsum('rhc,rsc->rhs', spread, keys, preferred_element_type=jnp.float32)  1.36 us
  transfers between devices with their start and end apart: 5, of which 5 were waited for; matrix products, arithmetic and copies ran while one was open for 0% of the time, Pallas kernels for 0%

profile of v11, /device:TPU:0, one launch (start us, length us, event | category | flops | bytes accessed | tf_op | source)
XLA Modules:
  0.0 66.5 jit_solution(14821766042399233981)
XLA Ops:
  1.5 0.8 %reduce.7 = bf16[4096]{0:T(1024)(128)(2,1)S(1)} reduce(bf16[1,4096]{1,0:T(2,128)(2,1)} %param.11, bf16[]{:T(256)} %constant.49), dimensions={0}, to_apply=%param.11.reduce_sub_computation | reduce | bytes 16386 | tf_op args[0]
  2.3 0.1 fusion.21
  2.3 0.1 broadcast_multiply_fusion
  2.4 1.4 %fusion.23 = (f32[32]{0:T(128)S(1)}, f32[32,384]{1,0:T(8,128)S(1)}) fusion(bf16[1,384,512]{2,1,0:T(8,128)(2,1)} %param.12, bf16[4,8,4,128]{3,2,1,0:T(4,128)(2,1)S(1)} %bitcast.82, pred[384]{0:T(512)(128)(4,1)S(1)} %iota_compare_fusion.1), kind=kOutput, calls=%fused_computation.52 | convolution fusion | flops 12619744 | bytes 475648 | tf_op jit(solution)/shard_map/rhc,rsc->rhs/dot_general | solution.py:84
  3.8 0.2 fusion.14
  4.0 1.2 %convolution_bitcast_fusion = f32[1,32,512]{2,1,0:T(8,128)S(1)} fusion(bf16[1,384,512]{2,1,0:T(8,128)(2,1)} %param.13, f32[32,384]{1,0:T(8,128)S(1)} %get-tuple-element.9, f32[32]{0:T(128)S(1)} %fusion.14, f32[32]{0:T(128)S(1)} %get-tuple-element.8), kind=kOutput, calls=%fused_computation.2 | convolution fusion | flops 12619776 | bytes 508160 | tf_op jit(solution)/shard_map/rhs,rsc->rhc/dot_general | solution.py:92
  5.3 0.7 %multiply_reduce_fusion = bf16[32,128]{1,0:T(8,128)(2,1)} fusion(f32[1,32,4,128]{3,2,1,0:T(4,128)S(1)} %reshape.347, f32[32,4]{1,0:T(8,128)S(1)} %get-tuple-element.6), kind=kLoop, calls=%fused_computation.30 | loop fusion | flops 28672 | bytes 74240 | tf_op jit(solution)/shard_map/reduce_sum | solution.py:94
  6.0 7.4 %all-to-all-start = ((bf16[16,2,128]{2,1,0:T(2,128)(2,1)}), bf16[16,2,128]{2,1,0:T(2,128)(2,1)S(1)}, u32[]{:S(2)}, u32[]{:S(2)}) async-start(bf16[16,2,128]{2,1,0:T(2,128)(2,1)} %bitcast.4), calls=%async_computation | async-start | bytes 16384 | tf_op jit(solution)/shard_map/all_to_all | solution.py:98
  13.4 6.4 %all-to-all-done = bf16[16,2,128]{2,1,0:T(2,128)(2,1)S(1)} async-done(((bf16[16,2,128]{2,1,0:T(2,128)(2,1)}), bf16[16,2,128]{2,1,0:T(2,128)(2,1)S(1)}, u32[]{:S(2)}, u32[]{:S(2)}) %all-to-all-start) | async-done | bytes 8224 | tf_op jit(solution)/shard_map/all_to_all | solution.py:98
  19.8 0.4 fusion
  20.2 0.1 collective-permute-start
  20.3 1.3 %collective-permute-done = f32[8,1,4096]{2,0,1:T(8,128)S(1)} collective-permute-done((f32[8,1,4096]{2,0,1:T(8,128)S(1)}, f32[8,1,4096]{2,0,1:T(8,128)S(1)}, u32[]{:S(2)}, u32[]{:S(2)}) %collective-permute-start) | collective-permute-done | bytes 131104 | tf_op jit(solution)/shard_map/ppermute | solution.py:33
  21.7 1.0 %broadcast_in_dim.47 = bf16[8,18,2048]{2,1,0:T(8,128)(2,1)} broadcast(bf16[18,2048]{1,0:T(8,128)(2,1)S(1)} %broadcast_in_dim.46), dimensions={1,2} | broadcast | bytes 663552 | tf_op jit(solution)/shard_map/broadcast_in_dim | solution.py:36
  22.7 3.5 %all-to-all-start.1 = ((bf16[8,18,2048]{2,1,0:T(8,128)(2,1)}), bf16[8,18,2048]{2,1,0:T(8,128)(2,1)S(1)}, u32[]{:S(2)}, u32[]{:S(2)}) async-start(bf16[8,18,2048]{2,1,0:T(8,128)(2,1)} %broadcast_in_dim.47), calls=%async_computation.1 | async-start | bytes 1572864 | tf_op jit(solution)/shard_map/all_to_all | solution.py:37
  26.2 20.6 %all-to-all-done.1 = bf16[8,18,2048]{2,1,0:T(8,128)(2,1)S(1)} async-done(((bf16[8,18,2048]{2,1,0:T(8,128)(2,1)}), bf16[8,18,2048]{2,1,0:T(8,128)(2,1)S(1)}, u32[]{:S(2)}, u32[]{:S(2)}) %all-to-all-start.1) | async-done | bytes 589856 | tf_op jit(solution)/shard_map/all_to_all | solution.py:37
  46.9 0.3 copy.43
  47.2 0.1 convert.1
  47.3 0.3 slice_reduce_fusion
  47.7 0.2 compare_reduce_fusion
  47.8 1.1 %collective-permute-done.1 = bf16[8,1,4096]{2,0,1:T(8,128)(2,1)S(1)} collective-permute-done((bf16[8,1,4096]{2,0,1:T(8,128)(2,1)S(1)}, bf16[8,1,4096]{2,0,1:T(8,128)(2,1)S(1)}, u32[]{:S(2)}, u32[]{:S(2)}) %collective-permute-start.1) | collective-permute-done | bytes 65568 | tf_op jit(solution)/shard_map/ppermute | solution.py:40
  49.0 0.1 copy.44
  49.2 3.0 %fusion.5 = bf16[16,512]{1,0:T(8,128)(2,1)S(1)} fusion(bf16[16,4096]{1,0:T(8,128)(2,1)S(1)} %reshape.349, bf16[4096,512]{1,0:T(8,128)(2,1)} %param.18, f32[512]{0:T(512)S(1)} %copy-done.5, pred[512]{0:T(512)(128)(4,1)S(1)} %compare_reduce_fusion), kind=kOutput, calls=%fused_computation.8 | convolution fusion | flops 67141632 | bytes 4344320 | tf_op jit(solution)/shard_map/dot_general | solution.py:116
  52.2 0.5 copy-done.1
  52.6 0.7 fusion.24
  53.3 0.2 reshape.350
  53.5 0.2 fusion.22
  53.7 0.2 select_bitcast_fusion
  53.9 0.2 collective-permute-start.2
  54.1 1.2 %collective-permute-done.2 = f32[8,1,4096]{2,0,1:T(8,128)S(1)} collective-permute-done((f32[8,1,4096]{2,0,1:T(8,128)S(1)}, f32[8,1,4096]{2,0,1:T(8,128)S(1)}, u32[]{:S(2)}, u32[]{:S(2)}) %collective-permute-start.2) | collective-permute-done | bytes 131104 | tf_op jit(solution)/shard_map/ppermute | solution.py:51
  55.3 0.1 fusion.10
  55.5 10.3 %all_to_all.20 = bf16[8,2,2048]{2,1,0:T(2,128)(2,1)S(1)} all-to-all(bf16[8,2,2048]{2,1,0:T(2,128)(2,1)S(1)} %copy.47), channel_id=1, replica_groups=mesh['groups'=2,'chip'=8,'core'=2] {'chip'}, dimensions={0} | all-to-all | bytes 131072 | tf_op jit(solution)/shard_map/all_to_all | solution.py:54
  65.9 0.6 convert_element_type.90
  (32 shorter events, 0.5 us)
Async XLA Ops:
  0.6 19.1 %copy-start = (bf16[256,4096]{1,0:T(8,128)(2,1)S(1)}, bf16[256,4096]{1,0:T(8,128)(2,1)}, u32[]{:S(2)}) copy-start(bf16[256,4096]{1,0:T(8,128)(2,1)} %param.16) | copy-start | bytes 6291460
  0.6 21.0 %copy-start.4 = (bf16[1,4096]{1,0:T(2,128)(2,1)S(1)}, bf16[1,4096]{1,0:T(2,128)(2,1)}, u32[]{:S(2)}) copy-start(bf16[1,4096]{1,0:T(2,128)(2,1)} %param.15) | copy-start | bytes 24580
  6.0 13.8 %all-to-all-start = ((bf16[16,2,128]{2,1,0:T(2,128)(2,1)}), bf16[16,2,128]{2,1,0:T(2,128)(2,1)S(1)}, u32[]{:S(2)}, u32[]{:S(2)}) async-start(bf16[16,2,128]{2,1,0:T(2,128)(2,1)} %bitcast.4), calls=%async_computation | async-start | bytes 16384 | tf_op jit(solution)/shard_map/all_to_all | solution.py:98
  20.1 27.5 %copy-start.6 = (s32[256]{0:T(256)S(1)}, s32[256]{0:T(256)}, u32[]{:S(2)}) copy-start(s32[256]{0:T(256)} %param.17) | copy-start | bytes 3076
  20.2 1.4 %collective-permute-start = (f32[8,1,4096]{2,0,1:T(8,128)S(1)}, f32[8,1,4096]{2,0,1:T(8,128)S(1)}, u32[]{:S(2)}, u32[]{:S(2)}) collective-permute-start(f32[8,1,4096]{2,0,1:T(8,128)S(1)} %fusion.11), channel_id=1, source_target_pairs={{0,1},{1,0},{2,3},{3,2},{4,5},{5,4},{6,7},{7,6},{8,9},{9,8},{10,11... | collective-permute-start | bytes 393224 | tf_op jit(solution)/shard_map/ppermute | solution.py:33
  21.7 27.5 %copy-start.5 = (f32[512]{0:T(512)S(1)}, f32[512]{0:T(512)}, u32[]{:S(2)}) copy-start(f32[512]{0:T(512)} %param.19) | copy-start | bytes 6148
  22.7 24.2 %all-to-all-start.1 = ((bf16[8,18,2048]{2,1,0:T(8,128)(2,1)}), bf16[8,18,2048]{2,1,0:T(8,128)(2,1)S(1)}, u32[]{:S(2)}, u32[]{:S(2)}) async-start(bf16[8,18,2048]{2,1,0:T(8,128)(2,1)} %broadcast_in_dim.47), calls=%async_computation.1 | async-start | bytes 1572864 | tf_op jit(solution)/shard_map/all_to_all | solution.py:37
  47.6 1.3 %collective-permute-start.1 = (bf16[8,1,4096]{2,0,1:T(8,128)(2,1)S(1)}, bf16[8,1,4096]{2,0,1:T(8,128)(2,1)S(1)}, u32[]{:S(2)}, u32[]{:S(2)}) collective-permute-start(bf16[8,1,4096]{2,0,1:T(8,128)(2,1)S(1)} %fusion.9), channel_id=1, source_target_pairs={{0,1},{1,0},{2,3},{3,2},{4,5},{5,4},{6,7},{7,6},{8,9},{9,8},{10,11... | collective-permute-start | bytes 196616 | tf_op jit(solution)/shard_map/ppermute | solution.py:40
  49.2 3.5 %copy-start.1 = (bf16[512,4096]{1,0:T(8,128)(2,1)S(1)}, bf16[512,4096]{1,0:T(8,128)(2,1)}, u32[]{:S(2)}) copy-start(bf16[512,4096]{1,0:T(8,128)(2,1)} %param.20) | copy-start | bytes 12582916
  52.6 13.9 %copy-start.2 = (bf16[16,512]{1,0:T(8,128)(2,1)}, bf16[16,512]{1,0:T(8,128)(2,1)S(1)}, u32[]{:S(2)}) copy-start(bf16[16,512]{1,0:T(8,128)(2,1)S(1)} %fusion.5) | copy-start | bytes 49156
  52.6 13.3 %copy-start.3 = (f32[4096]{0:T(1024)S(1)}, f32[4096]{0:T(1024)}, u32[]{:S(2)}) copy-start(f32[4096]{0:T(1024)} %param.21) | copy-start | bytes 49156
  53.9 1.4 %collective-permute-start.2 = (f32[8,1,4096]{2,0,1:T(8,128)S(1)}, f32[8,1,4096]{2,0,1:T(8,128)S(1)}, u32[]{:S(2)}, u32[]{:S(2)}) collective-permute-start(f32[8,1,4096]{2,0,1:T(8,128)S(1)} %select_bitcast_fusion), channel_id=1, source_target_pairs={{0,1},{1,0},{2,3},{3,2},{4,5},{5,4},{6,7},{7,6},{8,9},{9,8},{10,11... | collective-permute-start | bytes 393224 | tf_op jit(solution)/shard_map/ppermute | solution.py:51

commit v12 on v7

--- a/solution.py
+++ b/solution.py
@@ -24,14 +24,19 @@
     return jnp.stack([first, second], axis=1).reshape(chips * 2 * x.shape[0], x.shape[1])
 
 
-def scatter_rows(x, chips):
-    per = x.shape[0] // (2 * chips)
-    split = x.reshape(chips, 2, per, x.shape[1])
-    keep = pick((split[:, 0], split[:, 1]), 0)
-    give = pick((split[:, 1], split[:, 0]), 0)
-    summed = keep + lax.ppermute(give, "core", [(0, 1), (1, 0)])
-    got = lax.all_to_all(summed.reshape(chips * per, x.shape[1]), "chip", split_axis=0, concat_axis=0, tiled=True)
-    return got.reshape(chips, per, x.shape[1]).sum(axis=0)
+def scatter_rows(lhs, weight, chips):
+    per = lhs.shape[0] // (2 * chips)
+    split = lhs.reshape(chips, 2, per, lhs.shape[1])
+    keep = pick((split[:, 0], split[:, 1]), 0).reshape(chips * per, lhs.shape[1])
+    give = pick((split[:, 1], split[:, 0]), 0).reshape(chips * per, lhs.shape[1])
+    sent_over = lax.ppermute(
+        jnp.dot(give, weight, preferred_element_type=jnp.float32), "core", [(0, 1), (1, 0)]
+    )
+    summed = lax.optimization_barrier(jnp.dot(keep, weight, preferred_element_type=jnp.float32)) + sent_over
+    width = weight.shape[1]
+    sent = summed.astype(jnp.bfloat16).reshape(chips * per * 2, width // 2)
+    got = lax.all_to_all(sent, "chip", split_axis=0, concat_axis=0, tiled=True)
+    return got.astype(jnp.float32).reshape(chips, per, width).sum(axis=0)
 
 
 def shards(
@@ -77,8 +82,7 @@
     else:
         attended = attended.reshape(rows_here, heads * HEAD_DIM)
         features = lax.all_to_all(attended, ROWS, split_axis=1, concat_axis=0, tiled=True)
-    partial_value = jnp.dot(features, out_weight, preferred_element_type=jnp.float32)
-    hidden_here = (scatter_rows(partial_value, chips) + resid.astype(jnp.float32)).astype(jnp.bfloat16)
+    hidden_here = (scatter_rows(features, out_weight, chips) + resid.astype(jnp.float32)).astype(jnp.bfloat16)
     hidden = gather_rows(hidden_here, chips)
     lat_here = enc_weight.shape[1]
     latent_ids = lax.axis_index(ROWS) * lat_here + lax.broadcasted_iota(jnp.int32, (lat_here,), 0)
@@ -90,7 +94,7 @@
             jnp.dot(hidden, enc_weight, preferred_element_type=jnp.float32) + enc_bias[None, :]
         ),
     ).astype(jnp.bfloat16)
-    rebuilt = scatter_rows(jnp.dot(activity, dec_weight, preferred_element_type=jnp.float32), chips)
+    rebuilt = scatter_rows(activity, dec_weight, chips)
     spliced = (rebuilt + dec_bias[None, :]).astype(jnp.bfloat16)
     return (spliced, activity)
 

time: 62 us -> 61.4 us (level)
  matrix products: 6.59 us -> 9.81 us
  waiting for transfers between devices: 16.8 us -> 15.5 us
  blocking collectives: 19.9 us -> 18.6 us
  local copies, waits for them, and re-layouts: 2.73 us -> 2.05 us
    dot_general x2 -> x4, matrix products: 1.04 us -> 4.41 us  [the longest x2 3.37 us: scatter_rows(): jnp.dot(give, weight, preferred_element_type=jnp.float32)]
    all_to_all x2, blocking collectives: 19.9 us -> 18.6 us  [scatter_rows(): got = lax.all_to_all(sent, 'chip', split_axis=0, concat_axis=0, tiled=True)]
    ppermute x2, waiting for transfers between devices: 2.53 us -> 1.27 us  [scatter_rows(): lax.ppermute(jnp.dot(give, weight, preferred_element_type=jnp.float32), '...]
  transfers between devices with their start and end apart: 5 -> 5, of which waited for: 5 -> 5; matrix products, arithmetic and copies ran while one was open for 0% -> 2% of each run, Pallas kernels for 0% -> 0%
where the time goes in v12:
time: 61.4 us; the launch traced here: 60.9 us
  blocking collectives  18.6 us (30%)
  waiting for transfers between devices  15.5 us (25%)
  starting transfers between devices  11 us (18%)
  matrix products  9.81 us (16%)
  other arithmetic  2.32 us (4%)
  local copies, waits for them, and re-layouts  2.05 us (3%)
  between operations  1.69 us (3%)
    all_to_all x2, blocking collectives, scatter_rows(): got = lax.all_to_all(sent, 'chip', split_axis=0, concat_axis=0, tiled=True)  18.6 us
    all_to_all x1, starting transfers between devices, shards(): got = lax.all_to_all(blocks, ROWS, split_axis=0, concat_axis=0, tiled=True)  7.39 us
    all_to_all x1, waiting for transfers between devices, gather_rows(): lax.all_to_all(copies, 'chip', split_axis=0, concat_axis=0, tiled=True)  6.82 us
    all_to_all x1, waiting for transfers between devices, shards(): got = lax.all_to_all(blocks, ROWS, split_axis=0, concat_axis=0, tiled=True)  6.35 us
    dot_general x2, matrix products, scatter_rows(): jnp.dot(give, weight, preferred_element_type=jnp.float32)  3.37 us
    all_to_all x1, starting transfers between devices, gather_rows(): lax.all_to_all(copies, 'chip', split_axis=0, concat_axis=0, tiled=True)  3.35 us
    dot_general x1, matrix products, shards(): jnp.dot(hidden, enc_weight, preferred_element_type=jnp.float32)  2.83 us
    dot_general x1, matrix products, shards(): jnp.einsum('rhc,rsc->rhs', spread, keys, preferred_element_type=jnp.float32)  1.36 us
  transfers between devices with their start and end apart: 5, of which 5 were waited for; matrix products, arithmetic and copies ran while one was open for 2% of the time, Pallas kernels for 0%

profile of v12, /device:TPU:0, one launch (start us, length us, event | category | flops | bytes accessed | tf_op | source)
XLA Modules:
  0.0 60.9 jit_solution(15956828903616810211)
XLA Ops:
  1.5 0.8 %reduce.7 = bf16[4096]{0:T(1024)(128)(2,1)S(1)} reduce(bf16[1,4096]{1,0:T(2,128)(2,1)} %param.11, bf16[]{:T(256)} %constant.49), dimensions={0}, to_apply=%param.11.reduce_sub_computation | reduce | bytes 16386 | tf_op args[0]
  2.3 0.1 fusion.30
  2.4 0.1 broadcast_multiply_fusion
  2.5 1.4 %fusion.32 = (f32[32]{0:T(128)S(1)}, f32[32,384]{1,0:T(8,128)S(1)}) fusion(bf16[1,384,512]{2,1,0:T(8,128)(2,1)} %param.12, bf16[4,8,4,128]{3,2,1,0:T(4,128)(2,1)S(1)} %bitcast.53, pred[384]{0:T(512)(128)(4,1)S(1)} %iota_compare_fusion.1), kind=kOutput, calls=%fused_computation.59 | convolution fusion | flops 12619744 | bytes 475648 | tf_op jit(solution)/shard_map/rhc,rsc->rhs/dot_general | solution.py:66
  3.8 0.2 fusion.6
  4.0 1.2 %convolution_bitcast_fusion = f32[1,32,512]{2,1,0:T(8,128)S(1)} fusion(bf16[1,384,512]{2,1,0:T(8,128)(2,1)} %param.13, f32[32,384]{1,0:T(8,128)S(1)} %get-tuple-element.11, f32[32]{0:T(128)S(1)} %fusion.6, f32[32]{0:T(128)S(1)} %get-tuple-element.10), kind=kOutput, calls=%fused_computation | convolution fusion | flops 12619776 | bytes 508160 | tf_op jit(solution)/shard_map/rhs,rsc->rhc/dot_general | solution.py:74
  5.3 0.7 %multiply_reduce_fusion = bf16[32,128]{1,0:T(8,128)(2,1)} fusion(f32[1,32,4,128]{3,2,1,0:T(4,128)S(1)} %reshape.262, f32[32,4]{1,0:T(8,128)S(1)} %get-tuple-element.8), kind=kLoop, calls=%fused_computation.17 | loop fusion | flops 28672 | bytes 74240 | tf_op jit(solution)/shard_map/reduce_sum | solution.py:76
  6.0 7.4 %all-to-all-start = ((bf16[16,2,128]{2,1,0:T(2,128)(2,1)}), bf16[16,2,128]{2,1,0:T(2,128)(2,1)S(1)}, u32[]{:S(2)}, u32[]{:S(2)}) async-start(bf16[16,2,128]{2,1,0:T(2,128)(2,1)} %bitcast.4), calls=%async_computation | async-start | bytes 16384 | tf_op jit(solution)/shard_map/all_to_all | solution.py:80
  13.4 6.4 %all-to-all-done = bf16[16,2,128]{2,1,0:T(2,128)(2,1)S(1)} async-done(((bf16[16,2,128]{2,1,0:T(2,128)(2,1)}), bf16[16,2,128]{2,1,0:T(2,128)(2,1)S(1)}, u32[]{:S(2)}, u32[]{:S(2)}) %all-to-all-start) | async-done | bytes 8224 | tf_op jit(solution)/shard_map/all_to_all | solution.py:80
  19.8 0.4 fusion.20
  20.2 0.4 fusion.23
  20.6 1.0 %collective-permute-done = f32[8,4096]{1,0:T(8,128)S(1)} collective-permute-done((f32[8,4096]{1,0:T(8,128)S(1)}, f32[8,4096]{1,0:T(8,128)S(1)}, u32[]{:S(2)}, u32[]{:S(2)}) %collective-permute-start) | collective-permute-done | bytes 131104 | tf_op jit(solution)/shard_map/ppermute | solution.py:32
  21.6 0.1 copy.24
  21.6 9.3 %all_to_all.29 = bf16[8,2,2048]{2,1,0:T(2,128)(2,1)S(1)} all-to-all(bf16[8,2,2048]{2,1,0:T(2,128)(2,1)S(1)} %copy.24), channel_id=1, replica_groups=mesh['groups'=2,'chip'=8,'core'=2] {'chip'}, dimensions={0} | all-to-all | bytes 131072 | tf_op jit(solution)/shard_map/all_to_all | solution.py:38
  30.9 0.1 convert_reduce_fusion.1
  31.1 0.7 %broadcast_in_dim.47 = bf16[8,2,2048]{2,1,0:T(2,128)(2,1)} broadcast(bf16[2,2048]{1,0:T(2,128)(2,1)S(1)} %broadcast_in_dim.46), dimensions={1,2} | broadcast | bytes 73728 | tf_op jit(solution)/shard_map/broadcast_in_dim | solution.py:18
  31.8 3.3 %all-to-all-start.2 = ((bf16[8,2,2048]{2,1,0:T(2,128)(2,1)}), bf16[8,2,2048]{2,1,0:T(2,128)(2,1)S(1)}, u32[]{:S(2)}, u32[]{:S(2)}) async-start(bf16[8,2,2048]{2,1,0:T(2,128)(2,1)} %broadcast_in_dim.47), calls=%async_computation.2 | async-start | bytes 131072 | tf_op jit(solution)/shard_map/all_to_all | solution.py:19
  35.1 6.8 %all-to-all-done.2 = bf16[8,2,2048]{2,1,0:T(2,128)(2,1)S(1)} async-done(((bf16[8,2,2048]{2,1,0:T(2,128)(2,1)}), bf16[8,2,2048]{2,1,0:T(2,128)(2,1)S(1)}, u32[]{:S(2)}, u32[]{:S(2)}) %all-to-all-start.2) | async-done | bytes 65568 | tf_op jit(solution)/shard_map/all_to_all | solution.py:19
  42.0 0.1 collective-permute-start.1
  42.1 0.2 compare_reduce_fusion
  42.2 1.1 %collective-permute-done.1 = bf16[8,1,4096]{2,0,1:T(8,128)(2,1)S(1)} collective-permute-done((bf16[8,1,4096]{2,0,1:T(8,128)(2,1)S(1)}, bf16[8,1,4096]{2,0,1:T(8,128)(2,1)S(1)}, u32[]{:S(2)}, u32[]{:S(2)}) %collective-permute-start.1) | collective-permute-done | bytes 65568 | tf_op jit(solution)/shard_map/ppermute | solution.py:21
  43.4 0.1 copy.25
  43.6 2.8 %fusion.3 = bf16[16,512]{1,0:T(8,128)(2,1)S(1)} fusion(bf16[16,4096]{1,0:T(8,128)(2,1)S(1)} %reshape.264, bf16[4096,512]{1,0:T(8,128)(2,1)} %param.18, f32[512]{0:T(512)S(1)} %copy-done.5, pred[512]{0:T(512)(128)(4,1)S(1)} %compare_reduce_fusion), kind=kOutput, calls=%fused_computation.6 | convolution fusion | flops 67141632 | bytes 4344320 | tf_op jit(solution)/shard_map/dot_general | solution.py:94
  46.5 3.0 %fusion.12 = f32[8,4096]{1,0:T(8,128)S(1)} fusion(bf16[512,4096]{1,0:T(8,128)(2,1)} %param.20, pred[]{:T(512)S(6)} %eq.33, bf16[8,1,1,512]{3,1,0,2:T(2,128)(2,1)S(1)} %get-tuple-element.5, bf16[8,1,1,512]{3,1,0,2:T(2,128)(2,1)S(1)} %get-tuple-element.4), kind=kOutput, calls=%fused_computation.32 | convolution fusion | flops 33558528 | bytes 4341761 | tf_op jit(solution)/shard_map/dot_general | solution.py:33
  49.5 0.2 collective-permute-start.2
  49.7 0.2 copy-done.1
  49.9 0.6 %fusion.14 = f32[8,4096]{1,0:T(8,128)S(1)} fusion(bf16[512,4096]{1,0:T(8,128)(2,1)S(1)} %copy-done.1, pred[]{:T(512)S(6)} %eq.33, bf16[8,1,1,512]{3,1,0,2:T(2,128)(2,1)S(1)} %get-tuple-element.5, bf16[8,1,1,512]{3,1,0,2:T(2,128)(2,1)S(1)} %get-tuple-element.4), kind=kOutput, calls=%fused_computation.34 | convolution fusion | flops 33558528 | bytes 4341761 | tf_op jit(solution)/shard_map/dot_general | solution.py:35
  50.6 0.3 collective-permute-done.2
  50.9 0.1 copy.28
  50.9 9.3 %all_to_all.30 = bf16[8,2,2048]{2,1,0:T(2,128)(2,1)S(1)} all-to-all(bf16[8,2,2048]{2,1,0:T(2,128)(2,1)S(1)} %copy.28), channel_id=1, replica_groups=mesh['groups'=2,'chip'=8,'core'=2] {'chip'}, dimensions={0} | all-to-all | bytes 131072 | tf_op jit(solution)/shard_map/all_to_all | solution.py:38
  60.2 0.1 convert_reduce_fusion
  60.3 0.6 %convert_element_type.76 = bf16[1,4096]{1,0:T(2,128)(2,1)} reshape(bf16[4096]{0:T(1024)(128)(2,1)S(1)} %add_convert_fusion.2) | data formatting | bytes 16384 | tf_op jit(solution)/shard_map/convert_element_type | solution.py:98
  (34 shorter events, 0.4 us)
Async XLA Ops:
  0.6 19.2 %copy-start = (bf16[256,4096]{1,0:T(8,128)(2,1)S(1)}, bf16[256,4096]{1,0:T(8,128)(2,1)}, u32[]{:S(2)}) copy-start(bf16[256,4096]{1,0:T(8,128)(2,1)} %param.16) | copy-start | bytes 6291460
  0.6 30.4 %copy-start.3 = (bf16[1,4096]{1,0:T(2,128)(2,1)S(1)}, bf16[1,4096]{1,0:T(2,128)(2,1)}, u32[]{:S(2)}) copy-start(bf16[1,4096]{1,0:T(2,128)(2,1)} %param.15) | copy-start | bytes 24580
  0.7 41.4 %copy-start.6 = (s32[256]{0:T(256)S(1)}, s32[256]{0:T(256)}, u32[]{:S(2)}) copy-start(s32[256]{0:T(256)} %param.17) | copy-start | bytes 3076
  0.7 42.9 %copy-start.5 = (f32[512]{0:T(512)S(1)}, f32[512]{0:T(512)}, u32[]{:S(2)}) copy-start(f32[512]{0:T(512)} %param.19) | copy-start | bytes 6148
  6.0 13.8 %all-to-all-start = ((bf16[16,2,128]{2,1,0:T(2,128)(2,1)}), bf16[16,2,128]{2,1,0:T(2,128)(2,1)S(1)}, u32[]{:S(2)}, u32[]{:S(2)}) async-start(bf16[16,2,128]{2,1,0:T(2,128)(2,1)} %bitcast.4), calls=%async_computation | async-start | bytes 16384 | tf_op jit(solution)/shard_map/all_to_all | solution.py:80
  20.2 1.4 %collective-permute-start = (f32[8,4096]{1,0:T(8,128)S(1)}, f32[8,4096]{1,0:T(8,128)S(1)}, u32[]{:S(2)}, u32[]{:S(2)}) collective-permute-start(f32[8,4096]{1,0:T(8,128)S(1)} %fusion.20), channel_id=1, source_target_pairs={{0,1},{1,0},{2,3},{3,2},{4,5},{5,4},{6,7},{7,6},{8,9},{9,8},{10,11... | collective-permute-start | bytes 393224 | tf_op jit(solution)/shard_map/ppermute | solution.py:32
  31.8 10.2 %all-to-all-start.2 = ((bf16[8,2,2048]{2,1,0:T(2,128)(2,1)}), bf16[8,2,2048]{2,1,0:T(2,128)(2,1)S(1)}, u32[]{:S(2)}, u32[]{:S(2)}) async-start(bf16[8,2,2048]{2,1,0:T(2,128)(2,1)} %broadcast_in_dim.47), calls=%async_computation.2 | async-start | bytes 131072 | tf_op jit(solution)/shard_map/all_to_all | solution.py:19
  42.0 1.3 %collective-permute-start.1 = (bf16[8,1,4096]{2,0,1:T(8,128)(2,1)S(1)}, bf16[8,1,4096]{2,0,1:T(8,128)(2,1)S(1)}, u32[]{:S(2)}, u32[]{:S(2)}) collective-permute-start(bf16[8,1,4096]{2,0,1:T(8,128)(2,1)S(1)} %reshape.263), channel_id=1, source_target_pairs={{0,1},{1,0},{2,3},{3,2},{4,5},{5,4},{6,7},{7,6},{8,9},{9,8},{10,11... | collective-permute-start | bytes 196616 | tf_op jit(solution)/shard_map/ppermute | solution.py:21
  46.4 4.1 %copy-start.2 = (bf16[16,512]{1,0:T(8,128)(2,1)}, bf16[16,512]{1,0:T(8,128)(2,1)S(1)}, u32[]{:S(2)}) copy-start(bf16[16,512]{1,0:T(8,128)(2,1)S(1)} %fusion.3) | copy-start | bytes 49156
  46.4 3.5 %copy-start.1 = (bf16[512,4096]{1,0:T(8,128)(2,1)S(1)}, bf16[512,4096]{1,0:T(8,128)(2,1)}, u32[]{:S(2)}) copy-start(bf16[512,4096]{1,0:T(8,128)(2,1)} %param.20) | copy-start | bytes 12582916
  46.5 13.8 %copy-start.4 = (f32[4096]{0:T(1024)S(1)}, f32[4096]{0:T(1024)}, u32[]{:S(2)}) copy-start(f32[4096]{0:T(1024)} %param.21) | copy-start | bytes 49156
  49.5 1.4 %collective-permute-start.2 = (f32[8,4096]{1,0:T(8,128)S(1)}, f32[8,4096]{1,0:T(8,128)S(1)}, u32[]{:S(2)}, u32[]{:S(2)}) collective-permute-start(f32[8,4096]{1,0:T(8,128)S(1)} %fusion.12), channel_id=1, source_target_pairs={{0,1},{1,0},{2,3},{3,2},{4,5},{5,4},{6,7},{7,6},{8,9},{9,8},{10,11... | collective-permute-start | bytes 393224 | tf_op jit(solution)/shard_map/ppermute | solution.py:32

commit v13 on v9

--- a/solution.py
+++ b/solution.py
@@ -22,6 +22,13 @@
     first = pick((mine, mate), 0)
     second = pick((mate, mine), 0)
     return jnp.stack([first, second], axis=1).reshape(chips * 2 * x.shape[0], x.shape[1])
+
+
+def gather_all_rows(x, count):
+    halves = x.reshape(2 * x.shape[0], x.shape[1] // 2)
+    copies = jnp.broadcast_to(halves[None], (count,) + halves.shape).reshape((count * halves.shape[0], halves.shape[1]))
+    got = lax.all_to_all(copies, ROWS, split_axis=0, concat_axis=0, tiled=True)
+    return got.reshape(count * x.shape[0], x.shape[1])
 
 
 def scatter_rows(x, chips, narrow=False):
@@ -83,7 +90,7 @@
         features = lax.all_to_all(attended, ROWS, split_axis=1, concat_axis=0, tiled=True)
     partial_value = jnp.dot(features, out_weight, preferred_element_type=jnp.float32)
     hidden_here = (scatter_rows(partial_value, chips, narrow=True) + resid.astype(jnp.float32)).astype(jnp.bfloat16)
-    hidden = gather_rows(hidden_here, chips)
+    hidden = gather_all_rows(hidden_here, 2 * chips)
     lat_here = enc_weight.shape[1]
     latent_ids = lax.axis_index(ROWS) * lat_here + lax.broadcasted_iota(jnp.int32, (lat_here,), 0)
     listed = jnp.any(chat_ids[:, None] == latent_ids[None, :], axis=0)

time: 60.4 us -> 60 us (level)
    ppermute x1 -> x0, waiting for transfers between devices: 1.08 us -> none  [gather_rows(): mate = lax.ppermute(mine, 'core', [(0, 1), (1, 0)])]
    all_to_all x1, waiting for transfers between devices: 6.82 us -> 7.69 us  [gather_all_rows(): got = lax.all_to_all(copies, ROWS, split_axis=0, concat_axis=0, tiled=True)]
  transfers between devices with their start and end apart: 5 -> 4, of which waited for: 5 -> 4; matrix products, arithmetic and copies ran while one was open for 0% -> 0% of each run, Pallas kernels for 0% -> 0%
where the time goes in v13:
time: 60 us; the launch traced here: 59.6 us
  blocking collectives  18.6 us (31%)
  waiting for transfers between devices  16.7 us (28%)
  starting transfers between devices  11 us (18%)
  matrix products  6.59 us (11%)
  other arithmetic  2.58 us (4%)
  local copies, waits for them, and re-layouts  2.44 us (4%)
  between operations  1.66 us (3%)
    all_to_all x2, blocking collectives, scatter_rows(): got = lax.all_to_all(sent, 'chip', split_axis=0, concat_axis=0, tiled=True)  18.6 us
    all_to_all x1, waiting for transfers between devices, gather_all_rows(): got = lax.all_to_all(copies, ROWS, split_axis=0, concat_axis=0, tiled=True)  7.69 us
    all_to_all x1, starting transfers between devices, shards(): got = lax.all_to_all(blocks, ROWS, split_axis=0, concat_axis=0, tiled=True)  7.39 us
    all_to_all x1, waiting for transfers between devices, shards(): got = lax.all_to_all(blocks, ROWS, split_axis=0, concat_axis=0, tiled=True)  6.35 us
    all_to_all x1, starting transfers between devices, gather_all_rows(): got = lax.all_to_all(copies, ROWS, split_axis=0, concat_axis=0, tiled=True)  3.51 us
    dot_general x1, matrix products, shards(): jnp.dot(hidden, enc_weight, preferred_element_type=jnp.float32)  2.98 us
    ppermute x2, waiting for transfers between devices, scatter_rows(): summed = keep + lax.ppermute(give, 'core', [(0, 1), (1, 0)])  2.67 us
    dot_general x1, matrix products, shards(): jnp.einsum('rhc,rsc->rhs', spread, keys, preferred_element_type=jnp.float32)  1.36 us
  transfers between devices with their start and end apart: 4, of which 4 were waited for; matrix products, arithmetic and copies ran while one was open for 0% of the time, Pallas kernels for 0%

profile of v13, /device:TPU:0, one launch (start us, length us, event | category | flops | bytes accessed | tf_op | source)
XLA Modules:
  0.0 59.6 jit_solution(3273163790178994410)
XLA Ops:
  1.5 0.8 %reduce.7 = bf16[4096]{0:T(1024)(128)(2,1)S(1)} reduce(bf16[1,4096]{1,0:T(2,128)(2,1)} %param.11, bf16[]{:T(256)} %constant.49), dimensions={0}, to_apply=%param.11.reduce_sub_computation | reduce | bytes 16386 | tf_op args[0]
  2.3 0.1 fusion.18
  2.4 0.1 broadcast_multiply_fusion
  2.5 1.4 %fusion.20 = (f32[32]{0:T(128)S(1)}, f32[32,384]{1,0:T(8,128)S(1)}) fusion(bf16[1,384,512]{2,1,0:T(8,128)(2,1)} %param.12, bf16[4,8,4,128]{3,2,1,0:T(4,128)(2,1)S(1)} %bitcast.68, pred[384]{0:T(512)(128)(4,1)S(1)} %iota_compare_fusion.1), kind=kOutput, calls=%fused_computation.45 | convolution fusion | flops 12619744 | bytes 475648 | tf_op jit(solution)/shard_map/rhc,rsc->rhs/dot_general | solution.py:72
  3.8 0.2 fusion.11
  4.0 1.2 %convolution_bitcast_fusion = f32[1,32,512]{2,1,0:T(8,128)S(1)} fusion(bf16[1,384,512]{2,1,0:T(8,128)(2,1)} %param.13, f32[32,384]{1,0:T(8,128)S(1)} %get-tuple-element.7, f32[32]{0:T(128)S(1)} %fusion.11, f32[32]{0:T(128)S(1)} %get-tuple-element.6), kind=kOutput, calls=%fused_computation.2 | convolution fusion | flops 12619776 | bytes 508160 | tf_op jit(solution)/shard_map/rhs,rsc->rhc/dot_general | solution.py:80
  5.3 0.7 %multiply_reduce_fusion = bf16[32,128]{1,0:T(8,128)(2,1)} fusion(f32[1,32,4,128]{3,2,1,0:T(4,128)S(1)} %reshape.315, f32[32,4]{1,0:T(8,128)S(1)} %get-tuple-element.4), kind=kLoop, calls=%fused_computation.22 | loop fusion | flops 28672 | bytes 74240 | tf_op jit(solution)/shard_map/reduce_sum | solution.py:82
  6.0 7.4 %all-to-all-start = ((bf16[16,2,128]{2,1,0:T(2,128)(2,1)}), bf16[16,2,128]{2,1,0:T(2,128)(2,1)S(1)}, u32[]{:S(2)}, u32[]{:S(2)}) async-start(bf16[16,2,128]{2,1,0:T(2,128)(2,1)} %bitcast.4), calls=%async_computation | async-start | bytes 16384 | tf_op jit(solution)/shard_map/all_to_all | solution.py:86
  13.4 6.4 %all-to-all-done = bf16[16,2,128]{2,1,0:T(2,128)(2,1)S(1)} async-done(((bf16[16,2,128]{2,1,0:T(2,128)(2,1)}), bf16[16,2,128]{2,1,0:T(2,128)(2,1)S(1)}, u32[]{:S(2)}, u32[]{:S(2)}) %all-to-all-start) | async-done | bytes 8224 | tf_op jit(solution)/shard_map/all_to_all | solution.py:86
  19.8 0.4 fusion
  20.2 0.1 collective-permute-start
  20.3 1.3 %collective-permute-done = f32[8,1,4096]{2,0,1:T(8,128)S(1)} collective-permute-done((f32[8,1,4096]{2,0,1:T(8,128)S(1)}, f32[8,1,4096]{2,0,1:T(8,128)S(1)}, u32[]{:S(2)}, u32[]{:S(2)}) %collective-permute-start) | collective-permute-done | bytes 131104 | tf_op jit(solution)/shard_map/ppermute | solution.py:39
  21.6 0.1 copy.38
  21.7 9.3 %all_to_all.29 = bf16[8,2,2048]{2,1,0:T(2,128)(2,1)S(1)} all-to-all(bf16[8,2,2048]{2,1,0:T(2,128)(2,1)S(1)} %copy.38), channel_id=1, replica_groups=mesh['groups'=2,'chip'=8,'core'=2] {'chip'}, dimensions={0} | all-to-all | bytes 131072 | tf_op jit(solution)/shard_map/all_to_all | solution.py:42
  31.0 0.1 convert_reduce_fusion.1
  31.2 0.7 %broadcast_in_dim.47 = bf16[16,2,2048]{2,1,0:T(2,128)(2,1)} broadcast(bf16[2,2048]{1,0:T(2,128)(2,1)S(1)} %broadcast_in_dim.46), dimensions={1,2} | broadcast | bytes 139264 | tf_op jit(solution)/shard_map/broadcast_in_dim | solution.py:29
  31.9 3.5 %all-to-all-start.2 = ((bf16[16,2,2048]{2,1,0:T(2,128)(2,1)}), bf16[16,2,2048]{2,1,0:T(2,128)(2,1)S(1)}, u32[]{:S(2)}, u32[]{:S(2)}) async-start(bf16[16,2,2048]{2,1,0:T(2,128)(2,1)} %broadcast_in_dim.47), calls=%async_computation.2 | async-start | bytes 262144 | tf_op jit(solution)/shard_map/all_to_all | solution.py:30
  35.4 0.2 compare_reduce_fusion
  35.6 7.7 %all-to-all-done.2 = bf16[16,2,2048]{2,1,0:T(2,128)(2,1)S(1)} async-done(((bf16[16,2,2048]{2,1,0:T(2,128)(2,1)}), bf16[16,2,2048]{2,1,0:T(2,128)(2,1)S(1)}, u32[]{:S(2)}, u32[]{:S(2)}) %all-to-all-start.2) | async-done | bytes 131104 | tf_op jit(solution)/shard_map/all_to_all | solution.py:30
  43.3 3.0 %fusion.5 = bf16[16,512]{1,0:T(8,128)(2,1)S(1)} fusion(bf16[16,4096]{1,0:T(8,128)(2,1)S(1)} %bitcast.64, bf16[4096,512]{1,0:T(8,128)(2,1)} %param.18, f32[512]{0:T(512)S(1)} %copy-done.5, pred[512]{0:T(512)(128)(4,1)S(1)} %compare_reduce_fusion), kind=kOutput, calls=%fused_computation.8 | convolution fusion | flops 67141632 | bytes 4344320 | tf_op jit(solution)/shard_map/dot_general | solution.py:101
  46.3 0.4 copy-done.1
  46.7 0.7 %fusion.21 = f32[16,4096]{1,0:T(8,128)S(1)} fusion(bf16[16,512]{1,0:T(8,128)(2,1)S(1)} %fusion.5, bf16[512,4096]{1,0:T(8,128)(2,1)S(1)} %copy-done.1), kind=kOutput, calls=%fused_computation.46 | convolution fusion | flops 67108864 | bytes 4472832 | tf_op jit(solution)/shard_map/dot_general | solution.py:104
  47.4 0.2 reshape.317
  47.5 0.2 fusion.19
  47.8 0.2 select_bitcast_fusion
  48.0 0.1 collective-permute-start.1
  48.0 1.3 %collective-permute-done.1 = f32[8,1,4096]{2,0,1:T(8,128)S(1)} collective-permute-done((f32[8,1,4096]{2,0,1:T(8,128)S(1)}, f32[8,1,4096]{2,0,1:T(8,128)S(1)}, u32[]{:S(2)}, u32[]{:S(2)}) %collective-permute-start.1) | collective-permute-done | bytes 131104 | tf_op jit(solution)/shard_map/ppermute | solution.py:39
  49.4 0.1 fusion.8
  49.5 0.1 copy.41
  49.6 9.3 %all_to_all.30 = bf16[8,2,2048]{2,1,0:T(2,128)(2,1)S(1)} all-to-all(bf16[8,2,2048]{2,1,0:T(2,128)(2,1)S(1)} %copy.41), channel_id=1, replica_groups=mesh['groups'=2,'chip'=8,'core'=2] {'chip'}, dimensions={0} | all-to-all | bytes 131072 | tf_op jit(solution)/shard_map/all_to_all | solution.py:42
  58.9 0.1 convert_reduce_fusion
  59.0 0.6 %convert_element_type.76 = bf16[1,4096]{1,0:T(2,128)(2,1)} reshape(bf16[4096]{0:T(1024)(128)(2,1)S(1)} %add_convert_fusion) | data formatting | bytes 16384 | tf_op jit(solution)/shard_map/convert_element_type | solution.py:105
  (27 shorter events, 0.3 us)
Async XLA Ops:
  0.6 19.1 %copy-start = (bf16[256,4096]{1,0:T(8,128)(2,1)S(1)}, bf16[256,4096]{1,0:T(8,128)(2,1)}, u32[]{:S(2)}) copy-start(bf16[256,4096]{1,0:T(8,128)(2,1)} %param.16) | copy-start | bytes 6291460
  0.6 30.4 %copy-start.3 = (bf16[1,4096]{1,0:T(2,128)(2,1)S(1)}, bf16[1,4096]{1,0:T(2,128)(2,1)}, u32[]{:S(2)}) copy-start(bf16[1,4096]{1,0:T(2,128)(2,1)} %param.15) | copy-start | bytes 24580
  0.7 34.8 %copy-start.6 = (s32[256]{0:T(256)S(1)}, s32[256]{0:T(256)}, u32[]{:S(2)}) copy-start(s32[256]{0:T(256)} %param.17) | copy-start | bytes 3076
  0.7 42.7 %copy-start.5 = (f32[512]{0:T(512)S(1)}, f32[512]{0:T(512)}, u32[]{:S(2)}) copy-start(f32[512]{0:T(512)} %param.19) | copy-start | bytes 6148
  6.0 13.8 %all-to-all-start = ((bf16[16,2,128]{2,1,0:T(2,128)(2,1)}), bf16[16,2,128]{2,1,0:T(2,128)(2,1)S(1)}, u32[]{:S(2)}, u32[]{:S(2)}) async-start(bf16[16,2,128]{2,1,0:T(2,128)(2,1)} %bitcast.4), calls=%async_computation | async-start | bytes 16384 | tf_op jit(solution)/shard_map/all_to_all | solution.py:86
  20.2 1.4 %collective-permute-start = (f32[8,1,4096]{2,0,1:T(8,128)S(1)}, f32[8,1,4096]{2,0,1:T(8,128)S(1)}, u32[]{:S(2)}, u32[]{:S(2)}) collective-permute-start(f32[8,1,4096]{2,0,1:T(8,128)S(1)} %fusion.9), channel_id=1, source_target_pairs={{0,1},{1,0},{2,3},{3,2},{4,5},{5,4},{6,7},{7,6},{8,9},{9,8},{10,11... | collective-permute-start | bytes 393224 | tf_op jit(solution)/shard_map/ppermute | solution.py:39
  31.9 11.4 %all-to-all-start.2 = ((bf16[16,2,2048]{2,1,0:T(2,128)(2,1)}), bf16[16,2,2048]{2,1,0:T(2,128)(2,1)S(1)}, u32[]{:S(2)}, u32[]{:S(2)}) async-start(bf16[16,2,2048]{2,1,0:T(2,128)(2,1)} %broadcast_in_dim.47), calls=%async_computation.2 | async-start | bytes 262144 | tf_op jit(solution)/shard_map/all_to_all | solution.py:30
  43.3 3.4 %copy-start.1 = (bf16[512,4096]{1,0:T(8,128)(2,1)S(1)}, bf16[512,4096]{1,0:T(8,128)(2,1)}, u32[]{:S(2)}) copy-start(bf16[512,4096]{1,0:T(8,128)(2,1)} %param.20) | copy-start | bytes 12582916
  46.7 12.9 %copy-start.2 = (bf16[16,512]{1,0:T(8,128)(2,1)}, bf16[16,512]{1,0:T(8,128)(2,1)S(1)}, u32[]{:S(2)}) copy-start(bf16[16,512]{1,0:T(8,128)(2,1)S(1)} %fusion.5) | copy-start | bytes 49156
  46.7 12.2 %copy-start.4 = (f32[4096]{0:T(1024)S(1)}, f32[4096]{0:T(1024)}, u32[]{:S(2)}) copy-start(f32[4096]{0:T(1024)} %param.21) | copy-start | bytes 49156
  48.0 1.4 %collective-permute-start.1 = (f32[8,1,4096]{2,0,1:T(8,128)S(1)}, f32[8,1,4096]{2,0,1:T(8,128)S(1)}, u32[]{:S(2)}, u32[]{:S(2)}) collective-permute-start(f32[8,1,4096]{2,0,1:T(8,128)S(1)} %select_bitcast_fusion), channel_id=1, source_target_pairs={{0,1},{1,0},{2,3},{3,2},{4,5},{5,4},{6,7},{7,6},{8,9},{9,8},{10,11... | collective-permute-start | bytes 393224 | tf_op jit(solution)/shard_map/ppermute | solution.py:39

commit v14 on v13

--- a/solution.py
+++ b/solution.py
@@ -29,6 +29,13 @@
     copies = jnp.broadcast_to(halves[None], (count,) + halves.shape).reshape((count * halves.shape[0], halves.shape[1]))
     got = lax.all_to_all(copies, ROWS, split_axis=0, concat_axis=0, tiled=True)
     return got.reshape(count * x.shape[0], x.shape[1])
+
+
+def scatter_all_rows(x, count):
+    per = x.shape[0] // count
+    sent = x.astype(jnp.bfloat16).reshape(count * per * 2, x.shape[1] // 2)
+    got = lax.all_to_all(sent, ROWS, split_axis=0, concat_axis=0, tiled=True)
+    return got.astype(jnp.float32).reshape(count, per, x.shape[1]).sum(axis=0)
 
 
 def scatter_rows(x, chips, narrow=False):
@@ -89,7 +96,7 @@
         attended = attended.reshape(rows_here, heads * HEAD_DIM)
         features = lax.all_to_all(attended, ROWS, split_axis=1, concat_axis=0, tiled=True)
     partial_value = jnp.dot(features, out_weight, preferred_element_type=jnp.float32)
-    hidden_here = (scatter_rows(partial_value, chips, narrow=True) + resid.astype(jnp.float32)).astype(jnp.bfloat16)
+    hidden_here = (scatter_all_rows(partial_value, 2 * chips) + resid.astype(jnp.float32)).astype(jnp.bfloat16)
     hidden = gather_all_rows(hidden_here, 2 * chips)
     lat_here = enc_weight.shape[1]
     latent_ids = lax.axis_index(ROWS) * lat_here + lax.broadcasted_iota(jnp.int32, (lat_here,), 0)
@@ -101,7 +108,7 @@
             jnp.dot(hidden, enc_weight, preferred_element_type=jnp.float32) + enc_bias[None, :]
         ),
     ).astype(jnp.bfloat16)
-    rebuilt = scatter_rows(jnp.dot(activity, dec_weight, preferred_element_type=jnp.float32), chips, narrow=True)
+    rebuilt = scatter_all_rows(jnp.dot(activity, dec_weight, preferred_element_type=jnp.float32), 2 * chips)
     spliced = (rebuilt + dec_bias[None, :]).astype(jnp.bfloat16)
     return (spliced, activity)
 

time: 60 us -> 58.2 us (0.970)
  blocking collectives: 18.6 us -> 34.6 us
  waiting for transfers between devices: 16.7 us -> 7.69 us
  starting transfers between devices: 11 us -> 3.51 us
  other arithmetic: 2.58 us -> 1.75 us
    all_to_all x2 -> x3, blocking collectives: 18.6 us -> 34.6 us  [the longest x2 21 us: scatter_all_rows(): got = lax.all_to_all(sent, ROWS, split_axis=0, concat_axis=0, tiled=True)]
    all_to_all x1 -> x0, starting transfers between devices: 7.39 us -> none  [shards(): got = lax.all_to_all(blocks, ROWS, split_axis=0, concat_axis=0, tiled=True)]
    all_to_all x1 -> x0, waiting for transfers between devices: 6.35 us -> none  [shards(): got = lax.all_to_all(blocks, ROWS, split_axis=0, concat_axis=0, tiled=True)]
    ppermute x2 -> x0, waiting for transfers between devices: 2.67 us -> none  [scatter_rows(): summed = keep + lax.ppermute(give, 'core', [(0, 1), (1, 0)])]
    reduce_sum x1, other arithmetic: 0.72 us -> 0.12 us  [shards(): attended = mixed.sum(axis=2).astype(jnp.bfloat16)]
  transfers between devices with their start and end apart: 4 -> 1, of which waited for: 4 -> 1; matrix products, arithmetic and copies ran while one was open for 0% -> 0% of each run, Pallas kernels for 0% -> 0%
where the time goes in v14:
time: 58.2 us; the launch traced here: 57.8 us
  blocking collectives  34.6 us (59%)
  waiting for transfers between devices  7.69 us (13%)
  matrix products  6.59 us (11%)
  starting transfers between devices  3.51 us (6%)
  local copies, waits for them, and re-layouts  2.04 us (4%)
  other arithmetic  1.75 us (3%)
  between operations  1.59 us (3%)
    all_to_all x2, blocking collectives, scatter_all_rows(): got = lax.all_to_all(sent, ROWS, split_axis=0, concat_axis=0, tiled=True)  21 us
    all_to_all x1, blocking collectives, shards(): got = lax.all_to_all(blocks, ROWS, split_axis=0, concat_axis=0, tiled=True)  13.6 us
    all_to_all x1, waiting for transfers between devices, gather_all_rows(): got = lax.all_to_all(copies, ROWS, split_axis=0, concat_axis=0, tiled=True)  7.69 us
    all_to_all x1, starting transfers between devices, gather_all_rows(): got = lax.all_to_all(copies, ROWS, split_axis=0, concat_axis=0, tiled=True)  3.51 us
    dot_general x1, matrix products, shards(): jnp.dot(hidden, enc_weight, preferred_element_type=jnp.float32)  2.98 us
    dot_general x1, matrix products, shards(): jnp.einsum('rhc,rsc->rhs', spread, keys, preferred_element_type=jnp.float32)  1.36 us
    dot_general x1, matrix products, shards(): jnp.einsum('rhs,rsc->rhc', weights, values, preferred_element_type=jnp.fl...  1.21 us
  transfers between devices with their start and end apart: 1, of which 1 were waited for; matrix products, arithmetic and copies ran while one was open for 0% of the time, Pallas kernels for 0%

profile of v14, /device:TPU:0, one launch (start us, length us, event | category | flops | bytes accessed | tf_op | source)
XLA Modules:
  0.0 57.8 jit_solution(14373841436185218065)
XLA Ops:
  0.6 0.0 copy-start
  0.6 0.0 copy-start.3
  0.7 0.0 copy-start.6
  0.7 0.0 copy-start.5
  1.5 0.8 %reduce.7 = bf16[4096]{0:T(1024)(128)(2,1)S(1)} reduce(bf16[1,4096]{1,0:T(2,128)(2,1)} %param.11, bf16[]{:T(256)} %constant.48), dimensions={0}, to_apply=%param.11.reduce_sub_computation | reduce | bytes 16386 | tf_op args[0]
  2.3 0.1 fusion.14
  2.4 0.1 broadcast_multiply_fusion
  2.5 1.4 %fusion.15 = (f32[32]{0:T(128)S(1)}, f32[32,384]{1,0:T(8,128)S(1)}) fusion(bf16[1,384,512]{2,1,0:T(8,128)(2,1)} %param.12, bf16[4,8,4,128]{3,2,1,0:T(4,128)(2,1)S(1)} %bitcast.38, pred[384]{0:T(512)(128)(4,1)S(1)} %iota_compare_fusion.1), kind=kOutput, calls=%fused_computation.37 | convolution fusion | flops 12619744 | bytes 475648 | tf_op jit(solution)/shard_map/rhc,rsc->rhs/dot_general | solution.py:79
  3.8 0.2 fusion.6
  4.0 1.2 %convolution_bitcast_fusion = f32[1,32,512]{2,1,0:T(8,128)S(1)} fusion(bf16[1,384,512]{2,1,0:T(8,128)(2,1)} %param.13, f32[32,384]{1,0:T(8,128)S(1)} %get-tuple-element.5, f32[32]{0:T(128)S(1)} %fusion.6, f32[32]{0:T(128)S(1)} %get-tuple-element.4), kind=kOutput, calls=%fused_computation.2 | convolution fusion | flops 12619776 | bytes 508160 | tf_op jit(solution)/shard_map/rhs,rsc->rhc/dot_general | solution.py:87
  5.3 0.1 multiply_reduce_fusion
  5.4 13.6 %all_to_all.29 = bf16[16,2,128]{2,1,0:T(2,128)(2,1)S(1)} all-to-all(bf16[16,2,128]{2,1,0:T(2,128)(2,1)S(1)} %bitcast.45), channel_id=1, replica_groups=mesh['groups'=2,'chip'=8,'core'=2] {'chip','core'}, dimensions={0} | all-to-all | bytes 16384 | tf_op jit(solution)/shard_map/all_to_all | solution.py:93
  19.0 0.0 copy-done
  19.0 0.4 convolution_convert_fusion.1
  19.4 0.1 all_to_all.20
  19.5 10.5 %all_to_all.30 = bf16[16,2,2048]{2,1,0:T(2,128)(2,1)S(1)} all-to-all(bf16[16,2,2048]{2,1,0:T(2,128)(2,1)S(1)} %all_to_all.20), channel_id=1, replica_groups=mesh['groups'=2,'chip'=8,'core'=2] {'chip','core'}, dimensions={0} | all-to-all | bytes 262144 | tf_op jit(solution)/shard_map/all_to_all | solution.py:37
  30.0 0.1 convert_reduce_fusion.1
  30.1 0.0 copy-done.3
  30.2 0.1 convert_reduce_fusion.2
  30.2 0.7 %broadcast_in_dim.47 = bf16[16,2,2048]{2,1,0:T(2,128)(2,1)} broadcast(bf16[2,2048]{1,0:T(2,128)(2,1)S(1)} %broadcast_in_dim.46), dimensions={1,2} | broadcast | bytes 139264 | tf_op jit(solution)/shard_map/broadcast_in_dim | solution.py:29
  30.9 3.5 %all-to-all-start.2 = ((bf16[16,2,2048]{2,1,0:T(2,128)(2,1)}), bf16[16,2,2048]{2,1,0:T(2,128)(2,1)S(1)}, u32[]{:S(2)}, u32[]{:S(2)}) async-start(bf16[16,2,2048]{2,1,0:T(2,128)(2,1)} %broadcast_in_dim.47), calls=%async_computation.2 | async-start | bytes 262144 | tf_op jit(solution)/shard_map/all_to_all | solution.py:30
  34.5 0.0 copy-done.6
  34.5 0.2 compare_reduce_fusion
  34.6 7.7 %all-to-all-done.2 = bf16[16,2,2048]{2,1,0:T(2,128)(2,1)S(1)} async-done(((bf16[16,2,2048]{2,1,0:T(2,128)(2,1)}), bf16[16,2,2048]{2,1,0:T(2,128)(2,1)S(1)}, u32[]{:S(2)}, u32[]{:S(2)}) %all-to-all-start.2) | async-done | bytes 131104 | tf_op jit(solution)/shard_map/all_to_all | solution.py:30
  42.4 0.0 copy-start.4
  42.4 3.0 %fusion.3 = bf16[16,512]{1,0:T(8,128)(2,1)S(1)} fusion(bf16[16,4096]{1,0:T(8,128)(2,1)S(1)} %bitcast.36, bf16[4096,512]{1,0:T(8,128)(2,1)} %param.18, f32[512]{0:T(512)S(1)} %copy-done.5, pred[512]{0:T(512)(128)(4,1)S(1)} %compare_reduce_fusion), kind=kOutput, calls=%fused_computation.8 | convolution fusion | flops 67141632 | bytes 4344320 | tf_op jit(solution)/shard_map/dot_general | solution.py:108
  45.4 0.4 copy-done.1
  45.8 0.7 %convolution_convert_fusion = bf16[16,4096]{1,0:T(8,128)(2,1)S(1)} fusion(bf16[16,512]{1,0:T(8,128)(2,1)S(1)} %fusion.3, bf16[512,4096]{1,0:T(8,128)(2,1)S(1)} %copy-done.1), kind=kOutput, calls=%fused_computation | convolution fusion | flops 67174400 | bytes 4341760 | tf_op jit(solution)/shard_map/dot_general | solution.py:111
  46.4 0.1 all_to_all.23
  46.5 10.5 %all_to_all.31 = bf16[16,2,2048]{2,1,0:T(2,128)(2,1)S(1)} all-to-all(bf16[16,2,2048]{2,1,0:T(2,128)(2,1)S(1)} %all_to_all.23), channel_id=1, replica_groups=mesh['groups'=2,'chip'=8,'core'=2] {'chip','core'}, dimensions={0} | all-to-all | bytes 262144 | tf_op jit(solution)/shard_map/all_to_all | solution.py:37
  57.0 0.1 convert_reduce_fusion
  57.2 0.6 %convert_element_type.76 = bf16[1,4096]{1,0:T(2,128)(2,1)} reshape(bf16[4096]{0:T(1024)(128)(2,1)S(1)} %add_convert_fusion) | data formatting | bytes 16384 | tf_op jit(solution)/shard_map/convert_element_type | solution.py:112
  (15 shorter events, 0.2 us)
Async XLA Ops:
  0.6 18.4 %copy-start = (bf16[256,4096]{1,0:T(8,128)(2,1)S(1)}, bf16[256,4096]{1,0:T(8,128)(2,1)}, u32[]{:S(2)}) copy-start(bf16[256,4096]{1,0:T(8,128)(2,1)} %param.16) | copy-start | bytes 6291460
  0.6 29.5 %copy-start.3 = (bf16[1,4096]{1,0:T(2,128)(2,1)S(1)}, bf16[1,4096]{1,0:T(2,128)(2,1)}, u32[]{:S(2)}) copy-start(bf16[1,4096]{1,0:T(2,128)(2,1)} %param.15) | copy-start | bytes 24580
  0.7 33.8 %copy-start.6 = (s32[256]{0:T(256)S(1)}, s32[256]{0:T(256)}, u32[]{:S(2)}) copy-start(s32[256]{0:T(256)} %param.17) | copy-start | bytes 3076
  0.7 41.7 %copy-start.5 = (f32[512]{0:T(512)S(1)}, f32[512]{0:T(512)}, u32[]{:S(2)}) copy-start(f32[512]{0:T(512)} %param.19) | copy-start | bytes 6148
  30.9 11.4 %all-to-all-start.2 = ((bf16[16,2,2048]{2,1,0:T(2,128)(2,1)}), bf16[16,2,2048]{2,1,0:T(2,128)(2,1)S(1)}, u32[]{:S(2)}, u32[]{:S(2)}) async-start(bf16[16,2,2048]{2,1,0:T(2,128)(2,1)} %broadcast_in_dim.47), calls=%async_computation.2 | async-start | bytes 262144 | tf_op jit(solution)/shard_map/all_to_all | solution.py:30
  42.3 3.4 %copy-start.1 = (bf16[512,4096]{1,0:T(8,128)(2,1)S(1)}, bf16[512,4096]{1,0:T(8,128)(2,1)}, u32[]{:S(2)}) copy-start(bf16[512,4096]{1,0:T(8,128)(2,1)} %param.20) | copy-start | bytes 12582916
  42.4 14.8 %copy-start.4 = (f32[4096]{0:T(1024)S(1)}, f32[4096]{0:T(1024)}, u32[]{:S(2)}) copy-start(f32[4096]{0:T(1024)} %param.21) | copy-start | bytes 49156
  45.8 12.0 %copy-start.2 = (bf16[16,512]{1,0:T(8,128)(2,1)}, bf16[16,512]{1,0:T(8,128)(2,1)S(1)}, u32[]{:S(2)}) copy-start(bf16[16,512]{1,0:T(8,128)(2,1)S(1)} %fusion.3) | copy-start | bytes 49156

commit v15 on v14

--- a/solution.py
+++ b/solution.py
@@ -79,7 +79,7 @@
     scores = jnp.einsum("rhc,rsc->rhs", spread, keys, preferred_element_type=jnp.float32)
     scores = scores / jnp.sqrt(jnp.float32(HEAD_DIM))
     cache_span = keys.shape[1]
-    visible = lax.broadcasted_iota(jnp.int32, (rows_here, cache_span), 1) < lengths[:, None]
+    visible = lax.broadcasted_iota(jnp.float32, (rows_here, cache_span), 1) < lengths.astype(jnp.float32)[:, None]
     scores = jnp.where(visible[:, None, :], scores, -jnp.inf)
     highest = jnp.max(scores, axis=-1, keepdims=True)
     expo = jnp.exp(scores - highest)

time: 58.2 us -> 58.2 us (level)
  no operation moved by 1% of the time
where the time goes in v15:
time: 58.2 us; the launch traced here: 57.8 us
  blocking collectives  34.6 us (59%)
  waiting for transfers between devices  7.69 us (13%)
  matrix products  6.59 us (11%)
  starting transfers between devices  3.51 us (6%)
  local copies, waits for them, and re-layouts  2.04 us (4%)
  other arithmetic  1.75 us (3%)
  between operations  1.59 us (3%)
    all_to_all x2, blocking collectives, scatter_all_rows(): got = lax.all_to_all(sent, ROWS, split_axis=0, concat_axis=0, tiled=True)  21 us
    all_to_all x1, blocking collectives, shards(): got = lax.all_to_all(blocks, ROWS, split_axis=0, concat_axis=0, tiled=True)  13.6 us
    all_to_all x1, waiting for transfers between devices, gather_all_rows(): got = lax.all_to_all(copies, ROWS, split_axis=0, concat_axis=0, tiled=True)  7.69 us
    all_to_all x1, starting transfers between devices, gather_all_rows(): got = lax.all_to_all(copies, ROWS, split_axis=0, concat_axis=0, tiled=True)  3.51 us
    dot_general x1, matrix products, shards(): jnp.dot(hidden, enc_weight, preferred_element_type=jnp.float32)  2.98 us
    dot_general x1, matrix products, shards(): jnp.einsum('rhc,rsc->rhs', spread, keys, preferred_element_type=jnp.float32)  1.36 us
    dot_general x1, matrix products, shards(): jnp.einsum('rhs,rsc->rhc', weights, values, preferred_element_type=jnp.fl...  1.21 us
  transfers between devices with their start and end apart: 1, of which 1 were waited for; matrix products, arithmetic and copies ran while one was open for 0% of the time, Pallas kernels for 0%

profile of v15, /device:TPU:0, one launch (start us, length us, event | category | flops | bytes accessed | tf_op | source)
XLA Modules:
  0.0 57.8 jit_solution(598267540868956610)
XLA Ops:
  0.6 0.0 copy-start
  0.6 0.0 copy-start.3
  0.7 0.0 copy-start.6
  0.7 0.0 copy-start.5
  1.5 0.8 %reduce.7 = bf16[4096]{0:T(1024)(128)(2,1)S(1)} reduce(bf16[1,4096]{1,0:T(2,128)(2,1)} %param.11, bf16[]{:T(256)} %constant.48), dimensions={0}, to_apply=%param.11.reduce_sub_computation | reduce | bytes 16386 | tf_op args[0]
  2.3 0.1 fusion.14
  2.4 0.1 broadcast_multiply_fusion
  2.5 1.4 %fusion.15 = (f32[32]{0:T(128)S(1)}, f32[32,384]{1,0:T(8,128)S(1)}) fusion(bf16[1,384,512]{2,1,0:T(8,128)(2,1)} %param.12, bf16[4,8,4,128]{3,2,1,0:T(4,128)(2,1)S(1)} %bitcast.37, pred[384]{0:T(512)(128)(4,1)S(1)} %iota_compare_fusion.1), kind=kOutput, calls=%fused_computation.37 | convolution fusion | flops 12619744 | bytes 475648 | tf_op jit(solution)/shard_map/rhc,rsc->rhs/dot_general | solution.py:79
  3.8 0.2 fusion.6
  4.0 1.2 %convolution_bitcast_fusion = f32[1,32,512]{2,1,0:T(8,128)S(1)} fusion(bf16[1,384,512]{2,1,0:T(8,128)(2,1)} %param.13, f32[32,384]{1,0:T(8,128)S(1)} %get-tuple-element.5, f32[32]{0:T(128)S(1)} %fusion.6, f32[32]{0:T(128)S(1)} %get-tuple-element.4), kind=kOutput, calls=%fused_computation.2 | convolution fusion | flops 12619776 | bytes 508160 | tf_op jit(solution)/shard_map/rhs,rsc->rhc/dot_general | solution.py:87
  5.3 0.1 multiply_reduce_fusion
  5.4 13.6 %all_to_all.29 = bf16[16,2,128]{2,1,0:T(2,128)(2,1)S(1)} all-to-all(bf16[16,2,128]{2,1,0:T(2,128)(2,1)S(1)} %bitcast.44), channel_id=1, replica_groups=mesh['groups'=2,'chip'=8,'core'=2] {'chip','core'}, dimensions={0} | all-to-all | bytes 16384 | tf_op jit(solution)/shard_map/all_to_all | solution.py:93
  19.0 0.0 copy-done
  19.0 0.4 convolution_convert_fusion.1
  19.4 0.1 all_to_all.20
  19.5 10.5 %all_to_all.30 = bf16[16,2,2048]{2,1,0:T(2,128)(2,1)S(1)} all-to-all(bf16[16,2,2048]{2,1,0:T(2,128)(2,1)S(1)} %all_to_all.20), channel_id=1, replica_groups=mesh['groups'=2,'chip'=8,'core'=2] {'chip','core'}, dimensions={0} | all-to-all | bytes 262144 | tf_op jit(solution)/shard_map/all_to_all | solution.py:37
  30.0 0.1 convert_reduce_fusion.1
  30.1 0.0 copy-done.3
  30.2 0.1 convert_reduce_fusion.2
  30.2 0.7 %broadcast_in_dim.47 = bf16[16,2,2048]{2,1,0:T(2,128)(2,1)} broadcast(bf16[2,2048]{1,0:T(2,128)(2,1)S(1)} %broadcast_in_dim.46), dimensions={1,2} | broadcast | bytes 139264 | tf_op jit(solution)/shard_map/broadcast_in_dim | solution.py:29
  30.9 3.5 %all-to-all-start.2 = ((bf16[16,2,2048]{2,1,0:T(2,128)(2,1)}), bf16[16,2,2048]{2,1,0:T(2,128)(2,1)S(1)}, u32[]{:S(2)}, u32[]{:S(2)}) async-start(bf16[16,2,2048]{2,1,0:T(2,128)(2,1)} %broadcast_in_dim.47), calls=%async_computation.2 | async-start | bytes 262144 | tf_op jit(solution)/shard_map/all_to_all | solution.py:30
  34.5 0.0 copy-done.6
  34.5 0.2 compare_reduce_fusion
  34.6 7.7 %all-to-all-done.2 = bf16[16,2,2048]{2,1,0:T(2,128)(2,1)S(1)} async-done(((bf16[16,2,2048]{2,1,0:T(2,128)(2,1)}), bf16[16,2,2048]{2,1,0:T(2,128)(2,1)S(1)}, u32[]{:S(2)}, u32[]{:S(2)}) %all-to-all-start.2) | async-done | bytes 131104 | tf_op jit(solution)/shard_map/all_to_all | solution.py:30
  42.4 0.0 copy-start.4
  42.4 3.0 %fusion.3 = bf16[16,512]{1,0:T(8,128)(2,1)S(1)} fusion(bf16[16,4096]{1,0:T(8,128)(2,1)S(1)} %bitcast.35, bf16[4096,512]{1,0:T(8,128)(2,1)} %param.18, f32[512]{0:T(512)S(1)} %copy-done.5, pred[512]{0:T(512)(128)(4,1)S(1)} %compare_reduce_fusion), kind=kOutput, calls=%fused_computation.8 | convolution fusion | flops 67141632 | bytes 4344320 | tf_op jit(solution)/shard_map/dot_general | solution.py:108
  45.4 0.4 copy-done.1
  45.8 0.7 %convolution_convert_fusion = bf16[16,4096]{1,0:T(8,128)(2,1)S(1)} fusion(bf16[16,512]{1,0:T(8,128)(2,1)S(1)} %fusion.3, bf16[512,4096]{1,0:T(8,128)(2,1)S(1)} %copy-done.1), kind=kOutput, calls=%fused_computation | convolution fusion | flops 67174400 | bytes 4341760 | tf_op jit(solution)/shard_map/dot_general | solution.py:111
  46.4 0.1 all_to_all.23
  46.5 10.5 %all_to_all.31 = bf16[16,2,2048]{2,1,0:T(2,128)(2,1)S(1)} all-to-all(bf16[16,2,2048]{2,1,0:T(2,128)(2,1)S(1)} %all_to_all.23), channel_id=1, replica_groups=mesh['groups'=2,'chip'=8,'core'=2] {'chip','core'}, dimensions={0} | all-to-all | bytes 262144 | tf_op jit(solution)/shard_map/all_to_all | solution.py:37
  57.0 0.1 convert_reduce_fusion
  57.2 0.6 %convert_element_type.80 = bf16[1,4096]{1,0:T(2,128)(2,1)} reshape(bf16[4096]{0:T(1024)(128)(2,1)S(1)} %add_convert_fusion) | data formatting | bytes 16384 | tf_op jit(solution)/shard_map/convert_element_type | solution.py:112
  (15 shorter events, 0.2 us)
Async XLA Ops:
  0.6 18.4 %copy-start = (bf16[256,4096]{1,0:T(8,128)(2,1)S(1)}, bf16[256,4096]{1,0:T(8,128)(2,1)}, u32[]{:S(2)}) copy-start(bf16[256,4096]{1,0:T(8,128)(2,1)} %param.16) | copy-start | bytes 6291460
  0.6 29.5 %copy-start.3 = (bf16[1,4096]{1,0:T(2,128)(2,1)S(1)}, bf16[1,4096]{1,0:T(2,128)(2,1)}, u32[]{:S(2)}) copy-start(bf16[1,4096]{1,0:T(2,128)(2,1)} %param.15) | copy-start | bytes 24580
  0.7 33.8 %copy-start.6 = (s32[256]{0:T(256)S(1)}, s32[256]{0:T(256)}, u32[]{:S(2)}) copy-start(s32[256]{0:T(256)} %param.17) | copy-start | bytes 3076
  0.7 41.7 %copy-start.5 = (f32[512]{0:T(512)S(1)}, f32[512]{0:T(512)}, u32[]{:S(2)}) copy-start(f32[512]{0:T(512)} %param.19) | copy-start | bytes 6148
  30.9 11.4 %all-to-all-start.2 = ((bf16[16,2,2048]{2,1,0:T(2,128)(2,1)}), bf16[16,2,2048]{2,1,0:T(2,128)(2,1)S(1)}, u32[]{:S(2)}, u32[]{:S(2)}) async-start(bf16[16,2,2048]{2,1,0:T(2,128)(2,1)} %broadcast_in_dim.47), calls=%async_computation.2 | async-start | bytes 262144 | tf_op jit(solution)/shard_map/all_to_all | solution.py:30
  42.3 3.4 %copy-start.1 = (bf16[512,4096]{1,0:T(8,128)(2,1)S(1)}, bf16[512,4096]{1,0:T(8,128)(2,1)}, u32[]{:S(2)}) copy-start(bf16[512,4096]{1,0:T(8,128)(2,1)} %param.20) | copy-start | bytes 12582916
  42.4 14.8 %copy-start.4 = (f32[4096]{0:T(1024)S(1)}, f32[4096]{0:T(1024)}, u32[]{:S(2)}) copy-start(f32[4096]{0:T(1024)} %param.21) | copy-start | bytes 49156
  45.8 12.0 %copy-start.2 = (bf16[16,512]{1,0:T(8,128)(2,1)}, bf16[16,512]{1,0:T(8,128)(2,1)S(1)}, u32[]{:S(2)}) copy-start(bf16[16,512]{1,0:T(8,128)(2,1)S(1)} %fusion.3) | copy-start | bytes 49156

commit v16 on v15

--- a/solution.py
+++ b/solution.py
@@ -88,7 +88,16 @@
     mixed = lax.optimization_barrier(mixed).reshape(rows_here, heads, kv_count, HEAD_DIM) * onehot.astype(jnp.float32)[None, :, :, None]
     attended = mixed.sum(axis=2).astype(jnp.bfloat16)
     count = 2 * chips
-    if heads % count == 0:
+    if heads % count == 0 and rows_here == 1:
+        per = heads // count
+        got = lax.all_to_all(attended.reshape(chips, 2 * per, HEAD_DIM), "chip", split_axis=0, concat_axis=0, tiled=True)
+        got = got.reshape(chips, 2, per, HEAD_DIM)
+        mine = pick((got[:, 0], got[:, 1]), 0)
+        mate = lax.ppermute(pick((got[:, 1], got[:, 0]), 0), "core", [(0, 1), (1, 0)])
+        first = pick((mine, mate), 0)
+        second = pick((mate, mine), 0)
+        features = jnp.stack([first, second], axis=1).reshape(count, per * HEAD_DIM)
+    elif heads % count == 0:
         blocks = attended.reshape(rows_here * count, heads // count, HEAD_DIM)
         got = lax.all_to_all(blocks, ROWS, split_axis=0, concat_axis=0, tiled=True)
         features = got.reshape(count * rows_here, (heads // count) * HEAD_DIM)

time: 58.2 us -> 60.3 us (1.036)
  blocking collectives: 34.6 us -> 21 us
  waiting for transfers between devices: 7.69 us -> 15.4 us
  starting transfers between devices: 3.51 us -> 10.9 us
  other arithmetic: 1.75 us -> 2.37 us
    all_to_all x1 -> x0, blocking collectives: 13.6 us -> none  [shards(): got = lax.all_to_all(blocks, ROWS, split_axis=0, concat_axis=0, tiled=True)]
    all_to_all x0 -> x1, starting transfers between devices: none -> 7.28 us  [shards(): lax.all_to_all(attended.reshape(chips, 2 * per, HEAD_DIM), 'chip', split_...]
    all_to_all x0 -> x1, waiting for transfers between devices: none -> 6.52 us  [shards(): lax.all_to_all(attended.reshape(chips, 2 * per, HEAD_DIM), 'chip', split_...]
    ppermute x0 -> x1, waiting for transfers between devices: none -> 1.15 us  [shards(): lax.ppermute(pick((got[:, 1], got[:, 0]), 0), 'core', [(0, 1), (1, 0)])]
  transfers between devices with their start and end apart: 1 -> 3, of which waited for: 1 -> 3; matrix products, arithmetic and copies ran while one was open for 0% -> 0% of each run, Pallas kernels for 0% -> 0%
where the time goes in v16:
time: 60.3 us; the launch traced here: 59.9 us
  blocking collectives  21 us (35%)
  waiting for transfers between devices  15.4 us (26%)
  starting transfers between devices  10.9 us (18%)
  matrix products  6.59 us (11%)
  other arithmetic  2.37 us (4%)
  local copies, waits for them, and re-layouts  2.06 us (3%)
  between operations  1.61 us (3%)
    all_to_all x2, blocking collectives, scatter_all_rows(): got = lax.all_to_all(sent, ROWS, split_axis=0, concat_axis=0, tiled=True)  21 us
    all_to_all x1, waiting for transfers between devices, gather_all_rows(): got = lax.all_to_all(copies, ROWS, split_axis=0, concat_axis=0, tiled=True)  7.69 us
    all_to_all x1, starting transfers between devices, shards(): lax.all_to_all(attended.reshape(chips, 2 * per, HEAD_DIM), 'chip', split_...  7.28 us
    all_to_all x1, waiting for transfers between devices, shards(): lax.all_to_all(attended.reshape(chips, 2 * per, HEAD_DIM), 'chip', split_...  6.52 us
    all_to_all x1, starting transfers between devices, gather_all_rows(): got = lax.all_to_all(copies, ROWS, split_axis=0, concat_axis=0, tiled=True)  3.51 us
    dot_general x1, matrix products, shards(): jnp.dot(hidden, enc_weight, preferred_element_type=jnp.float32)  2.98 us
    dot_general x1, matrix products, shards(): jnp.einsum('rhc,rsc->rhs', spread, keys, preferred_element_type=jnp.float32)  1.36 us
    dot_general x1, matrix products, shards(): jnp.einsum('rhs,rsc->rhc', weights, values, preferred_element_type=jnp.fl...  1.21 us
  transfers between devices with their start and end apart: 3, of which 3 were waited for; matrix products, arithmetic and copies ran while one was open for 0% of the time, Pallas kernels for 0%

profile of v16, /device:TPU:0, one launch (start us, length us, event | category | flops | bytes accessed | tf_op | source)
XLA Modules:
  0.0 59.9 jit_solution(9215196126031261455)
XLA Ops:
  0.6 0.0 copy-start
  0.6 0.0 copy-start.3
  0.7 0.0 copy-start.6
  1.5 0.8 %reduce.7 = bf16[4096]{0:T(1024)(128)(2,1)S(1)} reduce(bf16[1,4096]{1,0:T(2,128)(2,1)} %param.11, bf16[]{:T(256)} %constant.49), dimensions={0}, to_apply=%param.11.reduce_sub_computation | reduce | bytes 16386 | tf_op args[0]
  2.3 0.1 fusion.16
  2.4 0.1 broadcast_multiply_fusion
  2.5 1.4 %fusion.17 = (f32[32]{0:T(128)S(1)}, f32[32,384]{1,0:T(8,128)S(1)}) fusion(bf16[1,384,512]{2,1,0:T(8,128)(2,1)} %param.12, bf16[4,8,4,128]{3,2,1,0:T(4,128)(2,1)S(1)} %bitcast.52, pred[384]{0:T(512)(128)(4,1)S(1)} %iota_compare_fusion.1), kind=kOutput, calls=%fused_computation.44 | convolution fusion | flops 12619744 | bytes 475648 | tf_op jit(solution)/shard_map/rhc,rsc->rhs/dot_general | solution.py:79
  3.8 0.2 fusion.6
  4.0 1.2 %convolution_bitcast_fusion = f32[1,32,512]{2,1,0:T(8,128)S(1)} fusion(bf16[1,384,512]{2,1,0:T(8,128)(2,1)} %param.13, f32[32,384]{1,0:T(8,128)S(1)} %get-tuple-element.7, f32[32]{0:T(128)S(1)} %fusion.6, f32[32]{0:T(128)S(1)} %get-tuple-element.6), kind=kOutput, calls=%fused_computation.2 | convolution fusion | flops 12619776 | bytes 508160 | tf_op jit(solution)/shard_map/rhs,rsc->rhc/dot_general | solution.py:87
  5.3 0.7 %multiply_reduce_fusion = bf16[32,128]{1,0:T(8,128)(2,1)} fusion(f32[1,32,4,128]{3,2,1,0:T(4,128)S(1)} %reshape.226, f32[32,4]{1,0:T(8,128)S(1)} %get-tuple-element.4), kind=kLoop, calls=%fused_computation.14 | loop fusion | flops 28672 | bytes 74240 | tf_op jit(solution)/shard_map/reduce_sum | solution.py:89
  6.0 7.3 %all-to-all-start = ((bf16[8,4,128]{2,1,0:T(4,128)(2,1)}), bf16[8,4,128]{2,1,0:T(4,128)(2,1)S(1)}, u32[]{:S(2)}, u32[]{:S(2)}) async-start(bf16[8,4,128]{2,1,0:T(4,128)(2,1)} %bitcast.4), calls=%async_computation | async-start | bytes 16384 | tf_op jit(solution)/shard_map/all_to_all | solution.py:93
  13.3 6.5 %all-to-all-done = bf16[8,4,128]{2,1,0:T(4,128)(2,1)S(1)} async-done(((bf16[8,4,128]{2,1,0:T(4,128)(2,1)}), bf16[8,4,128]{2,1,0:T(4,128)(2,1)S(1)}, u32[]{:S(2)}, u32[]{:S(2)}) %all-to-all-start) | async-done | bytes 8224 | tf_op jit(solution)/shard_map/all_to_all | solution.py:93
  19.8 0.1 collective-permute-start
  19.9 1.2 %collective-permute-done = bf16[8,2,128]{2,0,1:T(8,128)(2,1)S(1)} collective-permute-done((bf16[8,2,128]{2,0,1:T(8,128)(2,1)S(1)}, bf16[8,2,128]{2,0,1:T(8,128)(2,1)S(1)}, u32[]{:S(2)}, u32[]{:S(2)}) %collective-permute-start) | collective-permute-done | bytes 4128 | tf_op jit(solution)/shard_map/ppermute | solution.py:96
  21.1 0.4 convolution_convert_fusion.1
  21.5 0.1 all_to_all.20
  21.6 10.5 %all_to_all.29 = bf16[16,2,2048]{2,1,0:T(2,128)(2,1)S(1)} all-to-all(bf16[16,2,2048]{2,1,0:T(2,128)(2,1)S(1)} %all_to_all.20), channel_id=1, replica_groups=mesh['groups'=2,'chip'=8,'core'=2] {'chip','core'}, dimensions={0} | all-to-all | bytes 262144 | tf_op jit(solution)/shard_map/all_to_all | solution.py:37
  32.1 0.1 convert_reduce_fusion.1
  32.2 0.1 convert_reduce_fusion.2
  32.3 0.7 %broadcast_in_dim.47 = bf16[16,2,2048]{2,1,0:T(2,128)(2,1)} broadcast(bf16[2,2048]{1,0:T(2,128)(2,1)S(1)} %broadcast_in_dim.46), dimensions={1,2} | broadcast | bytes 139264 | tf_op jit(solution)/shard_map/broadcast_in_dim | solution.py:29
  33.0 3.5 %all-to-all-start.2 = ((bf16[16,2,2048]{2,1,0:T(2,128)(2,1)}), bf16[16,2,2048]{2,1,0:T(2,128)(2,1)S(1)}, u32[]{:S(2)}, u32[]{:S(2)}) async-start(bf16[16,2,2048]{2,1,0:T(2,128)(2,1)} %broadcast_in_dim.47), calls=%async_computation.2 | async-start | bytes 262144 | tf_op jit(solution)/shard_map/all_to_all | solution.py:30
  36.5 0.2 compare_reduce_fusion
  36.7 7.7 %all-to-all-done.2 = bf16[16,2,2048]{2,1,0:T(2,128)(2,1)S(1)} async-done(((bf16[16,2,2048]{2,1,0:T(2,128)(2,1)}), bf16[16,2,2048]{2,1,0:T(2,128)(2,1)S(1)}, u32[]{:S(2)}, u32[]{:S(2)}) %all-to-all-start.2) | async-done | bytes 131104 | tf_op jit(solution)/shard_map/all_to_all | solution.py:30
  44.5 0.0 copy-start.4
  44.5 3.0 %fusion.3 = bf16[16,512]{1,0:T(8,128)(2,1)S(1)} fusion(bf16[16,4096]{1,0:T(8,128)(2,1)S(1)} %bitcast.50, bf16[4096,512]{1,0:T(8,128)(2,1)} %param.18, f32[512]{0:T(512)S(1)} %copy-done.5, pred[512]{0:T(512)(128)(4,1)S(1)} %compare_reduce_fusion), kind=kOutput, calls=%fused_computation.8 | convolution fusion | flops 67141632 | bytes 4344320 | tf_op jit(solution)/shard_map/dot_general | solution.py:117
  47.4 0.4 copy-done.1
  47.8 0.7 %convolution_convert_fusion = bf16[16,4096]{1,0:T(8,128)(2,1)S(1)} fusion(bf16[16,512]{1,0:T(8,128)(2,1)S(1)} %fusion.3, bf16[512,4096]{1,0:T(8,128)(2,1)S(1)} %copy-done.1), kind=kOutput, calls=%fused_computation | convolution fusion | flops 67174400 | bytes 4341760 | tf_op jit(solution)/shard_map/dot_general | solution.py:120
  48.5 0.1 all_to_all.23
  48.6 10.5 %all_to_all.30 = bf16[16,2,2048]{2,1,0:T(2,128)(2,1)S(1)} all-to-all(bf16[16,2,2048]{2,1,0:T(2,128)(2,1)S(1)} %all_to_all.23), channel_id=1, replica_groups=mesh['groups'=2,'chip'=8,'core'=2] {'chip','core'}, dimensions={0} | all-to-all | bytes 262144 | tf_op jit(solution)/shard_map/all_to_all | solution.py:37
  59.1 0.1 convert_reduce_fusion
  59.2 0.6 %convert_element_type.80 = bf16[1,4096]{1,0:T(2,128)(2,1)} reshape(bf16[4096]{0:T(1024)(128)(2,1)S(1)} %add_convert_fusion) | data formatting | bytes 16384 | tf_op jit(solution)/shard_map/convert_element_type | solution.py:121
  59.8 0.0 copy-done.2
  (23 shorter events, 0.2 us)
Async XLA Ops:
  0.6 20.5 %copy-start = (bf16[256,4096]{1,0:T(8,128)(2,1)S(1)}, bf16[256,4096]{1,0:T(8,128)(2,1)}, u32[]{:S(2)}) copy-start(bf16[256,4096]{1,0:T(8,128)(2,1)} %param.16) | copy-start | bytes 6291460
  0.6 31.6 %copy-start.3 = (bf16[1,4096]{1,0:T(2,128)(2,1)S(1)}, bf16[1,4096]{1,0:T(2,128)(2,1)}, u32[]{:S(2)}) copy-start(bf16[1,4096]{1,0:T(2,128)(2,1)} %param.15) | copy-start | bytes 24580
  0.7 35.9 %copy-start.6 = (s32[256]{0:T(256)S(1)}, s32[256]{0:T(256)}, u32[]{:S(2)}) copy-start(s32[256]{0:T(256)} %param.17) | copy-start | bytes 3076
  0.7 43.8 %copy-start.5 = (f32[512]{0:T(512)S(1)}, f32[512]{0:T(512)}, u32[]{:S(2)}) copy-start(f32[512]{0:T(512)} %param.19) | copy-start | bytes 6148
  6.0 13.8 %all-to-all-start = ((bf16[8,4,128]{2,1,0:T(4,128)(2,1)}), bf16[8,4,128]{2,1,0:T(4,128)(2,1)S(1)}, u32[]{:S(2)}, u32[]{:S(2)}) async-start(bf16[8,4,128]{2,1,0:T(4,128)(2,1)} %bitcast.4), calls=%async_computation | async-start | bytes 16384 | tf_op jit(solution)/shard_map/all_to_all | solution.py:93
  19.8 1.2 %collective-permute-start = (bf16[8,2,128]{2,0,1:T(8,128)(2,1)S(1)}, bf16[8,2,128]{2,0,1:T(8,128)(2,1)S(1)}, u32[]{:S(2)}, u32[]{:S(2)}) collective-permute-start(bf16[8,2,128]{2,0,1:T(8,128)(2,1)S(1)} %select_bitcast_fusion), channel_id=1, source_target_pairs={{0,1},{1,0},{2,3},{3,2},{4,5},{5,4},{6,7},{7,6},{8,9},{9,8},{10,11... | collective-permute-start | bytes 12296 | tf_op jit(solution)/shard_map/ppermute | solution.py:96
  33.0 11.4 %all-to-all-start.2 = ((bf16[16,2,2048]{2,1,0:T(2,128)(2,1)}), bf16[16,2,2048]{2,1,0:T(2,128)(2,1)S(1)}, u32[]{:S(2)}, u32[]{:S(2)}) async-start(bf16[16,2,2048]{2,1,0:T(2,128)(2,1)} %broadcast_in_dim.47), calls=%async_computation.2 | async-start | bytes 262144 | tf_op jit(solution)/shard_map/all_to_all | solution.py:30
  44.4 3.4 %copy-start.1 = (bf16[512,4096]{1,0:T(8,128)(2,1)S(1)}, bf16[512,4096]{1,0:T(8,128)(2,1)}, u32[]{:S(2)}) copy-start(bf16[512,4096]{1,0:T(8,128)(2,1)} %param.20) | copy-start | bytes 12582916
  44.5 14.8 %copy-start.4 = (f32[4096]{0:T(1024)S(1)}, f32[4096]{0:T(1024)}, u32[]{:S(2)}) copy-start(f32[4096]{0:T(1024)} %param.21) | copy-start | bytes 49156
  47.8 12.0 %copy-start.2 = (bf16[16,512]{1,0:T(8,128)(2,1)}, bf16[16,512]{1,0:T(8,128)(2,1)S(1)}, u32[]{:S(2)}) copy-start(bf16[16,512]{1,0:T(8,128)(2,1)S(1)} %fusion.3) | copy-start | bytes 49156
